TPU v7x, 768 devices: a whole 4x8x12 slice. The times are simulated.
768 devices in a mesh: fsdp: 192 (over y_lo, x, z, core), sp: 4 (over y_hi).
Axes of the slice: x: 4, y: 8 (y_hi: 4, y_lo: 2; y = y_hi * 2 + y_lo), z: 12, core: 2. Of those that a mesh axis runs over, the one named last changes fastest.
Arguments:
- hidden_rows: bfloat16 [98304, 8192], P('fsdp'), may hold values from -6 to 6
- queries: bfloat16 [98304, 4096], P(('fsdp', 'sp')), may hold values from -12 to 12
- key_weight: bfloat16 [8256, 512], P('fsdp', 'sp'), may hold values from -0.0625 to 0.0625
- value_weight: bfloat16 [8256, 512], P('fsdp', 'sp'), may hold values from -0.0625 to 0.0625
- cache_keys: bfloat16 [192, 256, 512], P('fsdp', None, 'sp'), may hold values from -10 to 10
- cache_values: bfloat16 [192, 256, 512], P('fsdp', None, 'sp'), may hold values from -6 to 6
- span_index: int32 [192], P('fsdp'), may hold values from 1 to 255
- prefix_len: int32 [192], P('fsdp'), may hold values from 2 to 256, as said below
Outputs:
- attended: bfloat16 [98304, 4096], P(('fsdp', 'sp'))
Inputs may be any that keep to these rules, and one draw needn't show every extreme that they name: `prefix_len`: some group has exactly 256 live slots.
All inputs are finite; a program needn't handle non-finite values.
Results may differ from a plain program's by a relative error of at most 0.014.
Values may be sent and summed in bfloat16 or wider, within the bound.
No kernel may reach another device: no remote copies, remote signals or barrier semaphores. Data moves between devices by JAX's collectives and lax.ppermute only.
A program may use at most 64 MiB of HBM per device.

v0:
```python
import math

import jax
import jax.numpy as jnp
from jax import lax
from jax.sharding import PartitionSpec as P

HD = 128
HQ = 32
KVH = 4
YARN_SCALE = 16
ORIG_CTX = 8192


rope_base = 500000.0
beta_fast = 32.0
beta_slow = 1.0


def yarn_tables(positions, head_size):
    half_size = head_size // 2
    index_row = jnp.arange(half_size, dtype=jnp.float32)
    inverse = jnp.power(rope_base, -2.0 * index_row / head_size)
    wavelength = 2.0 * math.pi / inverse
    ratio = ORIG_CTX / wavelength
    ramp = jnp.clip((ratio - beta_slow) / (beta_fast - beta_slow), 0.0, 1.0)
    freq = inverse / YARN_SCALE * (1.0 - ramp) + inverse * ramp
    factor = 0.1 * math.log(YARN_SCALE) + 1.0
    angles = positions[:, None] * freq[None, :]
    return (jnp.cos(angles) * factor, jnp.sin(angles) * factor)


def rotate(values, cosine_table, sine_table, head_count):
    row_count = values.shape[0]
    half_size = cosine_table.shape[1]
    split = values.reshape(row_count, head_count, 2, half_size)
    first_half = split[:, :, 0]
    second_half = split[:, :, 1]
    cos_part = cosine_table[:, None, :]
    sin_part = sine_table[:, None, :]
    joined = jnp.stack(
        [
            first_half * cos_part - second_half * sin_part,
            second_half * cos_part + first_half * sin_part,
        ],
        axis=2,
    )
    return joined.reshape(row_count, head_count * 2 * half_size)


def attend_block(state, query_heads, key_block, value_block, visible):
    running_max, running_sum, weighted = state
    block_len = key_block.shape[0]
    kv_heads = query_heads.shape[0]
    key_heads = key_block.reshape(block_len, kv_heads, HD)
    value_heads = value_block.reshape(block_len, kv_heads, HD)
    scores = jnp.einsum(
        "hgqd,khd->hgqk", query_heads, key_heads, preferred_element_type=jnp.float32
    ) * HD ** (-0.5)
    scores = jnp.where(visible, scores, -1e30)
    new_max = jnp.maximum(running_max, jnp.max(scores, axis=-1))
    rescale = jnp.exp(running_max - new_max)
    weights = jnp.where(visible, jnp.exp(scores - new_max[..., None]), 0.0)
    running_sum = running_sum * rescale + jnp.sum(weights, axis=-1)
    product = jnp.einsum(
        "hgqk,khd->hgqd",
        weights.astype(jnp.bfloat16),
        value_heads,
        preferred_element_type=jnp.float32,
    )
    weighted = weighted * rescale[..., None] + product
    return (new_max, running_sum, weighted)


def attend_all(query_heads, old_keys, old_values, new_keys, new_values, live_count):
    kv_heads, group_size, query_rows, head_size = query_heads.shape
    slot_total = old_keys.shape[0]
    span_rows = new_keys.shape[0]
    state = (
        jnp.full((kv_heads, group_size, query_rows), -1e30, jnp.float32),
        jnp.zeros((kv_heads, group_size, query_rows), jnp.float32),
        jnp.zeros((kv_heads, group_size, query_rows, head_size), jnp.float32),
    )
    cache_block = min(256, slot_total)

    def cache_step(block_number, carried):
        start = block_number * cache_block
        slot_index = start + jnp.arange(cache_block, dtype=jnp.int32)
        visible = (slot_index >= slot_total - live_count)[None, None, None, :]
        return attend_block(carried, query_heads, old_keys, old_values, visible)

    state = lax.fori_loop(0, slot_total // cache_block, cache_step, state)
    new_block = min(256, span_rows)
    query_index = jnp.arange(query_rows, dtype=jnp.int32)

    def new_step(block_number, carried):
        start = block_number * new_block
        key_block = lax.dynamic_slice_in_dim(new_keys, start, new_block, 0)
        value_block = lax.dynamic_slice_in_dim(new_values, start, new_block, 0)
        key_index = start + jnp.arange(new_block, dtype=jnp.int32)
        visible = (key_index[None, :] <= query_index[:, None])[None, None, :, :]
        return attend_block(carried, query_heads, key_block, value_block, visible)

    state = lax.fori_loop(0, span_rows // new_block, new_step, state)
    running_max, running_sum, weighted = state
    result = (weighted / running_sum[..., None]).astype(jnp.bfloat16)
    return result.transpose(2, 0, 1, 3).reshape(query_rows, kv_heads * group_size * head_size)


def per_device(
    hidden_rows, queries, key_weight, value_weight, cache_keys, cache_values, span_index, prefix_len
):
    sp_count = lax.axis_size("sp")
    span_rows = hidden_rows.shape[0]
    model_width = hidden_rows.shape[1]
    kv_cols = key_weight.shape[1]
    kv_local = kv_cols // HD
    heads_local = HQ // sp_count
    group_size = HQ // KVH
    positions = (span_index[0] * span_rows + jnp.arange(span_rows, dtype=jnp.int32)).astype(
        jnp.float32
    )
    cosine_table, sine_table = yarn_tables(positions, HD)
    live_count = prefix_len[0]
    old_keys = cache_keys[0]
    old_values = cache_values[0]
    full_old_keys, full_old_values = (old_keys, old_values)
    whole_keys, whole_values = (
        lax.all_gather(key_weight, "fsdp", axis=0, tiled=True),
        lax.all_gather(value_weight, "fsdp", axis=0, tiled=True),
    )
    key_sum = jnp.dot(hidden_rows, whole_keys[:model_width], preferred_element_type=jnp.float32)
    value_sum = jnp.dot(hidden_rows, whole_values[:model_width], preferred_element_type=jnp.float32)
    new_keys = rotate(key_sum, cosine_table, sine_table, kv_local).astype(jnp.bfloat16)
    new_values = value_sum.astype(jnp.bfloat16)
    by_heads = lax.all_to_all(queries, "sp", split_axis=1, concat_axis=0, tiled=True)
    rotated_q = rotate(by_heads.astype(jnp.float32), cosine_table, sine_table, heads_local).astype(
        jnp.bfloat16
    )
    query_heads = rotated_q.reshape(span_rows, kv_local, group_size, HD).transpose(1, 2, 0, 3)
    by_tokens = attend_all(
        query_heads, full_old_keys, full_old_values, new_keys, new_values, live_count
    )
    return lax.all_to_all(by_tokens, "sp", split_axis=0, concat_axis=1, tiled=True)


def solution(mesh):
    placed = (
        P("fsdp", None),
        P(("fsdp", "sp"), None),
        P("fsdp", "sp"),
        P("fsdp", "sp"),
        P("fsdp", None, "sp"),
        P("fsdp", None, "sp"),
        P("fsdp"),
        P("fsdp"),
    )
    return jax.shard_map(
        per_device, mesh=mesh, in_specs=placed, out_specs=P(("fsdp", "sp"), None), check_vma=False
    )
```

profile of v0, /device:TPU:1, one launch (start us, length us, event | category | flops | bytes accessed | tf_op | source)
XLA Modules:
  0.0 723.0 jit_solution(15710857800631402493)
XLA Ops:
  6.5 0.0 copy-start
  6.5 0.0 all-gather.5.cloned.1.call-start
  6.5 0.7 all-gather.5.cloned.1.call-update
  7.3 2.3 copy.27
  9.5 7.6 %all-to-all-start = ((bf16[128,4,1024]{0,2,1:T(8,128)(2,1)}), bf16[128,4,1024]{0,2,1:T(8,128)(2,1)S(1)}, u32[]{:S(2)}, u32[]{:S(2)}) async-start(bf16[128,4,1024]{0,2,1:T(8,128)(2,1)} %bitcast.1), calls=%async_computation | async-start | bytes 2097152 | tf_op jit(solution)/shard_map/all_to_all | solution.py:136
  17.2 0.0 all-gather.7.cloned.1.call-start
  17.2 0.7 all-gather.7.cloned.1.call-update
  19.2 0.5 fusion.48
  19.8 23.1 %all-to-all-done = bf16[128,4,1024]{0,2,1:T(8,128)(2,1)S(1)} async-done(((bf16[128,4,1024]{0,2,1:T(8,128)(2,1)}), bf16[128,4,1024]{0,2,1:T(8,128)(2,1)S(1)}, u32[]{:S(2)}, u32[]{:S(2)}) %all-to-all-start) | async-done | bytes 1048608 | tf_op jit(solution)/shard_map/all_to_all | solution.py:136
  42.9 0.1 convert_bitcast_fusion
  43.0 2.7 copy.28
  45.7 2.1 reshape.363
  47.8 0.4 subtract_convert_fusion
  48.2 0.1 pad_maximum_fusion
  48.3 0.7 copy.29
  49.0 0.0 copy-done
  49.0 0.0 copy-start.3
  49.0 0.7 fusion.26
  49.8 1.1 fusion.28
  50.9 0.0 copy-done.3
  50.9 2.8 add_bitcast_fusion
  53.7 283.2 %all-gather.5.cloned.1.call-done = bf16[192,43,128]{2,1,0:T(8,128)(2,1)} async-done(((bf16[1,43,128]{2,1,0:T(8,128)(2,1)}), bf16[192,43,128]{2,1,0:T(8,128)(2,1)}) %all-gather.5.cloned.1.call-update) | async-done | bytes 2113552 | tf_op jit(solution)/shard_map/all_gather | solution.py:129
  337.0 2.7 reshape.365
  339.7 6.3 fusion.33
  346.0 0.6 fusion.54
  346.6 314.5 %all-gather.7.cloned.1.call-done = bf16[192,43,128]{2,1,0:T(8,128)(2,1)} async-done(((bf16[1,43,128]{2,1,0:T(8,128)(2,1)}), bf16[192,43,128]{2,1,0:T(8,128)(2,1)}) %all-gather.7.cloned.1.call-update) | async-done | bytes 2113552 | tf_op jit(solution)/shard_map/all_gather | solution.py:130
  661.1 2.7 reshape.367
  663.8 6.4 fusion.42
  670.2 10.2 %while.5 = (s32[]{:T(128)}, f32[1,8,512]{2,1,0:T(8,128)S(1)}, f32[1,8,512]{2,1,0:T(8,128)S(1)}, f32[1,8,512,128]{3,2,1,0:T(8,128)}, bf16[512,128]{0,1:T(8,128)(2...) while((s32[]{:T(128)}, f32[1,8,512]{2,1,0:T(8,128)S(1)}, ...), condition=%wide.region_5.6_spmd.clone, body=%wide.region_2.5_spmd.clone.sunk | while | flops 551694592 | bytes 36047096 | solution.py:104
  670.4 0.0 copy-start.4
  670.4 0.1 iota_compare_fusion.3
  670.6 0.9 fusion.75
  671.5 0.5 copy-done.1
  672.0 2.0 bitcast_add_fusion.6
  674.0 1.0 fusion.77
  675.1 0.3 copy-done.2
  675.4 0.1 iota_compare_fusion.3
  675.6 0.9 fusion.75
  676.5 0.5 copy-done.1
  677.0 2.0 bitcast_add_fusion.6
  679.1 1.0 fusion.77
  680.1 0.3 copy-done.2
  680.4 2.0 fusion.47
  682.4 0.7 copy.32
  683.1 0.5 all_to_all.26
  683.6 30.6 %all_to_all.32 = bf16[4,128,1024]{2,1,0:T(8,128)(2,1)S(1)} all-to-all(bf16[4,128,1024]{2,1,0:T(8,128)(2,1)S(1)} %all_to_all.26), channel_id=1, replica_groups=mesh['fsdp'=192,'sp'=4] {'sp'}, dimensions={0} | all-to-all | bytes 2097152 | tf_op jit(solution)/shard_map/all_to_all | solution.py:144
  714.2 0.7 copy.33
  714.9 1.3 copy.34
  (21 shorter events, 0.2 us)
Async XLA Ops:
  6.5 42.4 %copy-start = (bf16[1,256,128]{2,1,0:T(8,128)(2,1)S(1)}, bf16[1,256,128]{2,1,0:T(8,128)(2,1)}, u32[]{:S(2)}) copy-start(bf16[1,256,128]{2,1,0:T(8,128)(2,1)} %param.14) | copy-start | bytes 196612
  6.5 330.5 %all-gather.5.cloned.1.call-start = ((), (), s32[]{:S(2)}) async-start(), calls=%async_computation.2 | async-start | bytes 2371584 | tf_op jit(solution)/shard_map/all_gather | solution.py:129
  9.5 33.3 %all-to-all-start = ((bf16[128,4,1024]{0,2,1:T(8,128)(2,1)}), bf16[128,4,1024]{0,2,1:T(8,128)(2,1)S(1)}, u32[]{:S(2)}, u32[]{:S(2)}) async-start(bf16[128,4,1024]{0,2,1:T(8,128)(2,1)} %bitcast.1), calls=%async_computation | async-start | bytes 2097152 | tf_op jit(solution)/shard_map/all_to_all | solution.py:136
  17.2 643.9 %all-gather.7.cloned.1.call-start = ((), (), s32[]{:S(2)}) async-start(), calls=%async_computation.3 | async-start | bytes 2371584 | tf_op jit(solution)/shard_map/all_gather | solution.py:130
  49.0 1.9 copy-start.3
  670.4 1.6 copy-start.1
  670.4 1.6 copy-start.4
  674.0 1.4 copy-start.2
  675.4 1.6 copy-start.1
  675.4 1.6 copy-start.4
  679.0 1.4 copy-start.2
Sparse Core Ops, SparseCore 0:
  9.9 327.0 all-gather.4
  339.5 321.5 all-gather.6
where the time goes:
time: 724 us; the launch traced here: 723 us
  waiting for transfers between devices  622 us (86%)
  blocking collectives  30.6 us (4%)
  matrix products  22 us (3%)
  local copies, waits for them, and re-layouts  18 us (2%)
  between operations  14.9 us (2%)
  starting transfers between devices  7.65 us (1%)
  other arithmetic  7.25 us (1%)
    all_gather x1, waiting for transfers between devices, per_device(): lax.all_gather(value_weight, 'fsdp', axis=0, tiled=True)  315 us
    all_gather x1, waiting for transfers between devices, per_device(): lax.all_gather(key_weight, 'fsdp', axis=0, tiled=True)  283 us
    all_to_all x1, blocking collectives, per_device(): lax.all_to_all(by_tokens, 'sp', split_axis=0, concat_axis=1, tiled=True)  30.6 us
    all_to_all x1, waiting for transfers between devices, per_device(): lax.all_to_all(queries, 'sp', split_axis=1, concat_axis=0, tiled=True)  23.1 us
  transfers between devices with their start and end apart: 3, of which 3 were waited for; matrix products, arithmetic and copies ran while one was open for 3% of the time, Pallas kernels for 0%

commit v1 on v0

--- a/solution.py
+++ b/solution.py
@@ -107,6 +107,27 @@
     return result.transpose(2, 0, 1, 3).reshape(query_rows, kv_heads * group_size * head_size)
 
 
+FSDP_PARTS = (("ylo", 2), ("x", 4), ("z", 12), ("core", 2))
+FSDP_AXES = tuple(name for name, _ in FSDP_PARTS)
+GATHER_STAGES = (("ylo",), ("x",), ("z",), ("core",))
+
+
+def gather_weights(shard):
+    gathered = shard
+    for stage in GATHER_STAGES:
+        gathered = lax.all_gather(gathered, stage, axis=0, tiled=False)
+        if len(stage) > 1:
+            sizes = tuple(dict(FSDP_PARTS)[name] for name in stage)
+            gathered = gathered.reshape(sizes + gathered.shape[1:])
+    layout = []
+    for stage in reversed(GATHER_STAGES):
+        layout.extend(stage)
+    perm = [layout.index(name) for name in FSDP_AXES]
+    rank = len(FSDP_AXES)
+    gathered = gathered.transpose(perm + [rank, rank + 1])
+    return gathered.reshape(-1, shard.shape[1])
+
+
 def per_device(
     hidden_rows, queries, key_weight, value_weight, cache_keys, cache_values, span_index, prefix_len
 ):
@@ -125,12 +146,10 @@
     old_keys = cache_keys[0]
     old_values = cache_values[0]
     full_old_keys, full_old_values = (old_keys, old_values)
-    whole_keys, whole_values = (
-        lax.all_gather(key_weight, "fsdp", axis=0, tiled=True),
-        lax.all_gather(value_weight, "fsdp", axis=0, tiled=True),
-    )
-    key_sum = jnp.dot(hidden_rows, whole_keys[:model_width], preferred_element_type=jnp.float32)
-    value_sum = jnp.dot(hidden_rows, whole_values[:model_width], preferred_element_type=jnp.float32)
+    whole_kv = gather_weights(jnp.concatenate([key_weight, value_weight], axis=1))
+    kv_sum = jnp.dot(hidden_rows, whole_kv[:model_width], preferred_element_type=jnp.float32)
+    key_sum = kv_sum[:, :kv_cols]
+    value_sum = kv_sum[:, kv_cols:]
     new_keys = rotate(key_sum, cosine_table, sine_table, kv_local).astype(jnp.bfloat16)
     new_values = value_sum.astype(jnp.bfloat16)
     by_heads = lax.all_to_all(queries, "sp", split_axis=1, concat_axis=0, tiled=True)
@@ -145,16 +164,21 @@
 
 
 def solution(mesh):
+    sizes = tuple(size for _, size in FSDP_PARTS)
+    fine = jax.sharding.Mesh(
+        mesh.devices.reshape(sizes + (mesh.shape["sp"],)), FSDP_AXES + ("sp",)
+    )
+    fsdp = FSDP_AXES
     placed = (
-        P("fsdp", None),
-        P(("fsdp", "sp"), None),
-        P("fsdp", "sp"),
-        P("fsdp", "sp"),
-        P("fsdp", None, "sp"),
-        P("fsdp", None, "sp"),
-        P("fsdp"),
-        P("fsdp"),
+        P(fsdp, None),
+        P(fsdp + ("sp",), None),
+        P(fsdp, "sp"),
+        P(fsdp, "sp"),
+        P(fsdp, None, "sp"),
+        P(fsdp, None, "sp"),
+        P(fsdp),
+        P(fsdp),
     )
     return jax.shard_map(
-        per_device, mesh=mesh, in_specs=placed, out_specs=P(("fsdp", "sp"), None), check_vma=False
+        per_device, mesh=fine, in_specs=placed, out_specs=P(fsdp + ("sp",), None), check_vma=False
     )

time: 724 us -> 212 us (0.29)
  waiting for transfers between devices: 622 us -> 89.7 us
  local copies, waits for them, and re-layouts: 18 us -> 34.6 us
  blocking collectives: 30.6 us -> 39.5 us
    all_gather x2, waiting for transfers between devices: 598 us -> 65.7 us  [gather_weights(): gathered = lax.all_gather(gathered, stage, axis=0, tiled=False)]
    all_gather x0 -> x2, blocking collectives: none -> 13.7 us  [gather_weights(): gathered = lax.all_gather(gathered, stage, axis=0, tiled=False)]
    all_gather x0 -> x3, local copies, waits for them, and re-layouts: none -> 12.1 us  [gather_weights(): gathered = lax.all_gather(gathered, stage, axis=0, tiled=False)]
    reshape x0 -> x1, local copies, waits for them, and re-layouts: none -> 7.28 us  [gather_weights(): return gathered.reshape(-1, shard.shape[1])]
  transfers between devices with their start and end apart: 3 -> 3, of which waited for: 3 -> 2; matrix products, arithmetic and copies ran while one was open for 3% -> 6% of each run, Pallas kernels for 0% -> 0%
where the time goes in v1:
time: 212 us; the launch traced here: 208 us
  waiting for transfers between devices  89.7 us (42%)
  blocking collectives  39.5 us (19%)
  local copies, waits for them, and re-layouts  34.6 us (16%)
  matrix products  15.4 us (7%)
  between operations  14.9 us (7%)
  other arithmetic  6.84 us (3%)
  starting transfers between devices  6.49 us (3%)
    all_gather x2, waiting for transfers between devices, gather_weights(): gathered = lax.all_gather(gathered, stage, axis=0, tiled=False)  65.7 us
    all_to_all x1, blocking collectives, per_device(): lax.all_to_all(by_tokens, 'sp', split_axis=0, concat_axis=1, tiled=True)  25.7 us
    all_to_all x1, waiting for transfers between devices, per_device(): lax.all_to_all(queries, 'sp', split_axis=1, concat_axis=0, tiled=True)  24 us
    all_gather x2, blocking collectives, gather_weights(): gathered = lax.all_gather(gathered, stage, axis=0, tiled=False)  13.7 us
    all_gather x3, local copies, waits for them, and re-layouts, gather_weights(): gathered = lax.all_gather(gathered, stage, axis=0, tiled=False)  12.1 us
    reshape x1, local copies, waits for them, and re-layouts, gather_weights(): return gathered.reshape(-1, shard.shape[1])  7.28 us
    dot_general x1, matrix products, per_device(): jnp.dot(hidden_rows, whole_kv[:model_width], preferred_element_type=jnp.f...  7.04 us
    all_to_all x1, starting transfers between devices, per_device(): lax.all_to_all(queries, 'sp', split_axis=1, concat_axis=0, tiled=True)  6.45 us
  transfers between devices with their start and end apart: 3, of which 2 were waited for; matrix products, arithmetic and copies ran while one was open for 6% of the time, Pallas kernels for 0%

profile of v1, /device:TPU:1, one launch (start us, length us, event | category | flops | bytes accessed | tf_op | source)
XLA Modules:
  0.0 207.5 jit_solution(17009556482414962120)
XLA Ops:
  6.5 0.0 copy-start
  6.5 0.0 all-gather.8.cloned.1.call-start
  6.5 0.8 maximum_bitcast_fusion
  7.4 4.0 %all-gather.4 = bf16[2,43,256]{2,1,0:T(8,128)(2,1)S(1)} all-gather(bf16[1,43,256]{2,1,0:T(8,128)(2,1)S(1)} %maximum_bitcast_fusion), channel_id=2, replica_groups=mesh['ylo'=2,'x'=4,'z'=12,'core'=2,'sp'=4] {'ylo'}, dimensions={0}, use_global_device_ids=true | all-gather | bytes 66048 | tf_op jit(solution)/shard_map/all_gather | solution.py:118
  11.3 9.8 %all-gather.1 = bf16[8,43,256]{2,1,0:T(8,128)(2,1)S(1)} all-gather(bf16[2,43,256]{2,1,0:T(8,128)(2,1)S(1)} %all-gather.4), channel_id=3, replica_groups=mesh['ylo'=2,'x'=4,'z'=12,'core'=2,'sp'=4] {'x'}, dimensions={0}, use_global_device_ids=true | all-gather | bytes 220160 | tf_op jit(solution)/shard_map/all_gather | solution.py:118
  21.1 0.8 copy.36
  21.9 0.0 all-gather.8.cloned.1.call-update
  21.9 0.0 all-gather.10.cloned.1.call-start
  22.0 65.7 %all-gather.8.cloned.1.call-done = bf16[48,2,43,256]{3,1,2,0:T(2,128)(2,1)} async-done(((bf16[4,2,43,256]{3,1,2,0:T(2,128)(2,1)}), bf16[48,2,43,256]{3,1,2,0:T(2,128)(2,1)}) %all-gather.8.cloned.1.call-update) | async-done | bytes 2113552 | tf_op jit(solution)/shard_map/all_gather | solution.py:118
  87.7 3.7 %copy.37 = bf16[12,4,2,43,256]{4,1,3,2,0:T(4,128)(2,1)} copy(bf16[12,4,2,43,256]{4,2,3,1,0:T(2,128)(2,1)} %bitcast.118) | data formatting | bytes 4227072 | tf_op jit(solution)/shard_map/all_gather | solution.py:118
  91.4 0.0 all-gather.10.cloned.1.call-update
  91.4 0.0 copy-done.1
  91.5 1.3 copy.32
  92.8 6.4 %all-to-all-start = ((bf16[128,4,1024]{0,2,1:T(8,128)(2,1)}), bf16[128,4,1024]{0,2,1:T(8,128)(2,1)S(1)}, u32[]{:S(2)}, u32[]{:S(2)}) async-start(bf16[128,4,1024]{0,2,1:T(8,128)(2,1)} %bitcast.1), calls=%async_computation | async-start | bytes 2097152 | tf_op jit(solution)/shard_map/all_to_all | solution.py:155
  100.6 0.5 fusion.46
  101.1 24.0 %all-to-all-done = bf16[128,4,1024]{0,2,1:T(8,128)(2,1)S(1)} async-done(((bf16[128,4,1024]{0,2,1:T(8,128)(2,1)}), bf16[128,4,1024]{0,2,1:T(8,128)(2,1)S(1)}, u32[]{:S(2)}, u32[]{:S(2)}) %all-to-all-start) | async-done | bytes 1048608 | tf_op jit(solution)/shard_map/all_to_all | solution.py:155
  125.1 0.1 convert_bitcast_fusion
  125.2 2.7 %copy.33 = f32[4,128,1024]{1,0,2:T(4,128)} copy(f32[4,128,1024]{1,2,0:T(8,128)S(1)} %convert_bitcast_fusion) | data formatting | bytes 4194304 | tf_op jit(solution)/shard_map/convert_element_type | solution.py:156
  127.9 2.1 %reshape.367 = f32[512,8,2,64]{0,3,2,1:T(8,128)S(1)} reshape(f32[4,128,1024]{1,0,2:T(4,128)} %copy.33) | data formatting | bytes 4194304 | tf_op jit(solution)/shard_map/convert_element_type | solution.py:156
  130.0 0.4 subtract_convert_fusion
  130.4 0.1 pad_maximum_fusion
  130.5 0.7 copy.34
  131.1 0.0 copy-done
  131.2 0.0 copy-start.2
  131.2 0.7 fusion.28
  131.9 1.1 fusion.30
  133.1 1.6 add_bitcast_fusion
  134.7 0.0 all-gather.10.cloned.1.call-done
  134.8 7.5 %copy.38 = bf16[24,4,2,43,256]{4,2,3,1,0:T(2,128)(2,1)} copy(bf16[24,4,2,43,256]{4,1,3,2,0:T(4,128)(2,1)} %all-gather.10.cloned.1.call-done) | data formatting | bytes 8454144 | tf_op jit(solution)/shard_map/all_gather | solution.py:118
  142.3 5.3 %copy.39 = bf16[2,4,12,2,43,256]{5,4,3,2,1,0:T(8,128)(2,1)} copy(bf16[2,4,12,2,43,256]{5,0,4,1,2,3:T(2,128)(2,1)} %bitcast.112) | data formatting | bytes 8454144 | tf_op jit(solution)/shard_map/transpose | solution.py:127
  147.6 7.3 %reshape.365 = bf16[8256,256]{1,0:T(8,128)(2,1)} reshape(bf16[2,4,12,2,43,256]{5,4,3,2,1,0:T(8,128)(2,1)} %copy.39) | data formatting | bytes 8454144 | tf_op jit(solution)/shard_map/reshape | solution.py:128
  154.9 7.0 %fusion.40 = f32[512,256]{0,1:T(8,128)S(1)} fusion(bf16[512,8192]{1,0:T(8,128)(2,1)} %param.10, bf16[8256,256]{1,0:T(8,128)(2,1)} %reshape.365), kind=kOutput, calls=%fused_computation.46 | convolution fusion | flops 2147483648 | bytes 13107200 | tf_op jit(solution)/shard_map/dot_general | solution.py:150
  162.0 0.6 fusion.52
  162.6 8.5 %while.5 = (s32[]{:T(128)}, f32[1,8,512]{2,1,0:T(8,128)S(1)}, f32[1,8,512]{2,1,0:T(8,128)S(1)}, f32[1,8,512,128]{3,2,1,0:T(8,128)S(1)}, bf16[512,128]{0,1:T(8,12...) while((s32[]{:T(128)}, f32[1,8,512]{2,1,0:T(8,128)S(1)}, ...), condition=%wide.region_5.6_spmd.clone, body=%wide.region_2.5_spmd.clone.sunk | while | flops 551694592 | bytes 18745512 | solution.py:104
  162.6 0.1 iota_compare_fusion.3
  162.7 0.9 fusion.72
  163.6 1.0 fusion.74
  164.7 2.1 %bitcast_add_fusion.6 = f32[1,8,512,128]{3,2,1,0:T(8,128)S(1)} fusion(f32[1,8,512,128]{3,2,1,0:T(8,128)S(1)} %get-tuple-element.312, f32[256,8,512]{2,0,1:T(8,128)S(1)} %get-tuple-element.296, f32[8,512]{1,0:T(8,128)S(1)} %bitcast.114, pred[512,256]{0,1:T(8,128)(4,1)S(1)} %iota_compare_fusion.3, f32[8,512]{1,0:T(8,128)S(1)} %get-tuple-element.297, ...), kind=kOutput, calls=%fused_computation.7.clone.1 | convolution fusion | flops 274726912 | bytes 8617988 | tf_op jit(solution)/shard_map/while/body/eval_jaxpr/hgqk,khd->hgqd/dot_general | solution.py:65
  166.8 0.1 iota_compare_fusion.3
  167.0 0.9 fusion.72
  167.9 1.0 fusion.74
  168.9 2.1 %bitcast_add_fusion.6 = f32[1,8,512,128]{3,2,1,0:T(8,128)S(1)} fusion(f32[1,8,512,128]{3,2,1,0:T(8,128)S(1)} %get-tuple-element.312, f32[256,8,512]{2,0,1:T(8,128)S(1)} %get-tuple-element.296, f32[8,512]{1,0:T(8,128)S(1)} %bitcast.114, pred[512,256]{0,1:T(8,128)(4,1)S(1)} %iota_compare_fusion.3, f32[8,512]{1,0:T(8,128)S(1)} %get-tuple-element.297, ...), kind=kOutput, calls=%fused_computation.7.clone.1 | convolution fusion | flops 274726912 | bytes 8617988 | tf_op jit(solution)/shard_map/while/body/eval_jaxpr/hgqk,khd->hgqd/dot_general | solution.py:65
  171.1 0.7 fusion.45
  171.8 0.7 copy.42
  172.5 0.5 all_to_all.26
  173.0 25.7 %all_to_all.32 = bf16[4,128,1024]{2,1,0:T(8,128)(2,1)S(1)} all-to-all(bf16[4,128,1024]{2,1,0:T(8,128)(2,1)S(1)} %all_to_all.26), channel_id=1, replica_groups=mesh['ylo'=2,'x'=4,'z'=12,'core'=2,'sp'=4] {'sp'}, dimensions={0} | all-to-all | bytes 2097152 | tf_op jit(solution)/shard_map/all_to_all | solution.py:163
  198.7 0.7 copy.43
  199.4 1.3 copy.44
  (18 shorter events, 0.2 us)
Async XLA Ops:
  6.5 124.6 %copy-start = (bf16[1,256,128]{2,1,0:T(8,128)(2,1)S(1)}, bf16[1,256,128]{2,1,0:T(8,128)(2,1)}, u32[]{:S(2)}) copy-start(bf16[1,256,128]{2,1,0:T(8,128)(2,1)} %param.14) | copy-start | bytes 196612
  6.5 84.9 %copy-start.1 = (bf16[128,4096]{1,0:T(8,128)(2,1)S(1)}, bf16[128,4096]{1,0:T(8,128)(2,1)}, u32[]{:S(2)}) copy-start(bf16[128,4096]{1,0:T(8,128)(2,1)} %param.11) | copy-start | bytes 3145732
  6.5 81.1 %all-gather.8.cloned.1.call-start = ((), (), s32[]{:S(2)}) async-start(), calls=%async_computation.2 | async-start | bytes 2289664 | tf_op jit(solution)/shard_map/all_gather | solution.py:118
  21.9 112.8 %all-gather.10.cloned.1.call-start = ((), (), s32[]{:S(2)}) async-start(), calls=%async_computation.3 | async-start | bytes 6340608 | tf_op jit(solution)/shard_map/all_gather | solution.py:118
  92.8 32.3 %all-to-all-start = ((bf16[128,4,1024]{0,2,1:T(8,128)(2,1)}), bf16[128,4,1024]{0,2,1:T(8,128)(2,1)S(1)}, u32[]{:S(2)}, u32[]{:S(2)}) async-start(bf16[128,4,1024]{0,2,1:T(8,128)(2,1)} %bitcast.1), calls=%async_computation | async-start | bytes 2097152 | tf_op jit(solution)/shard_map/all_to_all | solution.py:155
  131.2 1.9 copy-start.2
Sparse Core Ops, SparseCore 0:
  22.1 65.5 all-gather.7
  91.6 30.5 all-gather.9

commit v2 on v1

--- a/solution.py
+++ b/solution.py
@@ -109,7 +109,7 @@
 
 FSDP_PARTS = (("ylo", 2), ("x", 4), ("z", 12), ("core", 2))
 FSDP_AXES = tuple(name for name, _ in FSDP_PARTS)
-GATHER_STAGES = (("ylo",), ("x",), ("z",), ("core",))
+GATHER_STAGES = (("ylo",), ("x", "z"), ("core",))
 
 
 def gather_weights(shard):

time: 212 us -> 241 us (1.14)
  waiting for transfers between devices: 89.7 us -> 143 us
  local copies, waits for them, and re-layouts: 34.6 us -> 20.6 us
  blocking collectives: 39.5 us -> 29.8 us
    all_gather x2, waiting for transfers between devices: 65.7 us -> 119 us  [gather_weights(): gathered = lax.all_gather(gathered, stage, axis=0, tiled=False)]
    all_gather x3 -> x0, local copies, waits for them, and re-layouts: 12.1 us -> none  [gather_weights(): gathered = lax.all_gather(gathered, stage, axis=0, tiled=False)]
    all_gather x2 -> x1, blocking collectives: 13.7 us -> 4.09 us  [gather_weights(): gathered = lax.all_gather(gathered, stage, axis=0, tiled=False)]
    transpose x1 -> x0, local copies, waits for them, and re-layouts: 5.31 us -> none  [gather_weights(): gathered = gathered.transpose(perm + [rank, rank + 1])]
    another operation x0 -> x1, local copies, waits for them, and re-layouts: none -> 3.33 us  [gather_weights(): gathered = lax.all_gather(gathered, stage, axis=0, tiled=False)]
  transfers between devices with their start and end apart: 3 -> 3, of which waited for: 2 -> 2; matrix products, arithmetic and copies ran while one was open for 6% -> 5% of each run, Pallas kernels for 0% -> 0%
where the time goes in v2:
time: 241 us; the launch traced here: 238 us
  waiting for transfers between devices  143 us (59%)
  blocking collectives  29.8 us (12%)
  local copies, waits for them, and re-layouts  20.6 us (9%)
  matrix products  15.4 us (6%)
  between operations  14.9 us (6%)
  other arithmetic  6.84 us (3%)
  starting transfers between devices  6.49 us (3%)
    all_gather x2, waiting for transfers between devices, gather_weights(): gathered = lax.all_gather(gathered, stage, axis=0, tiled=False)  119 us
    all_to_all x1, blocking collectives, per_device(): lax.all_to_all(by_tokens, 'sp', split_axis=0, concat_axis=1, tiled=True)  25.7 us
    all_to_all x1, waiting for transfers between devices, per_device(): lax.all_to_all(queries, 'sp', split_axis=1, concat_axis=0, tiled=True)  24.1 us
    reshape x1, local copies, waits for them, and re-layouts, gather_weights(): return gathered.reshape(-1, shard.shape[1])  7.28 us
    dot_general x1, matrix products, per_device(): jnp.dot(hidden_rows, whole_kv[:model_width], preferred_element_type=jnp.f...  7.04 us
    all_to_all x1, starting transfers between devices, per_device(): lax.all_to_all(queries, 'sp', split_axis=1, concat_axis=0, tiled=True)  6.45 us
    dot_general x3, matrix products, attend_block(): jnp.einsum('hgqk,khd->hgqd', weights.astype(jnp.bfloat16), value_heads, p...  5.82 us
    convert_element_type x2, local copies, waits for them, and re-layouts, per_device(): by_heads.astype(jnp.float32)  4.83 us
  transfers between devices with their start and end apart: 3, of which 2 were waited for; matrix products, arithmetic and copies ran while one was open for 5% of the time, Pallas kernels for 0%

profile of v2, /device:TPU:1, one launch (start us, length us, event | category | flops | bytes accessed | tf_op | source)
XLA Modules:
  0.0 237.8 jit_solution(11084900213481476087)
XLA Ops:
  6.5 0.0 copy-start
  6.5 0.0 copy-start.1
  6.5 0.0 all-gather.8.cloned.1.call-start
  6.5 0.8 maximum_bitcast_fusion
  7.4 4.1 %all-gather.2 = bf16[2,43,256]{2,1,0:T(8,128)(2,1)} all-gather(bf16[1,43,256]{2,1,0:T(8,128)(2,1)S(1)} %maximum_bitcast_fusion), channel_id=2, replica_groups=mesh['ylo'=2,'x'=4,'z'=12,'core'=2,'sp'=4] {'ylo'}, dimensions={0}, use_global_device_ids=true | all-gather | bytes 66048 | tf_op jit(solution)/shard_map/all_gather | solution.py:118
  11.5 0.0 all-gather.8.cloned.1.call-update
  11.5 0.0 all-gather.6.cloned.1.call-start
  11.5 119.2 %all-gather.8.cloned.1.call-done = bf16[96,43,256]{2,1,0:T(8,128)(2,1)} async-done(((bf16[2,43,256]{2,1,0:T(8,128)(2,1)}), bf16[96,43,256]{2,1,0:T(8,128)(2,1)}) %all-gather.8.cloned.1.call-update) | async-done | bytes 2113552 | tf_op jit(solution)/shard_map/all_gather | solution.py:118
  130.8 3.3 %copy.36 = bf16[1,4,12,2,43,256]{5,4,0,2,1,3:T(8,128)(2,1)} copy(bf16[1,4,12,2,43,256]{5,4,3,2,1,0:T(8,128)(2,1)} %bitcast.115) | data formatting | bytes 4227072 | tf_op jit(solution)/shard_map/all_gather;reshape | solution.py:118
  134.1 0.0 all-gather.6.cloned.1.call-update
  134.1 0.0 copy-done.1
  134.1 1.3 copy.32
  135.4 6.5 %all-to-all-start = ((bf16[128,4,1024]{0,2,1:T(8,128)(2,1)}), bf16[128,4,1024]{0,2,1:T(8,128)(2,1)S(1)}, u32[]{:S(2)}, u32[]{:S(2)}) async-start(bf16[128,4,1024]{0,2,1:T(8,128)(2,1)} %bitcast.1), calls=%async_computation | async-start | bytes 2097152 | tf_op jit(solution)/shard_map/all_to_all | solution.py:155
  143.2 0.5 fusion.46
  143.8 24.1 %all-to-all-done = bf16[128,4,1024]{0,2,1:T(8,128)(2,1)S(1)} async-done(((bf16[128,4,1024]{0,2,1:T(8,128)(2,1)}), bf16[128,4,1024]{0,2,1:T(8,128)(2,1)S(1)}, u32[]{:S(2)}, u32[]{:S(2)}) %all-to-all-start) | async-done | bytes 1048608 | tf_op jit(solution)/shard_map/all_to_all | solution.py:155
  167.9 0.1 convert_bitcast_fusion
  168.1 2.7 %copy.33 = f32[4,128,1024]{1,0,2:T(4,128)} copy(f32[4,128,1024]{1,2,0:T(8,128)S(1)} %convert_bitcast_fusion) | data formatting | bytes 4194304 | tf_op jit(solution)/shard_map/convert_element_type | solution.py:156
  170.8 2.1 reshape.367
  172.9 0.4 subtract_convert_fusion
  173.2 0.1 pad_maximum_fusion
  173.3 0.7 copy.34
  174.0 0.0 copy-done
  174.0 0.0 copy-start.2
  174.0 0.7 fusion.28
  174.8 1.1 fusion.30
  176.0 0.0 copy-done.2
  176.0 1.6 add_bitcast_fusion
  177.6 0.0 all-gather.6.cloned.1.call-done
  177.6 7.3 %reshape.365 = bf16[8256,256]{1,0:T(8,128)(2,1)} reshape(bf16[2,4,12,2,43,256]{5,4,3,2,1,0:T(8,128)(2,1)} %bitcast.111) | data formatting | bytes 8454144 | tf_op jit(solution)/shard_map/reshape | solution.py:128
  184.9 7.0 %fusion.40 = f32[512,256]{0,1:T(8,128)S(1)} fusion(bf16[512,8192]{1,0:T(8,128)(2,1)} %param.10, bf16[8256,256]{1,0:T(8,128)(2,1)} %reshape.365), kind=kOutput, calls=%fused_computation.46 | convolution fusion | flops 2147483648 | bytes 13107200 | tf_op jit(solution)/shard_map/dot_general | solution.py:150
  192.0 0.6 fusion.52
  192.6 8.7 %while.5 = (s32[]{:T(128)}, f32[1,8,512]{2,1,0:T(8,128)S(1)}, f32[1,8,512]{2,1,0:T(8,128)S(1)}, f32[1,8,512,128]{3,2,1,0:T(8,128)S(1)}, bf16[512,128]{0,1:T(8,12...) while((s32[]{:T(128)}, f32[1,8,512]{2,1,0:T(8,128)S(1)}, ...), condition=%wide.region_5.6_spmd.clone, body=%wide.region_2.5_spmd.clone.sunk | while | flops 551694592 | bytes 18745512 | solution.py:104
  192.8 0.1 iota_compare_fusion.3
  193.0 0.9 fusion.72
  193.9 1.0 fusion.74
  194.9 2.1 bitcast_add_fusion.6
  197.1 0.1 iota_compare_fusion.3
  197.2 0.9 fusion.72
  198.1 1.0 fusion.74
  199.2 2.1 bitcast_add_fusion.6
  201.3 0.7 fusion.45
  202.1 0.7 copy.39
  202.7 0.5 all_to_all.26
  203.2 25.7 %all_to_all.32 = bf16[4,128,1024]{2,1,0:T(8,128)(2,1)S(1)} all-to-all(bf16[4,128,1024]{2,1,0:T(8,128)(2,1)S(1)} %all_to_all.26), channel_id=1, replica_groups=mesh['ylo'=2,'x'=4,'z'=12,'core'=2,'sp'=4] {'sp'}, dimensions={0} | all-to-all | bytes 2097152 | tf_op jit(solution)/shard_map/all_to_all | solution.py:163
  229.0 0.7 copy.40
  229.6 1.3 copy.41
  (16 shorter events, 0.2 us)
Async XLA Ops:
  6.5 167.5 %copy-start = (bf16[1,256,128]{2,1,0:T(8,128)(2,1)S(1)}, bf16[1,256,128]{2,1,0:T(8,128)(2,1)}, u32[]{:S(2)}) copy-start(bf16[1,256,128]{2,1,0:T(8,128)(2,1)} %param.14) | copy-start | bytes 196612
  6.5 127.6 %copy-start.1 = (bf16[128,4096]{1,0:T(8,128)(2,1)S(1)}, bf16[128,4096]{1,0:T(8,128)(2,1)}, u32[]{:S(2)}) copy-start(bf16[128,4096]{1,0:T(8,128)(2,1)} %param.11) | copy-start | bytes 3145732
  6.5 124.2 %all-gather.8.cloned.1.call-start = ((), (), s32[]{:S(2)}) async-start(), calls=%async_computation.3 | async-start | bytes 2408448 | tf_op jit(solution)/shard_map/all_gather | solution.py:118
  11.5 166.2 %all-gather.6.cloned.1.call-start = ((), (), s32[]{:S(2)}) async-start(), calls=%async_computation.2 | async-start | bytes 7077888 | tf_op jit(solution)/shard_map/all_gather | solution.py:118
  135.4 32.5 %all-to-all-start = ((bf16[128,4,1024]{0,2,1:T(8,128)(2,1)}), bf16[128,4,1024]{0,2,1:T(8,128)(2,1)S(1)}, u32[]{:S(2)}, u32[]{:S(2)}) async-start(bf16[128,4,1024]{0,2,1:T(8,128)(2,1)} %bitcast.1), calls=%async_computation | async-start | bytes 2097152 | tf_op jit(solution)/shard_map/all_to_all | solution.py:155
  174.0 1.9 copy-start.2
Sparse Core Ops, SparseCore 0:
  11.6 119.1 all-gather.7
  134.2 30.0 all-gather.5

commit v3 on v1

--- a/solution.py
+++ b/solution.py
@@ -131,36 +131,74 @@
 def per_device(
     hidden_rows, queries, key_weight, value_weight, cache_keys, cache_values, span_index, prefix_len
 ):
-    sp_count = lax.axis_size("sp")
     span_rows = hidden_rows.shape[0]
     model_width = hidden_rows.shape[1]
+    query_rows = queries.shape[0]
     kv_cols = key_weight.shape[1]
     kv_local = kv_cols // HD
-    heads_local = HQ // sp_count
     group_size = HQ // KVH
-    positions = (span_index[0] * span_rows + jnp.arange(span_rows, dtype=jnp.int32)).astype(
-        jnp.float32
-    )
+    slot_total = cache_keys.shape[1]
+    sp_index = lax.axis_index("sp")
+    block_start = span_index[0] * span_rows
+    positions = (block_start + jnp.arange(span_rows, dtype=jnp.int32)).astype(jnp.float32)
     cosine_table, sine_table = yarn_tables(positions, HD)
+    first_query = sp_index * query_rows
+    query_positions = (
+        block_start + first_query + jnp.arange(query_rows, dtype=jnp.int32)
+    ).astype(jnp.float32)
+    query_cosine, query_sine = yarn_tables(query_positions, HD)
     live_count = prefix_len[0]
-    old_keys = cache_keys[0]
-    old_values = cache_values[0]
-    full_old_keys, full_old_values = (old_keys, old_values)
+
+    cache_kv = jnp.concatenate([cache_keys[0], cache_values[0]], axis=1)
+    cache_all = lax.all_gather(cache_kv, "sp", axis=0, tiled=False)
+
     whole_kv = gather_weights(jnp.concatenate([key_weight, value_weight], axis=1))
     kv_sum = jnp.dot(hidden_rows, whole_kv[:model_width], preferred_element_type=jnp.float32)
-    key_sum = kv_sum[:, :kv_cols]
-    value_sum = kv_sum[:, kv_cols:]
-    new_keys = rotate(key_sum, cosine_table, sine_table, kv_local).astype(jnp.bfloat16)
-    new_values = value_sum.astype(jnp.bfloat16)
-    by_heads = lax.all_to_all(queries, "sp", split_axis=1, concat_axis=0, tiled=True)
-    rotated_q = rotate(by_heads.astype(jnp.float32), cosine_table, sine_table, heads_local).astype(
+    new_keys = rotate(kv_sum[:, :kv_cols], cosine_table, sine_table, kv_local).astype(jnp.bfloat16)
+    new_values = kv_sum[:, kv_cols:].astype(jnp.bfloat16)
+    new_all = lax.all_gather(
+        jnp.concatenate([new_keys, new_values], axis=1), "sp", axis=0, tiled=False
+    )
+
+    rotated_q = rotate(queries.astype(jnp.float32), query_cosine, query_sine, HQ).astype(
         jnp.bfloat16
     )
-    query_heads = rotated_q.reshape(span_rows, kv_local, group_size, HD).transpose(1, 2, 0, 3)
-    by_tokens = attend_all(
-        query_heads, full_old_keys, full_old_values, new_keys, new_values, live_count
-    )
-    return lax.all_to_all(by_tokens, "sp", split_axis=0, concat_axis=1, tiled=True)
+    query_heads = rotated_q.reshape(query_rows, KVH, group_size, HD)
+    scale = HD ** (-0.5)
+    old_keys = cache_all[:, :, :HD]
+    old_values = cache_all[:, :, HD:]
+    fresh_keys = new_all[:, :, :HD]
+    fresh_values = new_all[:, :, HD:]
+    old_scores = jnp.einsum(
+        "thgd,hjd->hgtj", query_heads, old_keys, preferred_element_type=jnp.float32
+    ) * scale
+    new_scores = jnp.einsum(
+        "thgd,hud->hgtu", query_heads, fresh_keys, preferred_element_type=jnp.float32
+    ) * scale
+    slot_index = jnp.arange(slot_total, dtype=jnp.int32)
+    old_visible = (slot_index >= slot_total - live_count)[None, None, None, :]
+    key_index = jnp.arange(span_rows, dtype=jnp.int32)
+    query_index = first_query + jnp.arange(query_rows, dtype=jnp.int32)
+    new_visible = (key_index[None, :] <= query_index[:, None])[None, None, :, :]
+    old_scores = jnp.where(old_visible, old_scores, -1e30)
+    new_scores = jnp.where(new_visible, new_scores, -1e30)
+    row_max = jnp.maximum(jnp.max(old_scores, axis=-1), jnp.max(new_scores, axis=-1))[..., None]
+    old_weights = jnp.where(old_visible, jnp.exp(old_scores - row_max), 0.0)
+    new_weights = jnp.where(new_visible, jnp.exp(new_scores - row_max), 0.0)
+    total = jnp.sum(old_weights, axis=-1) + jnp.sum(new_weights, axis=-1)
+    summed = jnp.einsum(
+        "hgtj,hjd->hgtd",
+        old_weights.astype(jnp.bfloat16),
+        old_values,
+        preferred_element_type=jnp.float32,
+    ) + jnp.einsum(
+        "hgtu,hud->hgtd",
+        new_weights.astype(jnp.bfloat16),
+        fresh_values,
+        preferred_element_type=jnp.float32,
+    )
+    result = (summed / total[..., None]).astype(jnp.bfloat16)
+    return result.transpose(2, 0, 1, 3).reshape(query_rows, HQ * HD)
 
 
 def solution(mesh):

time: 212 us -> 207 us (0.976); the launches traced: 208 us -> 206 us
  waiting for transfers between devices: 89.7 us -> 115 us
  blocking collectives: 39.5 us -> 28.7 us
  local copies, waits for them, and re-layouts: 34.6 us -> 26.7 us
  starting transfers between devices: 6.49 us -> 0.09 us
    all_gather x2, waiting for transfers between devices: 65.7 us -> 95 us  [gather_weights(): gathered = lax.all_gather(gathered, stage, axis=0, tiled=False)]
    all_to_all x1 -> x0, blocking collectives: 25.7 us -> none  [per_device(): lax.all_to_all(by_tokens, 'sp', split_axis=0, concat_axis=1, tiled=True)]
    all_to_all x1 -> x0, waiting for transfers between devices: 24 us -> none  [per_device(): lax.all_to_all(queries, 'sp', split_axis=1, concat_axis=0, tiled=True)]
    all_gather x0 -> x1, waiting for transfers between devices: none -> 20.3 us  [per_device(): lax.all_gather(jnp.concatenate([new_keys, new_values], axis=1), 'sp', axi...]
    all_gather x0 -> x1, blocking collectives: none -> 14.9 us  [per_device(): cache_all = lax.all_gather(cache_kv, 'sp', axis=0, tiled=False)]
    all_to_all x1 -> x0, starting transfers between devices: 6.45 us -> none  [per_device(): lax.all_to_all(queries, 'sp', split_axis=1, concat_axis=0, tiled=True)]
    convert_element_type x3 -> x0, local copies, waits for them, and re-layouts: 5.45 us -> none  [the longest x2 4.79 us: per_device(): by_heads.astype(jnp.float32)]
    all_to_all x3 -> x0, local copies, waits for them, and re-layouts: 2.46 us -> none  [per_device(): lax.all_to_all(by_tokens, 'sp', split_axis=0, concat_axis=1, tiled=True)]
  transfers between devices with their start and end apart: 3 -> 3, of which waited for: 2 -> 3; matrix products, arithmetic and copies ran while one was open for 6% -> 2% of each run, Pallas kernels for 0% -> 0%
where the time goes in v3:
time: 207 us; the launch traced here: 206 us
  waiting for transfers between devices  115 us (56%)
  blocking collectives  28.7 us (14%)
  local copies, waits for them, and re-layouts  26.7 us (13%)
  matrix products  14.7 us (7%)
  between operations  14.7 us (7%)
  other arithmetic  6.27 us (3%)
    all_gather x2, waiting for transfers between devices, gather_weights(): gathered = lax.all_gather(gathered, stage, axis=0, tiled=False)  95 us
    all_gather x1, waiting for transfers between devices, per_device(): lax.all_gather(jnp.concatenate([new_keys, new_values], axis=1), 'sp', axi...  20.3 us
    all_gather x1, blocking collectives, per_device(): cache_all = lax.all_gather(cache_kv, 'sp', axis=0, tiled=False)  14.9 us
    all_gather x2, blocking collectives, gather_weights(): gathered = lax.all_gather(gathered, stage, axis=0, tiled=False)  13.7 us
    all_gather x3, local copies, waits for them, and re-layouts, gather_weights(): gathered = lax.all_gather(gathered, stage, axis=0, tiled=False)  10 us
    reshape x1, local copies, waits for them, and re-layouts, gather_weights(): return gathered.reshape(-1, shard.shape[1])  7.26 us
    dot_general x1, matrix products, per_device(): jnp.dot(hidden_rows, whole_kv[:model_width], preferred_element_type=jnp.f...  7.11 us
  transfers between devices with their start and end apart: 3, of which 3 were waited for; matrix products, arithmetic and copies ran while one was open for 2% of the time, Pallas kernels for 0%

profile of v3, /device:TPU:1, one launch (start us, length us, event | category | flops | bytes accessed | tf_op | source)
XLA Modules:
  0.0 206.5 jit_solution(8669007267215039043)
XLA Ops:
  6.5 0.0 all-gather.11.cloned.1.call-start
  6.5 0.7 maximum_bitcast_fusion
  7.3 4.0 %all-gather.6 = bf16[2,43,256]{2,1,0:T(8,128)(2,1)S(1)} all-gather(bf16[1,43,256]{2,1,0:T(8,128)(2,1)S(1)} %maximum_bitcast_fusion), channel_id=3, replica_groups=mesh['ylo'=2,'x'=4,'z'=12,'core'=2,'sp'=4] {'ylo'}, dimensions={0}, use_global_device_ids=true | all-gather | bytes 66048 | tf_op jit(solution)/shard_map/all_gather | solution.py:118
  11.2 9.8 %all-gather.2 = bf16[8,43,256]{2,1,0:T(8,128)(2,1)S(1)} all-gather(bf16[2,43,256]{2,1,0:T(8,128)(2,1)S(1)} %all-gather.6), channel_id=4, replica_groups=mesh['ylo'=2,'x'=4,'z'=12,'core'=2,'sp'=4] {'x'}, dimensions={0}, use_global_device_ids=true | all-gather | bytes 220160 | tf_op jit(solution)/shard_map/all_gather | solution.py:118
  21.0 0.8 copy.39
  21.8 0.0 all-gather.11.cloned.1.call-update
  21.8 0.0 all-gather.13.cloned.1.call-start
  21.9 65.7 %all-gather.11.cloned.1.call-done = bf16[48,2,43,256]{3,1,2,0:T(2,128)(2,1)} async-done(((bf16[4,2,43,256]{3,1,2,0:T(2,128)(2,1)}), bf16[48,2,43,256]{3,1,2,0:T(2,128)(2,1)}) %all-gather.11.cloned.1.call-update) | async-done | bytes 2113552 | tf_op jit(solution)/shard_map/all_gather | solution.py:118
  87.6 3.7 %copy.40 = bf16[12,4,2,43,256]{4,1,3,2,0:T(4,128)(2,1)} copy(bf16[12,4,2,43,256]{4,2,3,1,0:T(2,128)(2,1)} %bitcast.84) | data formatting | bytes 4227072 | tf_op jit(solution)/shard_map/all_gather | solution.py:118
  91.3 0.0 all-gather.13.cloned.1.call-update
  91.3 0.0 all-gather.15.cloned.1.call-start
  92.8 29.3 %all-gather.13.cloned.1.call-done = bf16[24,4,2,43,256]{4,1,3,2,0:T(4,128)(2,1)} async-done(((bf16[12,4,2,43,256]{4,1,3,2,0:T(4,128)(2,1)}), bf16[24,4,2,43,256]{4,1,3,2,0:T(4,128)(2,1)}) %all-gather.13.cloned.1.call-update) | async-done | bytes 4227088 | tf_op jit(solution)/shard_map/all_gather | solution.py:118
  122.0 5.5 %copy.41 = bf16[24,4,2,43,256]{4,2,3,1,0:T(2,128)(2,1)S(1)} copy(bf16[24,4,2,43,256]{4,1,3,2,0:T(4,128)(2,1)} %all-gather.13.cloned.1.call-done) | data formatting | bytes 8454144 | tf_op jit(solution)/shard_map/all_gather | solution.py:118
  127.5 3.1 %copy.42 = bf16[2,4,12,2,43,256]{5,4,3,2,1,0:T(8,128)(2,1)} copy(bf16[2,4,12,2,43,256]{5,0,4,1,2,3:T(2,128)(2,1)S(1)} %bitcast.80) | data formatting | bytes 8454144 | tf_op jit(solution)/shard_map/transpose | solution.py:127
  130.6 7.3 %reshape.233 = bf16[8256,256]{1,0:T(8,128)(2,1)} reshape(bf16[2,4,12,2,43,256]{5,4,3,2,1,0:T(8,128)(2,1)} %copy.42) | data formatting | bytes 8454144 | tf_op jit(solution)/shard_map/reshape | solution.py:128
  137.9 0.0 copy-start.1
  137.9 7.1 %fusion.23 = f32[512,256]{0,1:T(8,128)S(1)} fusion(bf16[512,8192]{1,0:T(8,128)(2,1)} %param.8, bf16[8256,256]{1,0:T(8,128)(2,1)} %reshape.233), kind=kOutput, calls=%fused_computation.25 | convolution fusion | flops 2147483648 | bytes 13107200 | tf_op jit(solution)/shard_map/dot_general | solution.py:156
  145.0 0.0 copy-start.3
  145.0 0.0 copy-start.4
  145.1 0.6 fusion.33
  145.7 0.7 pad_maximum_fusion.1
  146.4 0.0 all-gather.15.cloned.1.call-update
  146.5 0.0 copy-done.1
  146.5 0.7 copy.37
  147.1 0.3 convert.21
  147.4 0.0 copy-done.3
  147.4 0.0 copy-done.4
  147.4 0.2 fusion.39
  147.6 0.3 subtract_convert_fusion
  148.0 0.1 pad_maximum_fusion
  148.1 14.9 %all-gather = bf16[1024,256]{1,0:T(8,128)(2,1)S(1)} all-gather(bf16[256,256]{1,0:T(8,128)(2,1)S(1)} %pad_maximum_fusion.2), channel_id=2, replica_groups=mesh['ylo'=2,'x'=4,'z'=12,'core'=2,'sp'=4] {'sp'}, dimensions={0}, use_global_device_ids=true | all-gather | bytes 655360 | tf_op jit(solution)/shard_map/all_gather | solution.py:153
  163.0 2.7 %bitcast_reduce_fusion = (f32[4,8,128]{2,1,0:T(8,128)S(1)}, f32[4,256,128,8]{2,1,3,0:T(8,128)}) fusion(pred[256]{0:T(512)(128)(4,1)S(1)} %iota_compare_fusion.1, bf16[128,4,8,128]{0,3,2,1:T(8,128)(2,1)S(1)} %bitcast.81, bf16[4,256,256]{2,1,0:T(8,128)(2,1)S(1)} %bitcast.85), kind=kOutput, calls=%fused_computation.8 | convolution fusion | flops 271577088 | bytes 5521920 | tf_op jit(solution)/shard_map/thgd,hjd->hgtj/dot_general | solution.py:172
  165.7 20.3 %all-gather.15.cloned.1.call-done = bf16[2048,256]{0,1:T(8,128)(2,1)} async-done(((bf16[512,256]{0,1:T(8,128)(2,1)}), bf16[2048,256]{0,1:T(8,128)(2,1)}) %all-gather.15.cloned.1.call-update) | async-done | bytes 1048592 | tf_op jit(solution)/shard_map/all_gather | solution.py:159
  186.0 1.8 reshape.243
  187.9 1.2 fusion.47
  189.0 0.4 copy.60
  189.5 0.0 copy-start
  189.5 1.3 fusion
  190.8 0.9 copy-done
  191.7 1.2 fusion.12
  192.8 1.1 fusion.10
  194.0 0.0 copy-start.2
  194.0 2.1 %fusion.1 = f32[4,8,128]{2,1,0:T(8,128)S(1)} fusion(f32[4,512,128,8]{2,1,3,0:T(8,128)S(1)} %get-tuple-element.16, f32[4,8,128]{2,1,0:T(8,128)S(1)} %max.16, pred[128,512]{0,1:T(8,128)(4,1)S(1)} %iota_compare_fusion), kind=kLoop, calls=%fused_computation.3 | loop fusion | flops 10481664 | bytes 8486912 | tf_op jit(solution)/shard_map/reduce_sum | solution.py:188
  196.1 0.0 copy-done.2
  196.2 2.5 %fusion.14 = bf16[128,4,8,128]{0,3,2,1:T(8,128)(2,1)S(1)} fusion(f32[4,8,128,128]{2,3,1,0:T(8,128)S(1)} %fusion.12, f32[4,512,128,8]{2,1,3,0:T(8,128)S(1)} %get-tuple-element.16, f32[4,8,128]{2,1,0:T(8,128)S(1)} %max.16, pred[128,512]{0,1:T(8,128)(4,1)S(1)} %iota_compare_fusion, f32[128,4,8]{0,2,1:T(8,128)S(1)} %add_bitcast_fusion, ...), kind=kOutput, calls=%fused_computation.18 | convolution fusion | flops 548929536 | bytes 12156928 | tf_op jit(solution)/shard_map/hgtu,hud->hgtd/dot_general | solution.py:194
  198.6 1.3 copy.49
  (12 shorter events, 0.2 us)
Async XLA Ops:
  6.5 81.0 %all-gather.11.cloned.1.call-start = ((), (), s32[]{:S(2)}) async-start(), calls=%async_computation | async-start | bytes 2289664 | tf_op jit(solution)/shard_map/all_gather | solution.py:118
  21.8 100.2 %all-gather.13.cloned.1.call-start = ((), (), s32[]{:S(2)}) async-start(), calls=%async_computation.1 | async-start | bytes 6340608 | tf_op jit(solution)/shard_map/all_gather | solution.py:118
  91.3 94.7 %all-gather.15.cloned.1.call-start = ((), (), s32[]{:S(2)}) async-start(), calls=%async_computation.2 | async-start | bytes 1310720 | tf_op jit(solution)/shard_map/all_gather | solution.py:159
  137.9 8.6 %copy-start.1 = (bf16[128,4096]{1,0:T(8,128)(2,1)S(1)}, bf16[128,4096]{1,0:T(8,128)(2,1)}, u32[]{:S(2)}) copy-start(bf16[128,4096]{1,0:T(8,128)(2,1)} %param.9) | copy-start | bytes 3145732
  145.0 2.4 %copy-start.3 = (bf16[1,256,128]{2,1,0:T(8,128)(2,1)S(1)}, bf16[1,256,128]{2,1,0:T(8,128)(2,1)}, u32[]{:S(2)}) copy-start(bf16[1,256,128]{2,1,0:T(8,128)(2,1)} %param.13) | copy-start | bytes 196612
  145.0 2.4 %copy-start.4 = (bf16[1,256,128]{2,1,0:T(8,128)(2,1)S(1)}, bf16[1,256,128]{2,1,0:T(8,128)(2,1)}, u32[]{:S(2)}) copy-start(bf16[1,256,128]{2,1,0:T(8,128)(2,1)} %param.12) | copy-start | bytes 196612
  189.5 2.2 %copy-start = (f32[4,256,128,8]{2,1,3,0:T(8,128)S(1)}, f32[4,256,128,8]{2,1,3,0:T(8,128)}, u32[]{:S(2)}) copy-start(f32[4,256,128,8]{2,1,3,0:T(8,128)} %get-tuple-element.14) | copy-start | bytes 12582916
  194.0 2.2 %copy-start.2 = (bf16[4,512,128]{1,0,2:T(4,128)(2,1)S(1)}, bf16[4,512,128]{1,0,2:T(4,128)(2,1)}, u32[]{:S(2)}) copy-start(bf16[4,512,128]{1,0,2:T(4,128)(2,1)} %get-tuple-element.7) | copy-start | bytes 1572868
Sparse Core Ops, SparseCore 0:
  22.0 65.5 all-gather.10
  91.5 30.5 all-gather.12
  146.6 39.4 all-gather.14

commit v4 on v3

--- a/solution.py
+++ b/solution.py
@@ -126,6 +126,18 @@
     rank = len(FSDP_AXES)
     gathered = gathered.transpose(perm + [rank, rank + 1])
     return gathered.reshape(-1, shard.shape[1])
+
+
+def gather_sp(block):
+    count = lax.axis_size("sp")
+    here = lax.axis_index("sp")
+    pieces = [block]
+    for shift in range(1, count):
+        pairs = [(source, (source + shift) % count) for source in range(count)]
+        pieces.append(lax.ppermute(block, "sp", perm=pairs))
+    stacked = jnp.stack(pieces)
+    order = (here - jnp.arange(count, dtype=jnp.int32)) % count
+    return jnp.take(stacked, order, axis=0)
 
 
 def per_device(
@@ -150,15 +162,13 @@
     live_count = prefix_len[0]
 
     cache_kv = jnp.concatenate([cache_keys[0], cache_values[0]], axis=1)
-    cache_all = lax.all_gather(cache_kv, "sp", axis=0, tiled=False)
+    cache_all = gather_sp(cache_kv)
 
     whole_kv = gather_weights(jnp.concatenate([key_weight, value_weight], axis=1))
     kv_sum = jnp.dot(hidden_rows, whole_kv[:model_width], preferred_element_type=jnp.float32)
     new_keys = rotate(kv_sum[:, :kv_cols], cosine_table, sine_table, kv_local).astype(jnp.bfloat16)
     new_values = kv_sum[:, kv_cols:].astype(jnp.bfloat16)
-    new_all = lax.all_gather(
-        jnp.concatenate([new_keys, new_values], axis=1), "sp", axis=0, tiled=False
-    )
+    new_all = gather_sp(jnp.concatenate([new_keys, new_values], axis=1))
 
     rotated_q = rotate(queries.astype(jnp.float32), query_cosine, query_sine, HQ).astype(
         jnp.bfloat16

time: 207 us -> 197 us (0.952)
  the two profiles are of different devices: /device:TPU:1 before, /device:TPU:9 now
where the time goes in v4:
time: 197 us; the launch traced here: 196 us
  waiting for transfers between devices  96.9 us (49%)
  starting transfers between devices  25 us (13%)
  local copies, waits for them, and re-layouts  24.5 us (12%)
  between operations  15.1 us (8%)
  matrix products  14.8 us (8%)
  blocking collectives  12.9 us (7%)
  other arithmetic  7.29 us (4%)
    all_gather x2, waiting for transfers between devices, gather_weights(): gathered = lax.all_gather(gathered, stage, axis=0, tiled=False)  74.1 us
    ppermute x6, starting transfers between devices, gather_sp(): pieces.append(lax.ppermute(block, 'sp', perm=pairs))  24.9 us
    ppermute x6, waiting for transfers between devices, gather_sp(): pieces.append(lax.ppermute(block, 'sp', perm=pairs))  22.7 us
    all_gather x2, blocking collectives, gather_weights(): gathered = lax.all_gather(gathered, stage, axis=0, tiled=False)  12.9 us
    all_gather x3, local copies, waits for them, and re-layouts, gather_weights(): gathered = lax.all_gather(gathered, stage, axis=0, tiled=False)  10 us
    reshape x1, local copies, waits for them, and re-layouts, gather_weights(): return gathered.reshape(-1, shard.shape[1])  7.27 us
    dot_general x1, matrix products, per_device(): jnp.dot(hidden_rows, whole_kv[:model_width], preferred_element_type=jnp.f...  7.03 us
  transfers between devices with their start and end apart: 8, of which 6 were waited for; matrix products, arithmetic and copies ran while one was open for 3% of the time, Pallas kernels for 0%

profile of v4, /device:TPU:9, one launch (start us, length us, event | category | flops | bytes accessed | tf_op | source)
XLA Modules:
  0.0 196.4 jit_solution(637120315192423677)
XLA Ops:
  6.5 0.8 maximum_bitcast_fusion
  7.4 3.3 %all-gather.4 = bf16[2,43,256]{2,1,0:T(8,128)(2,1)S(1)} all-gather(bf16[1,43,256]{2,1,0:T(8,128)(2,1)S(1)} %maximum_bitcast_fusion), channel_id=2, replica_groups=mesh['ylo'=2,'x'=4,'z'=12,'core'=2,'sp'=4] {'ylo'}, dimensions={0}, use_global_device_ids=true | all-gather | bytes 66048 | tf_op jit(solution)/shard_map/all_gather | solution.py:118
  10.7 9.6 %all-gather.1 = bf16[8,43,256]{2,1,0:T(8,128)(2,1)S(1)} all-gather(bf16[2,43,256]{2,1,0:T(8,128)(2,1)S(1)} %all-gather.4), channel_id=3, replica_groups=mesh['ylo'=2,'x'=4,'z'=12,'core'=2,'sp'=4] {'x'}, dimensions={0}, use_global_device_ids=true | all-gather | bytes 220160 | tf_op jit(solution)/shard_map/all_gather | solution.py:118
  20.3 0.8 copy.36
  21.1 0.0 all-gather.8.cloned.1.call-update
  21.1 0.0 all-gather.10.cloned.1.call-start
  21.2 65.6 %all-gather.8.cloned.1.call-done = bf16[48,2,43,256]{3,1,2,0:T(2,128)(2,1)} async-done(((bf16[4,2,43,256]{3,1,2,0:T(2,128)(2,1)}), bf16[48,2,43,256]{3,1,2,0:T(2,128)(2,1)}) %all-gather.8.cloned.1.call-update) | async-done | bytes 2113552 | tf_op jit(solution)/shard_map/all_gather | solution.py:118
  86.8 3.8 %copy.37 = bf16[12,4,2,43,256]{4,1,3,2,0:T(4,128)(2,1)} copy(bf16[12,4,2,43,256]{4,2,3,1,0:T(2,128)(2,1)} %bitcast.93) | data formatting | bytes 4227072 | tf_op jit(solution)/shard_map/all_gather | solution.py:118
  90.5 0.0 all-gather.10.cloned.1.call-update
  90.6 4.4 %collective-permute-start.2 = (bf16[256,256]{1,0:T(8,128)(2,1)S(1)}, bf16[256,256]{1,0:T(8,128)(2,1)}, u32[]{:S(2)}, u32[]{:S(2)}) collective-permute-start(bf16[256,256]{1,0:T(8,128)(2,1)S(1)} %get-tuple-element.12), channel_id=1, source_target_pairs={{0,3},{1,0},{2,1},{3,2},{4,7},{5,4},{6,5},{7,6},{8,11},{9,8},{10,9... | collective-permute-start | bytes 393224 | tf_op jit(solution)/shard_map/ppermute | solution.py:137
  95.1 4.8 %collective-permute-start.1 = (bf16[256,256]{1,0:T(8,128)(2,1)S(1)}, bf16[256,256]{1,0:T(8,128)(2,1)}, u32[]{:S(2)}, u32[]{:S(2)}) collective-permute-start(bf16[256,256]{1,0:T(8,128)(2,1)S(1)} %get-tuple-element.12), channel_id=1, source_target_pairs={{0,2},{1,3},{2,0},{3,1},{4,6},{5,7},{6,4},{7,5},{8,10},{9,11},{10,... | collective-permute-start | bytes 393224 | tf_op jit(solution)/shard_map/ppermute | solution.py:137
  99.9 3.1 %collective-permute-start = (bf16[256,256]{1,0:T(8,128)(2,1)S(1)}, bf16[256,256]{1,0:T(8,128)(2,1)}, u32[]{:S(2)}, u32[]{:S(2)}) collective-permute-start(bf16[256,256]{1,0:T(8,128)(2,1)S(1)} %get-tuple-element.12), channel_id=1, source_target_pairs={{0,1},{1,2},{2,3},{3,0},{4,5},{5,6},{6,7},{7,4},{8,9},{9,10},{10,1... | collective-permute-start | bytes 393224 | tf_op jit(solution)/shard_map/ppermute | solution.py:137
  103.7 0.7 copy.34
  104.3 0.2 convert.21
  105.4 0.2 fusion.38
  105.6 0.3 subtract_convert_fusion
  106.0 0.1 pad_maximum_fusion
  106.1 0.0 collective-permute-done.2
  106.1 0.1 collective-permute-done.1
  106.2 3.0 %collective-permute-done = bf16[256,256]{1,0:T(8,128)(2,1)} collective-permute-done((bf16[256,256]{1,0:T(8,128)(2,1)S(1)}, bf16[256,256]{1,0:T(8,128)(2,1)}, u32[]{:S(2)}, u32[]{:S(2)}) %collective-permute-start) | collective-permute-done | bytes 131104 | tf_op jit(solution)/shard_map/ppermute | solution.py:137
  109.2 1.1 pad_maximum_fusion.2
  110.3 0.6 gather_fusion
  110.9 0.1 broadcast_select_fusion.1
  111.0 0.0 copy-start.1
  111.0 8.5 %all-gather.10.cloned.1.call-done = bf16[24,4,2,43,256]{4,1,3,2,0:T(4,128)(2,1)} async-done(((bf16[12,4,2,43,256]{4,1,3,2,0:T(4,128)(2,1)}), bf16[24,4,2,43,256]{4,1,3,2,0:T(4,128)(2,1)}) %all-gather.10.cloned.1.call-update) | async-done | bytes 4227088 | tf_op jit(solution)/shard_map/all_gather | solution.py:118
  119.5 5.5 %copy.38 = bf16[24,4,2,43,256]{4,2,3,1,0:T(2,128)(2,1)S(1)} copy(bf16[24,4,2,43,256]{4,1,3,2,0:T(4,128)(2,1)} %all-gather.10.cloned.1.call-done) | data formatting | bytes 8454144 | tf_op jit(solution)/shard_map/all_gather | solution.py:118
  125.0 3.1 %copy.39 = bf16[2,4,12,2,43,256]{5,4,3,2,1,0:T(8,128)(2,1)} copy(bf16[2,4,12,2,43,256]{5,0,4,1,2,3:T(2,128)(2,1)S(1)} %bitcast.89) | data formatting | bytes 8454144 | tf_op jit(solution)/shard_map/transpose | solution.py:127
  128.1 7.3 %reshape.287 = bf16[8256,256]{1,0:T(8,128)(2,1)} reshape(bf16[2,4,12,2,43,256]{5,4,3,2,1,0:T(8,128)(2,1)} %copy.39) | data formatting | bytes 8454144 | tf_op jit(solution)/shard_map/reshape | solution.py:128
  135.4 7.0 %fusion.23 = f32[512,256]{0,1:T(8,128)S(1)} fusion(bf16[512,8192]{1,0:T(8,128)(2,1)} %param.8, bf16[8256,256]{1,0:T(8,128)(2,1)} %reshape.287), kind=kOutput, calls=%fused_computation.27 | convolution fusion | flops 2147483648 | bytes 13107200 | tf_op jit(solution)/shard_map/dot_general | solution.py:168
  142.5 0.6 fusion.32
  143.1 4.4 %collective-permute-start.5 = (bf16[512,256]{0,1:T(8,128)(2,1)S(1)}, bf16[512,256]{0,1:T(8,128)(2,1)S(1)}, u32[]{:S(2)}, u32[]{:S(2)}) collective-permute-start(bf16[512,256]{0,1:T(8,128)(2,1)S(1)} %get-tuple-element.10), channel_id=1, source_target_pairs={{0,3},{1,0},{2,1},{3,2},{4,7},{5,4},{6,5},{7,6},{8,11},{9,8},{10,9... | collective-permute-start | bytes 786440 | tf_op jit(solution)/shard_map/ppermute | solution.py:137
  147.6 4.8 %collective-permute-start.4 = (bf16[512,256]{0,1:T(8,128)(2,1)S(1)}, bf16[512,256]{0,1:T(8,128)(2,1)S(1)}, u32[]{:S(2)}, u32[]{:S(2)}) collective-permute-start(bf16[512,256]{0,1:T(8,128)(2,1)S(1)} %get-tuple-element.10), channel_id=1, source_target_pairs={{0,2},{1,3},{2,0},{3,1},{4,6},{5,7},{6,4},{7,5},{8,10},{9,11},{10,... | collective-permute-start | bytes 786440 | tf_op jit(solution)/shard_map/ppermute | solution.py:137
  152.4 3.3 %collective-permute-start.3 = (bf16[512,256]{0,1:T(8,128)(2,1)S(1)}, bf16[512,256]{0,1:T(8,128)(2,1)S(1)}, u32[]{:S(2)}, u32[]{:S(2)}) collective-permute-start(bf16[512,256]{0,1:T(8,128)(2,1)S(1)} %get-tuple-element.10), channel_id=1, source_target_pairs={{0,1},{1,2},{2,3},{3,0},{4,5},{5,6},{6,7},{7,4},{8,9},{9,10},{10,1... | collective-permute-start | bytes 786440 | tf_op jit(solution)/shard_map/ppermute | solution.py:137
  155.7 2.7 %bitcast_reduce_fusion = (f32[4,8,128]{2,1,0:T(8,128)S(1)}, f32[4,256,128,8]{2,1,3,0:T(8,128)}) fusion(pred[256]{0:T(512)(128)(4,1)S(1)} %iota_compare_fusion.1, bf16[128,4,8,128]{0,3,2,1:T(8,128)(2,1)S(1)} %bitcast.90, bf16[4,256,256]{2,1,0:T(8,128)(2,1)S(1)} %broadcast_select_fusion.1), kind=kOutput, calls=%fused_computation.10 | convolution fusion | flops 271577088 | bytes 5521920 | tf_op jit(solution)/shard_map/thgd,hjd->hgtj/dot_general | solution.py:182
  158.4 15.1 %collective-permute-done.4 = bf16[512,256]{0,1:T(8,128)(2,1)S(1)} collective-permute-done((bf16[512,256]{0,1:T(8,128)(2,1)S(1)}, bf16[512,256]{0,1:T(8,128)(2,1)S(1)}, u32[]{:S(2)}, u32[]{:S(2)}) %collective-permute-start.4) | collective-permute-done | bytes 262176 | tf_op jit(solution)/shard_map/ppermute | solution.py:137
  173.5 4.5 %collective-permute-done.3 = bf16[512,256]{0,1:T(8,128)(2,1)S(1)} collective-permute-done((bf16[512,256]{0,1:T(8,128)(2,1)S(1)}, bf16[512,256]{0,1:T(8,128)(2,1)S(1)}, u32[]{:S(2)}, u32[]{:S(2)}) %collective-permute-start.3) | collective-permute-done | bytes 262176 | tf_op jit(solution)/shard_map/ppermute | solution.py:137
  178.0 0.1 pad_maximum_fusion.1
  178.2 0.6 gather_fusion.1
  178.8 0.2 broadcast_select_fusion
  179.0 0.0 copy-start.2
  179.0 1.4 fusion
  180.4 0.7 copy-done
  181.1 0.1 copy-done.2
  181.2 1.2 fusion.12
  182.4 1.2 fusion.10
  183.6 2.2 %fusion.1 = f32[4,8,128]{2,1,0:T(8,128)S(1)} fusion(f32[4,512,128,8]{2,1,3,0:T(8,128)S(1)} %get-tuple-element.18, f32[4,8,128]{2,1,0:T(8,128)S(1)} %max.16, pred[128,512]{0,1:T(8,128)(4,1)S(1)} %iota_compare_fusion), kind=kLoop, calls=%fused_computation.5 | loop fusion | flops 10481664 | bytes 8486912 | tf_op jit(solution)/shard_map/reduce_sum | solution.py:198
  185.8 2.5 %fusion.14 = bf16[128,4,8,128]{0,3,2,1:T(8,128)(2,1)S(1)} fusion(f32[4,8,128,128]{2,3,1,0:T(8,128)S(1)} %fusion.12, f32[4,512,128,8]{2,1,3,0:T(8,128)S(1)} %get-tuple-element.18, f32[4,8,128]{2,1,0:T(8,128)S(1)} %max.16, pred[128,512]{0,1:T(8,128)(4,1)S(1)} %iota_compare_fusion, f32[128,4,8]{0,2,1:T(8,128)S(1)} %add_bitcast_fusion, ...), kind=kOutput, calls=%fused_computation.20 | convolution fusion | flops 548929536 | bytes 12156928 | tf_op jit(solution)/shard_map/hgtu,hud->hgtd/dot_general | solution.py:204
  188.3 1.3 copy.45
  (26 shorter events, 0.3 us)
Async XLA Ops:
  6.5 84.0 %copy-start.4 = (bf16[1,256,128]{2,1,0:T(8,128)(2,1)S(1)}, bf16[1,256,128]{2,1,0:T(8,128)(2,1)}, u32[]{:S(2)}) copy-start(bf16[1,256,128]{2,1,0:T(8,128)(2,1)} %param.13) | copy-start | bytes 196612
  6.5 84.0 %copy-start.5 = (bf16[1,256,128]{2,1,0:T(8,128)(2,1)S(1)}, bf16[1,256,128]{2,1,0:T(8,128)(2,1)}, u32[]{:S(2)}) copy-start(bf16[1,256,128]{2,1,0:T(8,128)(2,1)} %param.12) | copy-start | bytes 196612
  6.5 97.1 %copy-start.3 = (bf16[128,4096]{1,0:T(8,128)(2,1)S(1)}, bf16[128,4096]{1,0:T(8,128)(2,1)}, u32[]{:S(2)}) copy-start(bf16[128,4096]{1,0:T(8,128)(2,1)} %param.9) | copy-start | bytes 3145732
  6.5 80.2 %all-gather.8.cloned.1.call-start = ((), (), s32[]{:S(2)}) async-start(), calls=%async_computation | async-start | bytes 2289664 | tf_op jit(solution)/shard_map/all_gather | solution.py:118
  21.1 98.4 %all-gather.10.cloned.1.call-start = ((), (), s32[]{:S(2)}) async-start(), calls=%async_computation.1 | async-start | bytes 6340608 | tf_op jit(solution)/shard_map/all_gather | solution.py:118
  90.6 15.5 %collective-permute-start.2 = (bf16[256,256]{1,0:T(8,128)(2,1)S(1)}, bf16[256,256]{1,0:T(8,128)(2,1)}, u32[]{:S(2)}, u32[]{:S(2)}) collective-permute-start(bf16[256,256]{1,0:T(8,128)(2,1)S(1)} %get-tuple-element.12), channel_id=1, source_target_pairs={{0,3},{1,0},{2,1},{3,2},{4,7},{5,4},{6,5},{7,6},{8,11},{9,8},{10,9... | collective-permute-start | bytes 393224 | tf_op jit(solution)/shard_map/ppermute | solution.py:137
  95.1 11.1 %collective-permute-start.1 = (bf16[256,256]{1,0:T(8,128)(2,1)S(1)}, bf16[256,256]{1,0:T(8,128)(2,1)}, u32[]{:S(2)}, u32[]{:S(2)}) collective-permute-start(bf16[256,256]{1,0:T(8,128)(2,1)S(1)} %get-tuple-element.12), channel_id=1, source_target_pairs={{0,2},{1,3},{2,0},{3,1},{4,6},{5,7},{6,4},{7,5},{8,10},{9,11},{10,... | collective-permute-start | bytes 393224 | tf_op jit(solution)/shard_map/ppermute | solution.py:137
  99.9 9.3 %collective-permute-start = (bf16[256,256]{1,0:T(8,128)(2,1)S(1)}, bf16[256,256]{1,0:T(8,128)(2,1)}, u32[]{:S(2)}, u32[]{:S(2)}) collective-permute-start(bf16[256,256]{1,0:T(8,128)(2,1)S(1)} %get-tuple-element.12), channel_id=1, source_target_pairs={{0,1},{1,2},{2,3},{3,0},{4,5},{5,6},{6,7},{7,4},{8,9},{9,10},{10,1... | collective-permute-start | bytes 393224 | tf_op jit(solution)/shard_map/ppermute | solution.py:137
  111.0 44.7 %copy-start.1 = (bf16[4,256,256]{2,1,0:T(8,128)(2,1)}, bf16[4,256,256]{2,1,0:T(8,128)(2,1)S(1)}, u32[]{:S(2)}) copy-start(bf16[4,256,256]{2,1,0:T(8,128)(2,1)S(1)} %broadcast_select_fusion.1) | copy-start | bytes 1572868
  143.1 15.3 %collective-permute-start.5 = (bf16[512,256]{0,1:T(8,128)(2,1)S(1)}, bf16[512,256]{0,1:T(8,128)(2,1)S(1)}, u32[]{:S(2)}, u32[]{:S(2)}) collective-permute-start(bf16[512,256]{0,1:T(8,128)(2,1)S(1)} %get-tuple-element.10), channel_id=1, source_target_pairs={{0,3},{1,0},{2,1},{3,2},{4,7},{5,4},{6,5},{7,6},{8,11},{9,8},{10,9... | collective-permute-start | bytes 786440 | tf_op jit(solution)/shard_map/ppermute | solution.py:137
  147.6 26.0 %collective-permute-start.4 = (bf16[512,256]{0,1:T(8,128)(2,1)S(1)}, bf16[512,256]{0,1:T(8,128)(2,1)S(1)}, u32[]{:S(2)}, u32[]{:S(2)}) collective-permute-start(bf16[512,256]{0,1:T(8,128)(2,1)S(1)} %get-tuple-element.10), channel_id=1, source_target_pairs={{0,2},{1,3},{2,0},{3,1},{4,6},{5,7},{6,4},{7,5},{8,10},{9,11},{10,... | collective-permute-start | bytes 786440 | tf_op jit(solution)/shard_map/ppermute | solution.py:137
  152.4 25.6 %collective-permute-start.3 = (bf16[512,256]{0,1:T(8,128)(2,1)S(1)}, bf16[512,256]{0,1:T(8,128)(2,1)S(1)}, u32[]{:S(2)}, u32[]{:S(2)}) collective-permute-start(bf16[512,256]{0,1:T(8,128)(2,1)S(1)} %get-tuple-element.10), channel_id=1, source_target_pairs={{0,1},{1,2},{2,3},{3,0},{4,5},{5,6},{6,7},{7,4},{8,9},{9,10},{10,1... | collective-permute-start | bytes 786440 | tf_op jit(solution)/shard_map/ppermute | solution.py:137
  178.9 2.2 %copy-start = (f32[4,256,128,8]{2,1,3,0:T(8,128)S(1)}, f32[4,256,128,8]{2,1,3,0:T(8,128)}, u32[]{:S(2)}) copy-start(f32[4,256,128,8]{2,1,3,0:T(8,128)} %get-tuple-element.16) | copy-start | bytes 12582916
  179.0 2.3 %copy-start.2 = (bf16[4,256,256]{2,1,0:T(8,128)(2,1)S(1)}, bf16[4,256,256]{2,1,0:T(8,128)(2,1)}, u32[]{:S(2)}) copy-start(bf16[4,256,256]{2,1,0:T(8,128)(2,1)} %copy-done.1) | copy-start | bytes 1572868
Sparse Core Ops, SparseCore 0:
  21.2 65.4 all-gather.7
  90.7 28.8 all-gather.9

commit v5 on v4

--- a/solution.py
+++ b/solution.py
@@ -119,13 +119,22 @@
         if len(stage) > 1:
             sizes = tuple(dict(FSDP_PARTS)[name] for name in stage)
             gathered = gathered.reshape(sizes + gathered.shape[1:])
+    return gathered.reshape(-1, shard.shape[1])
+
+
+def gathered_order_columns(hidden_rows, shard_rows, padded_rows):
+    sizes = tuple(size for _, size in FSDP_PARTS)
+    devices = math.prod(sizes)
+    rows = hidden_rows.shape[0]
+    wide = jnp.pad(hidden_rows, ((0, 0), (0, devices * shard_rows - hidden_rows.shape[1])))
+    split = wide.reshape((rows,) + sizes + (shard_rows,))
     layout = []
     for stage in reversed(GATHER_STAGES):
         layout.extend(stage)
-    perm = [layout.index(name) for name in FSDP_AXES]
-    rank = len(FSDP_AXES)
-    gathered = gathered.transpose(perm + [rank, rank + 1])
-    return gathered.reshape(-1, shard.shape[1])
+    perm = [0] + [1 + FSDP_AXES.index(name) for name in layout] + [1 + len(FSDP_AXES)]
+    moved = split.transpose(perm)
+    moved = jnp.pad(moved, [(0, 0)] * (len(perm) - 1) + [(0, padded_rows - shard_rows)])
+    return moved.reshape(rows, -1)
 
 
 def gather_sp(block):
@@ -164,11 +173,17 @@
     cache_kv = jnp.concatenate([cache_keys[0], cache_values[0]], axis=1)
     cache_all = gather_sp(cache_kv)
 
-    whole_kv = gather_weights(jnp.concatenate([key_weight, value_weight], axis=1))
-    kv_sum = jnp.dot(hidden_rows, whole_kv[:model_width], preferred_element_type=jnp.float32)
+    shard = jnp.concatenate([key_weight, value_weight], axis=1)
+    shard_rows = shard.shape[0]
+    padded_rows = -(-shard_rows // 16) * 16
+    whole_kv = gather_weights(jnp.pad(shard, ((0, padded_rows - shard_rows), (0, 0))))
+    ordered_rows = gathered_order_columns(hidden_rows, shard_rows, padded_rows)
+    kv_sum = jnp.dot(ordered_rows, whole_kv, preferred_element_type=jnp.float32)
     new_keys = rotate(kv_sum[:, :kv_cols], cosine_table, sine_table, kv_local).astype(jnp.bfloat16)
     new_values = kv_sum[:, kv_cols:].astype(jnp.bfloat16)
-    new_all = gather_sp(jnp.concatenate([new_keys, new_values], axis=1))
+    new_all = lax.all_gather(
+        jnp.concatenate([new_keys, new_values], axis=1), "sp", axis=0, tiled=False
+    )
 
     rotated_q = rotate(queries.astype(jnp.float32), query_cosine, query_sine, HQ).astype(
         jnp.bfloat16

time: 197 us -> 217 us (1.10)
  the two profiles are of different devices: /device:TPU:9 before, /device:TPU:1 now
where the time goes in v5:
time: 217 us; the launch traced here: 216 us
  waiting for transfers between devices  101 us (47%)
  local copies, waits for them, and re-layouts  47.3 us (22%)
  matrix products  15.1 us (7%)
  between operations  14.7 us (7%)
  starting transfers between devices  14.6 us (7%)
  blocking collectives  14.5 us (7%)
  other arithmetic  8.46 us (4%)
    all_gather x2, waiting for transfers between devices, gather_weights(): gathered = lax.all_gather(gathered, stage, axis=0, tiled=False)  66.4 us
    all_gather x1, waiting for transfers between devices, per_device(): lax.all_gather(jnp.concatenate([new_keys, new_values], axis=1), 'sp', axi...  34.8 us
    reshape x2, local copies, waits for them, and re-layouts, gathered_order_columns(): split = wide.reshape((rows,) + sizes + (shard_rows,))  20.1 us
    unnamed x7, local copies, waits for them, and re-layouts  15.1 us
    ppermute x3, starting transfers between devices, gather_sp(): pieces.append(lax.ppermute(block, 'sp', perm=pairs))  14.5 us
    all_gather x2, blocking collectives, gather_weights(): gathered = lax.all_gather(gathered, stage, axis=0, tiled=False)  14.5 us
    dot_general x1, matrix products, per_device(): kv_sum = jnp.dot(ordered_rows, whole_kv, preferred_element_type=jnp.float32)  7.45 us
    pad x1, local copies, waits for them, and re-layouts, gathered_order_columns(): jnp.pad(hidden_rows, ((0, 0), (0, devices * shard_rows - hidden_rows.shap...  7.11 us
  transfers between devices with their start and end apart: 6, of which 2 were waited for; matrix products, arithmetic and copies ran while one was open for 26% of the time, Pallas kernels for 0%

profile of v5, /device:TPU:1, one launch (start us, length us, event | category | flops | bytes accessed | tf_op | source)
XLA Modules:
  0.0 215.8 jit_solution(8664949941994923579)
XLA Ops:
  6.5 0.0 all-gather.9.cloned.1.call-start
  6.5 0.7 fusion.43
  7.3 4.0 %all-gather = bf16[96,256]{1,0:T(8,128)(2,1)S(1)} all-gather(bf16[48,256]{1,0:T(8,128)(2,1)S(1)} %fusion.43), channel_id=2, replica_groups=mesh['ylo'=2,'x'=4,'z'=12,'core'=2,'sp'=4] {'ylo'}, dimensions={0}, use_global_device_ids=true | all-gather | bytes 73728 | tf_op jit(solution)/shard_map/all_gather | solution.py:118
  11.2 10.5 %all-gather.1 = bf16[8,48,256]{2,1,0:T(8,128)(2,1)} all-gather(bf16[2,48,256]{2,1,0:T(8,128)(2,1)S(1)} %bitcast.99), channel_id=3, replica_groups=mesh['ylo'=2,'x'=4,'z'=12,'core'=2,'sp'=4] {'x'}, dimensions={0}, use_global_device_ids=true | all-gather | bytes 245760 | tf_op jit(solution)/shard_map/all_gather | solution.py:118
  21.8 0.0 all-gather.9.cloned.1.call-update
  21.8 0.0 all-gather.11.cloned.1.call-start
  21.8 66.4 %all-gather.9.cloned.1.call-done = bf16[48,2,48,256]{3,2,1,0:T(8,128)(2,1)} async-done(((bf16[4,2,48,256]{3,2,1,0:T(8,128)(2,1)}), bf16[48,2,48,256]{3,2,1,0:T(8,128)(2,1)}) %all-gather.9.cloned.1.call-update) | async-done | bytes 2359312 | tf_op jit(solution)/shard_map/all_gather | solution.py:118
  88.2 0.0 all-gather.11.cloned.1.call-update
  88.2 0.0 all-gather.13.cloned.1.call-start
  88.3 0.9 fusion.54
  89.2 4.0 %collective-permute-start = (bf16[256,256]{1,0:T(8,128)(2,1)S(1)}, bf16[256,256]{1,0:T(8,128)(2,1)}, u32[]{:S(2)}, u32[]{:S(2)}) collective-permute-start(bf16[256,256]{1,0:T(8,128)(2,1)S(1)} %get-tuple-element.12), channel_id=1, source_target_pairs={{0,1},{1,2},{2,3},{3,0},{4,5},{5,6},{6,7},{7,4},{8,9},{9,10},{10,1... | collective-permute-start | bytes 393224 | tf_op jit(solution)/shard_map/ppermute | solution.py:146
  93.2 5.3 %collective-permute-start.1 = (bf16[256,256]{1,0:T(8,128)(2,1)S(1)}, bf16[256,256]{1,0:T(8,128)(2,1)}, u32[]{:S(2)}, u32[]{:S(2)}) collective-permute-start(bf16[256,256]{1,0:T(8,128)(2,1)S(1)} %get-tuple-element.12), channel_id=1, source_target_pairs={{0,2},{1,3},{2,0},{3,1},{4,6},{5,7},{6,4},{7,5},{8,10},{9,11},{10,... | collective-permute-start | bytes 393224 | tf_op jit(solution)/shard_map/ppermute | solution.py:146
  98.5 5.2 %collective-permute-start.2 = (bf16[256,256]{1,0:T(8,128)(2,1)S(1)}, bf16[256,256]{1,0:T(8,128)(2,1)}, u32[]{:S(2)}, u32[]{:S(2)}) collective-permute-start(bf16[256,256]{1,0:T(8,128)(2,1)S(1)} %get-tuple-element.12), channel_id=1, source_target_pairs={{0,3},{1,0},{2,1},{3,2},{4,7},{5,4},{6,5},{7,6},{8,11},{9,8},{10,9... | collective-permute-start | bytes 393224 | tf_op jit(solution)/shard_map/ppermute | solution.py:146
  104.3 1.6 copy.28
  106.0 0.2 convert.21
  106.9 12.2 %copy.52 = bf16[512,8192]{0,1:T(8,128)(2,1)} copy(bf16[512,8192]{1,0:T(8,128)(2,1)} %param.8) | data formatting | bytes 16777216
  119.1 7.1 %pad.12.clone = bf16[512,8256]{0,1:T(8,128)(2,1)} pad(bf16[512,8192]{0,1:T(8,128)(2,1)} %copy.52, bf16[]{:T(256)} %constant.78.clone.1), padding=0_0x0_64 | pad | bytes 16842754 | tf_op jit(solution)/shard_map/jit(_pad)/pad | solution.py:129
  126.2 11.6 %reshape.289 = bf16[512,2,4,12,2,43]{0,5,4,3,2,1:T(8,128)(2,1)} reshape(bf16[512,8256]{0,1:T(8,128)(2,1)} %pad.12.clone) | data formatting | bytes 16908288 | tf_op jit(solution)/shard_map/reshape | solution.py:130
  137.8 8.5 %copy.56 = bf16[512,2,4,12,2,43]{0,5,1,2,3,4:T(8,128)(2,1)} copy(bf16[512,2,4,12,2,43]{0,5,4,3,2,1:T(8,128)(2,1)} %reshape.289) | data formatting | bytes 16908288 | tf_op jit(solution)/shard_map/reshape | solution.py:130
  146.4 0.0 all-gather.11.cloned.1.call-done
  146.5 7.5 %fusion.23 = f32[512,256]{0,1:T(8,128)S(1)} fusion(bf16[2,12,4,2,48,256]{5,4,3,2,1,0:T(8,128)(2,1)} %bitcast.102, bf16[512,2,12,4,2,43]{0,5,4,3,2,1:T(8,128)(2,1)} %bitcast.92), kind=kOutput, calls=%fused_computation.27 | convolution fusion | flops 2415919104 | bytes 13697024 | tf_op jit(solution)/shard_map/dot_general | solution.py:181
  154.0 0.6 fusion.33
  154.6 0.7 pad_maximum_fusion.2
  155.3 0.0 all-gather.13.cloned.1.call-update
  155.4 0.2 fusion.41
  155.6 0.3 subtract_convert_fusion
  155.9 0.1 pad_maximum_fusion
  156.0 0.0 collective-permute-done
  156.0 0.0 collective-permute-done.1
  156.0 0.0 collective-permute-done.2
  156.0 1.1 pad_maximum_fusion.1
  157.1 0.6 gather_fusion
  157.7 0.1 broadcast_select_fusion
  157.9 2.7 %bitcast_reduce_fusion = (f32[4,8,128]{2,1,0:T(8,128)S(1)}, f32[4,256,128,8]{2,1,3,0:T(8,128)}) fusion(pred[256]{0:T(512)(128)(4,1)S(1)} %iota_compare_fusion.2, bf16[128,4,8,128]{0,3,2,1:T(8,128)(2,1)S(1)} %bitcast.90, bf16[4,256,256]{2,1,0:T(8,128)(2,1)S(1)} %broadcast_select_fusion), kind=kOutput, calls=%fused_computation.10 | convolution fusion | flops 271577088 | bytes 5521920 | tf_op jit(solution)/shard_map/thgd,hjd->hgtj/dot_general | solution.py:197
  160.5 34.8 %all-gather.13.cloned.1.call-done = bf16[2048,256]{0,1:T(8,128)(2,1)} async-done(((bf16[512,256]{0,1:T(8,128)(2,1)}), bf16[2048,256]{0,1:T(8,128)(2,1)}) %all-gather.13.cloned.1.call-update) | async-done | bytes 1048592 | tf_op jit(solution)/shard_map/all_gather | solution.py:184
  195.3 1.8 reshape.306
  197.2 1.2 fusion.55
  198.3 0.4 copy.50
  198.7 0.0 copy-start
  198.8 1.3 fusion.2
  200.1 0.9 copy-done
  200.9 1.2 fusion.10
  202.1 1.2 fusion.12
  203.3 0.0 copy-start.1
  203.3 2.2 %fusion.3 = f32[4,8,128]{2,1,0:T(8,128)S(1)} fusion(f32[4,512,128,8]{2,1,3,0:T(8,128)S(1)} %get-tuple-element.18, f32[4,8,128]{2,1,0:T(8,128)S(1)} %max.16, pred[128,512]{0,1:T(8,128)(4,1)S(1)} %iota_compare_fusion), kind=kLoop, calls=%fused_computation.7 | loop fusion | flops 10481664 | bytes 8486912 | tf_op jit(solution)/shard_map/reduce_sum | solution.py:213
  205.5 0.0 copy-done.1
  205.5 2.5 %fusion.14 = bf16[128,4,8,128]{0,3,2,1:T(8,128)(2,1)S(1)} fusion(f32[4,8,128,128]{2,3,1,0:T(8,128)S(1)} %fusion.12, f32[4,512,128,8]{2,1,3,0:T(8,128)S(1)} %get-tuple-element.18, f32[4,8,128]{2,1,0:T(8,128)S(1)} %max.16, pred[128,512]{0,1:T(8,128)(4,1)S(1)} %iota_compare_fusion, f32[128,4,8]{0,2,1:T(8,128)S(1)} %add_bitcast_fusion, ...), kind=kOutput, calls=%fused_computation.20 | convolution fusion | flops 548929536 | bytes 12156928 | tf_op jit(solution)/shard_map/hgtu,hud->hgtd/dot_general | solution.py:219
  208.0 1.3 copy.38
  (14 shorter events, 0.2 us)
Async XLA Ops:
  6.5 81.7 %all-gather.9.cloned.1.call-start = ((), (), s32[]{:S(2)}) async-start(), calls=%async_computation | async-start | bytes 2555904 | tf_op jit(solution)/shard_map/all_gather | solution.py:118
  21.8 124.7 %all-gather.11.cloned.1.call-start = ((), (), s32[]{:S(2)}) async-start(), calls=%async_computation.1 | async-start | bytes 7077888 | tf_op jit(solution)/shard_map/all_gather | solution.py:118
  88.2 107.1 %all-gather.13.cloned.1.call-start = ((), (), s32[]{:S(2)}) async-start(), calls=%async_computation.2 | async-start | bytes 1310720 | tf_op jit(solution)/shard_map/all_gather | solution.py:184
  89.2 66.8 %collective-permute-start = (bf16[256,256]{1,0:T(8,128)(2,1)S(1)}, bf16[256,256]{1,0:T(8,128)(2,1)}, u32[]{:S(2)}, u32[]{:S(2)}) collective-permute-start(bf16[256,256]{1,0:T(8,128)(2,1)S(1)} %get-tuple-element.12), channel_id=1, source_target_pairs={{0,1},{1,2},{2,3},{3,0},{4,5},{5,6},{6,7},{7,4},{8,9},{9,10},{10,1... | collective-permute-start | bytes 393224 | tf_op jit(solution)/shard_map/ppermute | solution.py:146
  93.2 62.8 %collective-permute-start.1 = (bf16[256,256]{1,0:T(8,128)(2,1)S(1)}, bf16[256,256]{1,0:T(8,128)(2,1)}, u32[]{:S(2)}, u32[]{:S(2)}) collective-permute-start(bf16[256,256]{1,0:T(8,128)(2,1)S(1)} %get-tuple-element.12), channel_id=1, source_target_pairs={{0,2},{1,3},{2,0},{3,1},{4,6},{5,7},{6,4},{7,5},{8,10},{9,11},{10,... | collective-permute-start | bytes 393224 | tf_op jit(solution)/shard_map/ppermute | solution.py:146
  98.5 57.5 %collective-permute-start.2 = (bf16[256,256]{1,0:T(8,128)(2,1)S(1)}, bf16[256,256]{1,0:T(8,128)(2,1)}, u32[]{:S(2)}, u32[]{:S(2)}) collective-permute-start(bf16[256,256]{1,0:T(8,128)(2,1)S(1)} %get-tuple-element.12), channel_id=1, source_target_pairs={{0,3},{1,0},{2,1},{3,2},{4,7},{5,4},{6,5},{7,6},{8,11},{9,8},{10,9... | collective-permute-start | bytes 393224 | tf_op jit(solution)/shard_map/ppermute | solution.py:146
  198.7 2.2 %copy-start = (f32[4,256,128,8]{2,1,3,0:T(8,128)S(1)}, f32[4,256,128,8]{2,1,3,0:T(8,128)}, u32[]{:S(2)}) copy-start(f32[4,256,128,8]{2,1,3,0:T(8,128)} %get-tuple-element.16) | copy-start | bytes 12582916
  203.3 2.2 %copy-start.1 = (bf16[4,512,128]{1,0,2:T(4,128)(2,1)S(1)}, bf16[4,512,128]{1,0,2:T(4,128)(2,1)}, u32[]{:S(2)}) copy-start(bf16[4,512,128]{1,0,2:T(4,128)(2,1)} %get-tuple-element.7) | copy-start | bytes 1572868
Sparse Core Ops, SparseCore 0:
  21.9 66.2 all-gather.8
  90.6 31.2 all-gather.10
  155.5 39.8 all-gather.12

commit v6 on v4

--- a/solution.py
+++ b/solution.py
@@ -107,9 +107,9 @@
     return result.transpose(2, 0, 1, 3).reshape(query_rows, kv_heads * group_size * head_size)
 
 
-FSDP_PARTS = (("ylo", 2), ("x", 4), ("z", 12), ("core", 2))
+FSDP_PARTS = (("ylo", 2), ("x", 4), ("zhi", 3), ("zlo", 4), ("core", 2))
 FSDP_AXES = tuple(name for name, _ in FSDP_PARTS)
-GATHER_STAGES = (("ylo",), ("x",), ("z",), ("core",))
+GATHER_STAGES = (("ylo",), ("x",), ("zlo",), ("zhi",), ("core",))
 
 
 def gather_weights(shard):

time: 197 us -> 236 us (1.20)
  waiting for transfers between devices: 96.9 us -> 122 us
  blocking collectives: 12.9 us -> 29.2 us
  local copies, waits for them, and re-layouts: 24.5 us -> 21.4 us
    all_gather x2, waiting for transfers between devices: 74.1 us -> 97 us  [gather_weights(): gathered = lax.all_gather(gathered, stage, axis=0, tiled=False)]
    all_gather x2 -> x3, blocking collectives: 12.9 us -> 29.2 us  [gather_weights(): gathered = lax.all_gather(gathered, stage, axis=0, tiled=False)]
    all_gather x3, local copies, waits for them, and re-layouts: 10 us -> 6.89 us  [gather_weights(): gathered = lax.all_gather(gathered, stage, axis=0, tiled=False)]
where the time goes in v6:
time: 236 us; the launch traced here: 235 us
  waiting for transfers between devices  122 us (52%)
  blocking collectives  29.2 us (12%)
  starting transfers between devices  25.3 us (11%)
  local copies, waits for them, and re-layouts  21.4 us (9%)
  between operations  15.1 us (6%)
  matrix products  14.8 us (6%)
  other arithmetic  7.29 us (3%)
    all_gather x2, waiting for transfers between devices, gather_weights(): gathered = lax.all_gather(gathered, stage, axis=0, tiled=False)  97 us
    all_gather x3, blocking collectives, gather_weights(): gathered = lax.all_gather(gathered, stage, axis=0, tiled=False)  29.2 us
    ppermute x6, starting transfers between devices, gather_sp(): pieces.append(lax.ppermute(block, 'sp', perm=pairs))  25.3 us
    ppermute x6, waiting for transfers between devices, gather_sp(): pieces.append(lax.ppermute(block, 'sp', perm=pairs))  24.9 us
    reshape x1, local copies, waits for them, and re-layouts, gather_weights(): return gathered.reshape(-1, shard.shape[1])  7.27 us
    dot_general x1, matrix products, per_device(): jnp.dot(hidden_rows, whole_kv[:model_width], preferred_element_type=jnp.f...  7.04 us
    all_gather x3, local copies, waits for them, and re-layouts, gather_weights(): gathered = lax.all_gather(gathered, stage, axis=0, tiled=False)  6.89 us
  transfers between devices with their start and end apart: 8, of which 6 were waited for; matrix products, arithmetic and copies ran while one was open for 3% of the time, Pallas kernels for 0%

profile of v6, /device:TPU:9, one launch (start us, length us, event | category | flops | bytes accessed | tf_op | source)
XLA Modules:
  0.0 235.0 jit_solution(10901017942317448998)
XLA Ops:
  6.5 0.8 maximum_bitcast_fusion
  7.4 3.3 %all-gather.5 = bf16[2,43,256]{2,1,0:T(8,128)(2,1)S(1)} all-gather(bf16[1,43,256]{2,1,0:T(8,128)(2,1)S(1)} %maximum_bitcast_fusion), channel_id=2, replica_groups=mesh['ylo'=2,'x'=4,'zhi'=3,'zlo'=4,'core'=2,'sp'=4] {'ylo'}, dimensions={0}, use_global_device_ids=true | all-gather | bytes 66048 | tf_op jit(solution)/shard_map/all_gather | solution.py:118
  10.7 9.6 %all-gather.1 = bf16[8,43,256]{2,1,0:T(8,128)(2,1)S(1)} all-gather(bf16[2,43,256]{2,1,0:T(8,128)(2,1)S(1)} %all-gather.5), channel_id=3, replica_groups=mesh['ylo'=2,'x'=4,'zhi'=3,'zlo'=4,'core'=2,'sp'=4] {'x'}, dimensions={0}, use_global_device_ids=true | all-gather | bytes 220160 | tf_op jit(solution)/shard_map/all_gather | solution.py:118
  20.3 0.1 copy.36
  20.4 16.3 %all-gather.2 = bf16[16,2,43,256]{3,1,2,0:T(2,128)(2,1)S(1)} all-gather(bf16[4,2,43,256]{3,1,2,0:T(2,128)(2,1)S(1)} %copy.36), channel_id=4, replica_groups=mesh['ylo'=2,'x'=4,'zhi'=3,'zlo'=4,'core'=2,'sp'=4] {'zlo'}, dimensions={0}, use_global_device_ids=true | all-gather | bytes 880640 | tf_op jit(solution)/shard_map/all_gather | solution.py:118
  36.7 1.1 copy.37
  37.9 0.0 all-gather.9.cloned.1.call-update
  37.9 0.0 all-gather.11.cloned.1.call-start
  37.9 97.0 %all-gather.9.cloned.1.call-done = bf16[12,4,2,43,256]{4,1,3,2,0:T(4,128)(2,1)} async-done(((bf16[4,4,2,43,256]{4,1,3,2,0:T(4,128)(2,1)}), bf16[12,4,2,43,256]{4,1,3,2,0:T(4,128)(2,1)}) %all-gather.9.cloned.1.call-update) | async-done | bytes 2113552 | tf_op jit(solution)/shard_map/all_gather | solution.py:118
  134.9 0.0 all-gather.11.cloned.1.call-update
  135.0 4.4 %collective-permute-start.2 = (bf16[256,256]{1,0:T(8,128)(2,1)S(1)}, bf16[256,256]{1,0:T(8,128)(2,1)}, u32[]{:S(2)}, u32[]{:S(2)}) collective-permute-start(bf16[256,256]{1,0:T(8,128)(2,1)S(1)} %get-tuple-element.12), channel_id=1, source_target_pairs={{0,3},{1,0},{2,1},{3,2},{4,7},{5,4},{6,5},{7,6},{8,11},{9,8},{10,9... | collective-permute-start | bytes 393224 | tf_op jit(solution)/shard_map/ppermute | solution.py:137
  139.5 4.8 %collective-permute-start.1 = (bf16[256,256]{1,0:T(8,128)(2,1)S(1)}, bf16[256,256]{1,0:T(8,128)(2,1)}, u32[]{:S(2)}, u32[]{:S(2)}) collective-permute-start(bf16[256,256]{1,0:T(8,128)(2,1)S(1)} %get-tuple-element.12), channel_id=1, source_target_pairs={{0,2},{1,3},{2,0},{3,1},{4,6},{5,7},{6,4},{7,5},{8,10},{9,11},{10,... | collective-permute-start | bytes 393224 | tf_op jit(solution)/shard_map/ppermute | solution.py:137
  144.3 3.1 %collective-permute-start = (bf16[256,256]{1,0:T(8,128)(2,1)S(1)}, bf16[256,256]{1,0:T(8,128)(2,1)}, u32[]{:S(2)}, u32[]{:S(2)}) collective-permute-start(bf16[256,256]{1,0:T(8,128)(2,1)S(1)} %get-tuple-element.12), channel_id=1, source_target_pairs={{0,1},{1,2},{2,3},{3,0},{4,5},{5,6},{6,7},{7,4},{8,9},{9,10},{10,1... | collective-permute-start | bytes 393224 | tf_op jit(solution)/shard_map/ppermute | solution.py:137
  148.1 0.7 copy.34
  148.7 0.2 convert.21
  149.8 0.2 fusion.38
  150.0 0.3 subtract_convert_fusion
  150.4 0.1 pad_maximum_fusion
  150.5 5.3 %collective-permute-done.1 = bf16[256,256]{1,0:T(8,128)(2,1)} collective-permute-done((bf16[256,256]{1,0:T(8,128)(2,1)S(1)}, bf16[256,256]{1,0:T(8,128)(2,1)}, u32[]{:S(2)}, u32[]{:S(2)}) %collective-permute-start.1) | collective-permute-done | bytes 131104 | tf_op jit(solution)/shard_map/ppermute | solution.py:137
  155.7 1.7 collective-permute-done
  157.4 1.1 pad_maximum_fusion.2
  158.5 0.6 gather_fusion
  159.1 0.1 broadcast_select_fusion.1
  159.2 0.0 copy-start.1
  159.2 0.0 all-gather.11.cloned.1.call-done
  159.2 5.6 %copy.38 = bf16[6,4,4,2,43,256]{5,3,4,2,1,0:T(2,128)(2,1)S(1)} copy(bf16[6,4,4,2,43,256]{5,2,4,3,1,0:T(4,128)(2,1)} %all-gather.11.cloned.1.call-done) | data formatting | bytes 8454144 | tf_op jit(solution)/shard_map/all_gather | solution.py:118
  164.9 3.1 %copy.39 = bf16[2,4,3,4,2,43,256]{6,5,4,3,2,1,0:T(8,128)(2,1)} copy(bf16[2,4,3,4,2,43,256]{6,0,5,1,3,2,4:T(2,128)(2,1)S(1)} %bitcast.90) | data formatting | bytes 8454144 | tf_op jit(solution)/shard_map/transpose | solution.py:127
  168.0 7.3 %reshape.287 = bf16[8256,256]{1,0:T(8,128)(2,1)} reshape(bf16[2,4,3,4,2,43,256]{6,5,4,3,2,1,0:T(8,128)(2,1)} %copy.39) | data formatting | bytes 8454144 | tf_op jit(solution)/shard_map/reshape | solution.py:128
  175.3 7.0 %fusion.23 = f32[512,256]{0,1:T(8,128)S(1)} fusion(bf16[512,8192]{1,0:T(8,128)(2,1)} %param.8, bf16[8256,256]{1,0:T(8,128)(2,1)} %reshape.287), kind=kOutput, calls=%fused_computation.27 | convolution fusion | flops 2147483648 | bytes 13107200 | tf_op jit(solution)/shard_map/dot_general | solution.py:168
  182.4 0.6 fusion.32
  183.0 4.9 %collective-permute-start.5 = (bf16[512,256]{0,1:T(8,128)(2,1)S(1)}, bf16[512,256]{0,1:T(8,128)(2,1)S(1)}, u32[]{:S(2)}, u32[]{:S(2)}) collective-permute-start(bf16[512,256]{0,1:T(8,128)(2,1)S(1)} %get-tuple-element.10), channel_id=1, source_target_pairs={{0,3},{1,0},{2,1},{3,2},{4,7},{5,4},{6,5},{7,6},{8,11},{9,8},{10,9... | collective-permute-start | bytes 786440 | tf_op jit(solution)/shard_map/ppermute | solution.py:137
  187.9 3.8 %collective-permute-start.4 = (bf16[512,256]{0,1:T(8,128)(2,1)S(1)}, bf16[512,256]{0,1:T(8,128)(2,1)S(1)}, u32[]{:S(2)}, u32[]{:S(2)}) collective-permute-start(bf16[512,256]{0,1:T(8,128)(2,1)S(1)} %get-tuple-element.10), channel_id=1, source_target_pairs={{0,2},{1,3},{2,0},{3,1},{4,6},{5,7},{6,4},{7,5},{8,10},{9,11},{10,... | collective-permute-start | bytes 786440 | tf_op jit(solution)/shard_map/ppermute | solution.py:137
  191.7 4.2 %collective-permute-start.3 = (bf16[512,256]{0,1:T(8,128)(2,1)S(1)}, bf16[512,256]{0,1:T(8,128)(2,1)S(1)}, u32[]{:S(2)}, u32[]{:S(2)}) collective-permute-start(bf16[512,256]{0,1:T(8,128)(2,1)S(1)} %get-tuple-element.10), channel_id=1, source_target_pairs={{0,1},{1,2},{2,3},{3,0},{4,5},{5,6},{6,7},{7,4},{8,9},{9,10},{10,1... | collective-permute-start | bytes 786440 | tf_op jit(solution)/shard_map/ppermute | solution.py:137
  195.9 2.7 %bitcast_reduce_fusion = (f32[4,8,128]{2,1,0:T(8,128)S(1)}, f32[4,256,128,8]{2,1,3,0:T(8,128)}) fusion(pred[256]{0:T(512)(128)(4,1)S(1)} %iota_compare_fusion.1, bf16[128,4,8,128]{0,3,2,1:T(8,128)(2,1)S(1)} %bitcast.91, bf16[4,256,256]{2,1,0:T(8,128)(2,1)S(1)} %broadcast_select_fusion.1), kind=kOutput, calls=%fused_computation.10 | convolution fusion | flops 271577088 | bytes 5521920 | tf_op jit(solution)/shard_map/thgd,hjd->hgtj/dot_general | solution.py:182
  198.6 0.1 collective-permute-done.5
  198.8 13.8 %collective-permute-done.4 = bf16[512,256]{0,1:T(8,128)(2,1)S(1)} collective-permute-done((bf16[512,256]{0,1:T(8,128)(2,1)S(1)}, bf16[512,256]{0,1:T(8,128)(2,1)S(1)}, u32[]{:S(2)}, u32[]{:S(2)}) %collective-permute-start.4) | collective-permute-done | bytes 262176 | tf_op jit(solution)/shard_map/ppermute | solution.py:137
  212.5 4.1 %collective-permute-done.3 = bf16[512,256]{0,1:T(8,128)(2,1)S(1)} collective-permute-done((bf16[512,256]{0,1:T(8,128)(2,1)S(1)}, bf16[512,256]{0,1:T(8,128)(2,1)S(1)}, u32[]{:S(2)}, u32[]{:S(2)}) %collective-permute-start.3) | collective-permute-done | bytes 262176 | tf_op jit(solution)/shard_map/ppermute | solution.py:137
  216.6 0.1 pad_maximum_fusion.1
  216.8 0.6 gather_fusion.1
  217.4 0.2 broadcast_select_fusion
  217.6 1.4 fusion
  219.0 0.7 copy-done
  219.7 0.1 copy-done.2
  219.9 1.2 fusion.12
  221.0 1.2 fusion.10
  222.2 2.2 fusion.1
  224.4 2.5 %fusion.14 = bf16[128,4,8,128]{0,3,2,1:T(8,128)(2,1)S(1)} fusion(f32[4,8,128,128]{2,3,1,0:T(8,128)S(1)} %fusion.12, f32[4,512,128,8]{2,1,3,0:T(8,128)S(1)} %get-tuple-element.18, f32[4,8,128]{2,1,0:T(8,128)S(1)} %max.16, pred[128,512]{0,1:T(8,128)(4,1)S(1)} %iota_compare_fusion, f32[128,4,8]{0,2,1:T(8,128)S(1)} %add_bitcast_fusion, ...), kind=kOutput, calls=%fused_computation.20 | convolution fusion | flops 548929536 | bytes 12156928 | tf_op jit(solution)/shard_map/hgtu,hud->hgtd/dot_general | solution.py:204
  226.9 1.3 copy.45
  (27 shorter events, 0.3 us)
Async XLA Ops:
  6.5 128.4 %copy-start.4 = (bf16[1,256,128]{2,1,0:T(8,128)(2,1)S(1)}, bf16[1,256,128]{2,1,0:T(8,128)(2,1)}, u32[]{:S(2)}) copy-start(bf16[1,256,128]{2,1,0:T(8,128)(2,1)} %param.13) | copy-start | bytes 196612
  6.5 128.4 %copy-start.5 = (bf16[1,256,128]{2,1,0:T(8,128)(2,1)S(1)}, bf16[1,256,128]{2,1,0:T(8,128)(2,1)}, u32[]{:S(2)}) copy-start(bf16[1,256,128]{2,1,0:T(8,128)(2,1)} %param.12) | copy-start | bytes 196612
  6.5 141.5 %copy-start.3 = (bf16[128,4096]{1,0:T(8,128)(2,1)S(1)}, bf16[128,4096]{1,0:T(8,128)(2,1)}, u32[]{:S(2)}) copy-start(bf16[128,4096]{1,0:T(8,128)(2,1)} %param.9) | copy-start | bytes 3145732
  6.5 128.4 %all-gather.9.cloned.1.call-start = ((), (), s32[]{:S(2)}) async-start(), calls=%async_computation | async-start | bytes 2818048 | tf_op jit(solution)/shard_map/all_gather | solution.py:118
  37.9 121.3 %all-gather.11.cloned.1.call-start = ((), (), s32[]{:S(2)}) async-start(), calls=%async_computation.1 | async-start | bytes 6340608 | tf_op jit(solution)/shard_map/all_gather | solution.py:118
  135.0 15.5 %collective-permute-start.2 = (bf16[256,256]{1,0:T(8,128)(2,1)S(1)}, bf16[256,256]{1,0:T(8,128)(2,1)}, u32[]{:S(2)}, u32[]{:S(2)}) collective-permute-start(bf16[256,256]{1,0:T(8,128)(2,1)S(1)} %get-tuple-element.12), channel_id=1, source_target_pairs={{0,3},{1,0},{2,1},{3,2},{4,7},{5,4},{6,5},{7,6},{8,11},{9,8},{10,9... | collective-permute-start | bytes 393224 | tf_op jit(solution)/shard_map/ppermute | solution.py:137
  139.5 16.3 %collective-permute-start.1 = (bf16[256,256]{1,0:T(8,128)(2,1)S(1)}, bf16[256,256]{1,0:T(8,128)(2,1)}, u32[]{:S(2)}, u32[]{:S(2)}) collective-permute-start(bf16[256,256]{1,0:T(8,128)(2,1)S(1)} %get-tuple-element.12), channel_id=1, source_target_pairs={{0,2},{1,3},{2,0},{3,1},{4,6},{5,7},{6,4},{7,5},{8,10},{9,11},{10,... | collective-permute-start | bytes 393224 | tf_op jit(solution)/shard_map/ppermute | solution.py:137
  144.3 13.1 %collective-permute-start = (bf16[256,256]{1,0:T(8,128)(2,1)S(1)}, bf16[256,256]{1,0:T(8,128)(2,1)}, u32[]{:S(2)}, u32[]{:S(2)}) collective-permute-start(bf16[256,256]{1,0:T(8,128)(2,1)S(1)} %get-tuple-element.12), channel_id=1, source_target_pairs={{0,1},{1,2},{2,3},{3,0},{4,5},{5,6},{6,7},{7,4},{8,9},{9,10},{10,1... | collective-permute-start | bytes 393224 | tf_op jit(solution)/shard_map/ppermute | solution.py:137
  159.2 36.7 %copy-start.1 = (bf16[4,256,256]{2,1,0:T(8,128)(2,1)}, bf16[4,256,256]{2,1,0:T(8,128)(2,1)S(1)}, u32[]{:S(2)}) copy-start(bf16[4,256,256]{2,1,0:T(8,128)(2,1)S(1)} %broadcast_select_fusion.1) | copy-start | bytes 1572868
  183.0 15.8 %collective-permute-start.5 = (bf16[512,256]{0,1:T(8,128)(2,1)S(1)}, bf16[512,256]{0,1:T(8,128)(2,1)S(1)}, u32[]{:S(2)}, u32[]{:S(2)}) collective-permute-start(bf16[512,256]{0,1:T(8,128)(2,1)S(1)} %get-tuple-element.10), channel_id=1, source_target_pairs={{0,3},{1,0},{2,1},{3,2},{4,7},{5,4},{6,5},{7,6},{8,11},{9,8},{10,9... | collective-permute-start | bytes 786440 | tf_op jit(solution)/shard_map/ppermute | solution.py:137
  187.9 24.6 %collective-permute-start.4 = (bf16[512,256]{0,1:T(8,128)(2,1)S(1)}, bf16[512,256]{0,1:T(8,128)(2,1)S(1)}, u32[]{:S(2)}, u32[]{:S(2)}) collective-permute-start(bf16[512,256]{0,1:T(8,128)(2,1)S(1)} %get-tuple-element.10), channel_id=1, source_target_pairs={{0,2},{1,3},{2,0},{3,1},{4,6},{5,7},{6,4},{7,5},{8,10},{9,11},{10,... | collective-permute-start | bytes 786440 | tf_op jit(solution)/shard_map/ppermute | solution.py:137
  191.7 24.9 %collective-permute-start.3 = (bf16[512,256]{0,1:T(8,128)(2,1)S(1)}, bf16[512,256]{0,1:T(8,128)(2,1)S(1)}, u32[]{:S(2)}, u32[]{:S(2)}) collective-permute-start(bf16[512,256]{0,1:T(8,128)(2,1)S(1)} %get-tuple-element.10), channel_id=1, source_target_pairs={{0,1},{1,2},{2,3},{3,0},{4,5},{5,6},{6,7},{7,4},{8,9},{9,10},{10,1... | collective-permute-start | bytes 786440 | tf_op jit(solution)/shard_map/ppermute | solution.py:137
  217.6 2.2 copy-start
  217.6 2.3 copy-start.2
Sparse Core Ops, SparseCore 0:
  38.0 96.8 all-gather.8
  137.3 20.8 all-gather.10

commit v7 on v4

--- a/solution.py
+++ b/solution.py
@@ -109,17 +109,18 @@
 
 FSDP_PARTS = (("ylo", 2), ("x", 4), ("z", 12), ("core", 2))
 FSDP_AXES = tuple(name for name, _ in FSDP_PARTS)
-GATHER_STAGES = (("ylo",), ("x",), ("z",), ("core",))
+GATHER_STAGES = (("ylo",), ("x",), ("z",))
 
 
 def gather_weights(shard):
     gathered = shard
     for stage in GATHER_STAGES:
         gathered = lax.all_gather(gathered, stage, axis=0, tiled=False)
-        if len(stage) > 1:
-            sizes = tuple(dict(FSDP_PARTS)[name] for name in stage)
-            gathered = gathered.reshape(sizes + gathered.shape[1:])
-    layout = []
+    other = lax.ppermute(gathered, "core", perm=[(0, 1), (1, 0)])
+    here = lax.axis_index("core")
+    order = (jnp.arange(2, dtype=jnp.int32) + here) % 2
+    gathered = jnp.take(jnp.stack([gathered, other]), order, axis=0)
+    layout = ["core"]
     for stage in reversed(GATHER_STAGES):
         layout.extend(stage)
     perm = [layout.index(name) for name in FSDP_AXES]
@@ -162,13 +163,17 @@
     live_count = prefix_len[0]
 
     cache_kv = jnp.concatenate([cache_keys[0], cache_values[0]], axis=1)
-    cache_all = gather_sp(cache_kv)
 
     whole_kv = gather_weights(jnp.concatenate([key_weight, value_weight], axis=1))
     kv_sum = jnp.dot(hidden_rows, whole_kv[:model_width], preferred_element_type=jnp.float32)
     new_keys = rotate(kv_sum[:, :kv_cols], cosine_table, sine_table, kv_local).astype(jnp.bfloat16)
     new_values = kv_sum[:, kv_cols:].astype(jnp.bfloat16)
-    new_all = gather_sp(jnp.concatenate([new_keys, new_values], axis=1))
+    local_kv = jnp.concatenate(
+        [cache_kv, jnp.concatenate([new_keys, new_values], axis=1)], axis=0
+    )
+    every_kv = gather_sp(local_kv)
+    cache_all = every_kv[:, :slot_total]
+    new_all = every_kv[:, slot_total:]
 
     rotated_q = rotate(queries.astype(jnp.float32), query_cosine, query_sine, HQ).astype(
         jnp.bfloat16

time: 197 us -> 209 us (1.061)
  the two profiles are of different devices: /device:TPU:9 before, /device:TPU:1 now
where the time goes in v7:
time: 209 us; the launch traced here: 208 us
  waiting for transfers between devices  93.5 us (45%)
  local copies, waits for them, and re-layouts  29.5 us (14%)
  starting transfers between devices  23.9 us (11%)
  other arithmetic  19.7 us (9%)
  between operations  15 us (7%)
  blocking collectives  13.7 us (7%)
  matrix products  13 us (6%)
    all_gather x1, waiting for transfers between devices, gather_weights(): gathered = lax.all_gather(gathered, stage, axis=0, tiled=False)  65.7 us
    ppermute x3, waiting for transfers between devices, gather_sp(): pieces.append(lax.ppermute(block, 'sp', perm=pairs))  27.7 us
    ppermute x3, starting transfers between devices, gather_sp(): pieces.append(lax.ppermute(block, 'sp', perm=pairs))  14.5 us
    all_gather x2, blocking collectives, gather_weights(): gathered = lax.all_gather(gathered, stage, axis=0, tiled=False)  13.7 us
    ppermute x1, starting transfers between devices, gather_weights(): other = lax.ppermute(gathered, 'core', perm=[(0, 1), (1, 0)])  9.42 us
    gather x2, local copies, waits for them, and re-layouts, gather_weights(): gathered = jnp.take(jnp.stack([gathered, other]), order, axis=0)  8.75 us
    reshape x1, local copies, waits for them, and re-layouts, gather_weights(): return gathered.reshape(-1, shard.shape[1])  7.27 us
    dot_general x1, matrix products, per_device(): jnp.dot(hidden_rows, whole_kv[:model_width], preferred_element_type=jnp.f...  7.04 us
  transfers between devices with their start and end apart: 5, of which 4 were waited for; matrix products, arithmetic and copies ran while one was open for 3% of the time, Pallas kernels for 0%

profile of v7, /device:TPU:1, one launch (start us, length us, event | category | flops | bytes accessed | tf_op | source)
XLA Modules:
  0.0 208.3 jit_solution(18266820571067294837)
XLA Ops:
  6.5 0.0 copy-start.1
  6.5 0.0 all-gather.6.cloned.1.call-start
  6.5 0.8 maximum_bitcast_fusion
  7.3 4.0 %all-gather.3 = bf16[2,43,256]{2,1,0:T(8,128)(2,1)S(1)} all-gather(bf16[1,43,256]{2,1,0:T(8,128)(2,1)S(1)} %maximum_bitcast_fusion), channel_id=2, replica_groups=mesh['ylo'=2,'x'=4,'z'=12,'core'=2,'sp'=4] {'ylo'}, dimensions={0}, use_global_device_ids=true | all-gather | bytes 66048 | tf_op jit(solution)/shard_map/all_gather | solution.py:118
  11.3 9.8 %all-gather.1 = bf16[8,43,256]{2,1,0:T(8,128)(2,1)S(1)} all-gather(bf16[2,43,256]{2,1,0:T(8,128)(2,1)S(1)} %all-gather.3), channel_id=3, replica_groups=mesh['ylo'=2,'x'=4,'z'=12,'core'=2,'sp'=4] {'x'}, dimensions={0}, use_global_device_ids=true | all-gather | bytes 220160 | tf_op jit(solution)/shard_map/all_gather | solution.py:118
  21.1 0.8 copy.55
  21.9 0.0 all-gather.6.cloned.1.call-update
  21.9 65.7 %all-gather.6.cloned.1.call-done = bf16[48,2,43,256]{3,1,2,0:T(2,128)(2,1)} async-done(((bf16[4,2,43,256]{3,1,2,0:T(2,128)(2,1)}), bf16[48,2,43,256]{3,1,2,0:T(2,128)(2,1)}) %all-gather.6.cloned.1.call-update) | async-done | bytes 2113552 | tf_op jit(solution)/shard_map/all_gather | solution.py:118
  87.6 3.7 %copy.56 = bf16[12,4,2,43,256]{4,1,3,2,0:T(4,128)(2,1)} copy(bf16[12,4,2,43,256]{4,2,3,1,0:T(2,128)(2,1)} %bitcast.89) | data formatting | bytes 4227072 | tf_op jit(solution)/shard_map/all_gather | solution.py:118
  91.4 9.4 %collective-permute-start = (bf16[12,4,2,43,256]{4,1,3,2,0:T(4,128)(2,1)}, bf16[12,4,2,43,256]{4,1,3,2,0:T(4,128)(2,1)}, u32[]{:S(2)}, u32[]{:S(2)}) collective-permute-start(bf16[12,4,2,43,256]{4,1,3,2,0:T(4,128)(2,1)} %copy.56), channel_id=1, source_target_pairs={{0,4},{4,0},{1,5},{5,1},{2,6},{6,2},{3,7},{7,3},{8,12},{12,8},{9,1... | collective-permute-start | bytes 6340616 | tf_op jit(solution)/shard_map/ppermute | solution.py:119
  102.1 0.0 copy-done.1
  102.1 0.1 copy.53
  102.2 0.0 copy-done.2
  102.2 0.1 copy.54
  102.3 0.0 copy-start
  102.3 1.8 copy.59
  104.1 1.6 convert.21
  105.9 0.2 fusion.40
  106.1 1.9 subtract_convert_fusion
  107.9 0.0 copy-done
  108.0 0.8 copy.57
  108.8 0.0 collective-permute-done
  108.8 4.0 %fusion.13 = (bf16[2,12,4,2,43,128]{5,2,4,3,1,0:T(4,128)(2,1)}, bf16[2,12,4,2,43,128]{5,2,4,3,1,0:T(4,128)(2,1)S(1)}) fusion(bf16[1,12,4,2,43,256]{5,2,4,3,1,0:T(4,128)(2,1)S(1)} %copy.57, bf16[1,12,4,2,43,256]{5,2,4,3,1,0:T(4,128)(2,1)} %bitcast.7), kind=kLoop, calls=%fused_computation.23 | loop fusion | flops 8454144 | bytes 8454144 | tf_op jit(solution)/shard_map/stack | solution.py:122
  112.8 5.2 %gather_fusion.1 = bf16[2,12,4,2,43,128]{5,2,4,3,1,0:T(4,128)(2,1)} fusion(bf16[2,12,4,2,43,128]{5,2,4,3,1,0:T(4,128)(2,1)} %get-tuple-element.5, s32[1024]{0:T(1024)S(1)} %pad_clamp_fusion.1), kind=kCustom, calls=%fused_computation.1 | custom fusion | bytes 4227080 | tf_op jit(solution)/shard_map/jit(_take)/gather | solution.py:122
  118.0 3.6 %gather_fusion.2 = bf16[2,12,4,2,43,128]{5,2,4,3,1,0:T(4,128)(2,1)} fusion(bf16[2,12,4,2,43,128]{5,2,4,3,1,0:T(4,128)(2,1)S(1)} %get-tuple-element.6, s32[1024]{0:T(1024)S(1)} %pad_clamp_fusion.1), kind=kCustom, calls=%fused_computation.2 | custom fusion | bytes 4227080 | tf_op jit(solution)/shard_map/jit(_take)/gather | solution.py:122
  121.6 5.1 %fusion.3 = bf16[2,4,12,2,43,256]{5,1,4,0,2,3:T(4,128)(2,1)S(1)} fusion(bf16[2,12,4,2,43,128]{5,2,4,3,1,0:T(4,128)(2,1)} %gather_fusion.2, bf16[2,12,4,2,43,128]{5,2,4,3,1,0:T(4,128)(2,1)} %gather_fusion.1, pred[2]{0:T(512)(128)(4,1)S(1)} %compare_and_fusion), kind=kLoop, calls=%fused_computation.11 | loop fusion | flops 10567680 | bytes 8454146 | tf_op jit(solution)/shard_map/jit(_take)/select_n | solution.py:122
  126.7 3.0 %copy.58 = bf16[2,4,12,2,43,256]{5,4,3,2,1,0:T(8,128)(2,1)} copy(bf16[2,4,12,2,43,256]{5,1,4,0,2,3:T(4,128)(2,1)S(1)} %fusion.3) | data formatting | bytes 8454144 | tf_op jit(solution)/shard_map/jit(_take)/select_n | solution.py:122
  129.7 7.3 %reshape.339 = bf16[8256,256]{1,0:T(8,128)(2,1)} reshape(bf16[2,4,12,2,43,256]{5,4,3,2,1,0:T(8,128)(2,1)} %copy.58) | data formatting | bytes 8454144 | tf_op jit(solution)/shard_map/reshape | solution.py:129
  137.0 7.0 %fusion.25 = f32[512,256]{0,1:T(8,128)S(1)} fusion(bf16[512,8192]{1,0:T(8,128)(2,1)} %param.8, bf16[8256,256]{1,0:T(8,128)(2,1)} %reshape.339), kind=kOutput, calls=%fused_computation.36 | convolution fusion | flops 2147483648 | bytes 13107200 | tf_op jit(solution)/shard_map/dot_general | solution.py:168
  144.1 0.6 fusion.34
  144.7 0.1 fusion.54
  144.7 7.1 %collective-permute-start.2 = (bf16[768,256]{0,1:T(8,128)(2,1)S(1)}, bf16[768,256]{0,1:T(8,128)(2,1)S(1)}, u32[]{:S(2)}, u32[]{:S(2)}) collective-permute-start(bf16[768,256]{0,1:T(8,128)(2,1)S(1)} %get-tuple-element.10), channel_id=1, source_target_pairs={{0,2},{1,3},{2,0},{3,1},{4,6},{5,7},{6,4},{7,5},{8,10},{9,11},{10,... | collective-permute-start | bytes 1179656 | tf_op jit(solution)/shard_map/ppermute | solution.py:138
  151.8 2.2 %collective-permute-start.1 = (bf16[768,256]{0,1:T(8,128)(2,1)S(1)}, bf16[768,256]{0,1:T(8,128)(2,1)S(1)}, u32[]{:S(2)}, u32[]{:S(2)}) collective-permute-start(bf16[768,256]{0,1:T(8,128)(2,1)S(1)} %get-tuple-element.10), channel_id=1, source_target_pairs={{0,1},{1,2},{2,3},{3,0},{4,5},{5,6},{6,7},{7,4},{8,9},{9,10},{10,1... | collective-permute-start | bytes 1179656 | tf_op jit(solution)/shard_map/ppermute | solution.py:138
  154.1 5.2 %collective-permute-start.3 = (bf16[768,256]{0,1:T(8,128)(2,1)S(1)}, bf16[768,256]{0,1:T(8,128)(2,1)S(1)}, u32[]{:S(2)}, u32[]{:S(2)}) collective-permute-start(bf16[768,256]{0,1:T(8,128)(2,1)S(1)} %get-tuple-element.10), channel_id=1, source_target_pairs={{0,3},{1,0},{2,1},{3,2},{4,7},{5,4},{6,5},{7,6},{8,11},{9,8},{10,9... | collective-permute-start | bytes 1179656 | tf_op jit(solution)/shard_map/ppermute | solution.py:138
  159.3 0.1 pad_maximum_fusion.2
  159.4 5.9 %collective-permute-done.2 = bf16[768,256]{0,1:T(8,128)(2,1)S(1)} collective-permute-done((bf16[768,256]{0,1:T(8,128)(2,1)S(1)}, bf16[768,256]{0,1:T(8,128)(2,1)S(1)}, u32[]{:S(2)}, u32[]{:S(2)}) %collective-permute-start.2) | collective-permute-done | bytes 393248 | tf_op jit(solution)/shard_map/ppermute | solution.py:138
  165.3 13.3 %collective-permute-done.1 = bf16[768,256]{0,1:T(8,128)(2,1)S(1)} collective-permute-done((bf16[768,256]{0,1:T(8,128)(2,1)S(1)}, bf16[768,256]{0,1:T(8,128)(2,1)S(1)}, u32[]{:S(2)}, u32[]{:S(2)}) %collective-permute-start.1) | collective-permute-done | bytes 393248 | tf_op jit(solution)/shard_map/ppermute | solution.py:138
  178.6 8.6 %collective-permute-done.3 = bf16[768,256]{0,1:T(8,128)(2,1)S(1)} collective-permute-done((bf16[768,256]{0,1:T(8,128)(2,1)S(1)}, bf16[768,256]{0,1:T(8,128)(2,1)S(1)}, u32[]{:S(2)}, u32[]{:S(2)}) %collective-permute-start.3) | collective-permute-done | bytes 393248 | tf_op jit(solution)/shard_map/ppermute | solution.py:138
  187.2 0.2 pad_maximum_fusion.1
  187.4 1.8 gather_fusion
  189.2 1.6 broadcast_select_fusion
  190.8 0.8 bitcast_reduce_fusion
  191.6 1.4 fusion
  193.1 1.2 fusion.11
  194.3 1.2 fusion.14
  195.5 2.2 %fusion.1 = f32[4,8,128]{2,1,0:T(8,128)S(1)} fusion(f32[4,512,128,8]{2,1,3,0:T(8,128)S(1)} %get-tuple-element.18, f32[4,8,128]{2,1,0:T(8,128)S(1)} %max.16, pred[128,512]{0,1:T(8,128)(4,1)S(1)} %iota_compare_fusion), kind=kLoop, calls=%fused_computation.6 | loop fusion | flops 10481664 | bytes 8486912 | tf_op jit(solution)/shard_map/reduce_sum | solution.py:203
  197.7 2.5 %fusion.16 = bf16[128,4,8,128]{0,3,2,1:T(8,128)(2,1)S(1)} fusion(f32[4,8,128,128]{2,3,1,0:T(8,128)S(1)} %fusion.14, f32[4,512,128,8]{2,1,3,0:T(8,128)S(1)} %get-tuple-element.18, f32[4,8,128]{2,1,0:T(8,128)S(1)} %max.16, pred[128,512]{0,1:T(8,128)(4,1)S(1)} %iota_compare_fusion, f32[128,4,8]{0,2,1:T(8,128)S(1)} %add_bitcast_fusion, ...), kind=kOutput, calls=%fused_computation.27 | convolution fusion | flops 548929536 | bytes 12156928 | tf_op jit(solution)/shard_map/hgtu,hud->hgtd/dot_general | solution.py:209
  200.2 1.3 copy.66
  (18 shorter events, 0.2 us)
Async XLA Ops:
  6.5 95.5 %copy-start.1 = (bf16[1,256,128]{2,1,0:T(8,128)(2,1)S(1)}, bf16[1,256,128]{2,1,0:T(8,128)(2,1)}, u32[]{:S(2)}) copy-start(bf16[1,256,128]{2,1,0:T(8,128)(2,1)} %param.12) | copy-start | bytes 196612
  6.5 95.7 %copy-start.2 = (bf16[1,256,128]{2,1,0:T(8,128)(2,1)S(1)}, bf16[1,256,128]{2,1,0:T(8,128)(2,1)}, u32[]{:S(2)}) copy-start(bf16[1,256,128]{2,1,0:T(8,128)(2,1)} %param.13) | copy-start | bytes 196612
  6.5 81.1 %all-gather.6.cloned.1.call-start = ((), (), s32[]{:S(2)}) async-start(), calls=%async_computation | async-start | bytes 2289664 | tf_op jit(solution)/shard_map/all_gather | solution.py:118
  91.4 17.4 %collective-permute-start = (bf16[12,4,2,43,256]{4,1,3,2,0:T(4,128)(2,1)}, bf16[12,4,2,43,256]{4,1,3,2,0:T(4,128)(2,1)}, u32[]{:S(2)}, u32[]{:S(2)}) collective-permute-start(bf16[12,4,2,43,256]{4,1,3,2,0:T(4,128)(2,1)} %copy.56), channel_id=1, source_target_pairs={{0,4},{4,0},{1,5},{5,1},{2,6},{6,2},{3,7},{7,3},{8,12},{12,8},{9,1... | collective-permute-start | bytes 6340616 | tf_op jit(solution)/shard_map/ppermute | solution.py:119
  102.3 5.6 %copy-start = (bf16[48,2,43,256]{3,1,2,0:T(2,128)(2,1)S(1)}, bf16[48,2,43,256]{3,1,2,0:T(2,128)(2,1)}, u32[]{:S(2)}) copy-start(bf16[48,2,43,256]{3,1,2,0:T(2,128)(2,1)} %all-gather.6.cloned.1.call-done) | copy-start | bytes 6340612
  144.7 20.6 %collective-permute-start.2 = (bf16[768,256]{0,1:T(8,128)(2,1)S(1)}, bf16[768,256]{0,1:T(8,128)(2,1)S(1)}, u32[]{:S(2)}, u32[]{:S(2)}) collective-permute-start(bf16[768,256]{0,1:T(8,128)(2,1)S(1)} %get-tuple-element.10), channel_id=1, source_target_pairs={{0,2},{1,3},{2,0},{3,1},{4,6},{5,7},{6,4},{7,5},{8,10},{9,11},{10,... | collective-permute-start | bytes 1179656 | tf_op jit(solution)/shard_map/ppermute | solution.py:138
  151.8 26.7 %collective-permute-start.1 = (bf16[768,256]{0,1:T(8,128)(2,1)S(1)}, bf16[768,256]{0,1:T(8,128)(2,1)S(1)}, u32[]{:S(2)}, u32[]{:S(2)}) collective-permute-start(bf16[768,256]{0,1:T(8,128)(2,1)S(1)} %get-tuple-element.10), channel_id=1, source_target_pairs={{0,1},{1,2},{2,3},{3,0},{4,5},{5,6},{6,7},{7,4},{8,9},{9,10},{10,1... | collective-permute-start | bytes 1179656 | tf_op jit(solution)/shard_map/ppermute | solution.py:138
  154.1 33.1 %collective-permute-start.3 = (bf16[768,256]{0,1:T(8,128)(2,1)S(1)}, bf16[768,256]{0,1:T(8,128)(2,1)S(1)}, u32[]{:S(2)}, u32[]{:S(2)}) collective-permute-start(bf16[768,256]{0,1:T(8,128)(2,1)S(1)} %get-tuple-element.10), channel_id=1, source_target_pairs={{0,3},{1,0},{2,1},{3,2},{4,7},{5,4},{6,5},{7,6},{8,11},{9,8},{10,9... | collective-permute-start | bytes 1179656 | tf_op jit(solution)/shard_map/ppermute | solution.py:138
Sparse Core Ops, SparseCore 0:
  22.0 65.5 all-gather.5

commit v8 on v4

--- a/solution.py
+++ b/solution.py
@@ -136,6 +136,24 @@
         pairs = [(source, (source + shift) % count) for source in range(count)]
         pieces.append(lax.ppermute(block, "sp", perm=pairs))
     stacked = jnp.stack(pieces)
+    order = (here - jnp.arange(count, dtype=jnp.int32)) % count
+    return jnp.take(stacked, order, axis=0)
+
+
+def gather_sp_relay(block):
+    count = lax.axis_size("sp")
+    if count != 4:
+        return gather_sp(block)
+    here = lax.axis_index("sp")
+    forward = [(source, (source + 1) % count) for source in range(count)]
+    backward = [(source, (source - 1) % count) for source in range(count)]
+    from_left = lax.ppermute(block, "sp", perm=forward)
+    from_right = lax.ppermute(block, "sp", perm=backward)
+    half = block.shape[1] // 2
+    far_first = lax.ppermute(from_left[:, :half], "sp", perm=forward)
+    far_second = lax.ppermute(from_right[:, half:], "sp", perm=backward)
+    far = jnp.concatenate([far_first, far_second], axis=1)
+    stacked = jnp.stack([block, from_left, far, from_right])
     order = (here - jnp.arange(count, dtype=jnp.int32)) % count
     return jnp.take(stacked, order, axis=0)
 
@@ -168,7 +186,7 @@
     kv_sum = jnp.dot(hidden_rows, whole_kv[:model_width], preferred_element_type=jnp.float32)
     new_keys = rotate(kv_sum[:, :kv_cols], cosine_table, sine_table, kv_local).astype(jnp.bfloat16)
     new_values = kv_sum[:, kv_cols:].astype(jnp.bfloat16)
-    new_all = gather_sp(jnp.concatenate([new_keys, new_values], axis=1))
+    new_all = gather_sp_relay(jnp.concatenate([new_keys, new_values], axis=1))
 
     rotated_q = rotate(queries.astype(jnp.float32), query_cosine, query_sine, HQ).astype(
         jnp.bfloat16

time: 197 us -> 198 us (level)
  the two profiles are of different devices: /device:TPU:9 before, /device:TPU:1 now
where the time goes in v8:
time: 198 us; the launch traced here: 195 us
  waiting for transfers between devices  90.7 us (46%)
  starting transfers between devices  26.8 us (14%)
  local copies, waits for them, and re-layouts  24.5 us (12%)
  between operations  15.1 us (8%)
  matrix products  14.9 us (8%)
  blocking collectives  13.7 us (7%)
  other arithmetic  9.04 us (5%)
    all_gather x2, waiting for transfers between devices, gather_weights(): gathered = lax.all_gather(gathered, stage, axis=0, tiled=False)  79.3 us
    all_gather x2, blocking collectives, gather_weights(): gathered = lax.all_gather(gathered, stage, axis=0, tiled=False)  13.7 us
    ppermute x3, starting transfers between devices, gather_sp(): pieces.append(lax.ppermute(block, 'sp', perm=pairs))  13.3 us
    all_gather x3, local copies, waits for them, and re-layouts, gather_weights(): gathered = lax.all_gather(gathered, stage, axis=0, tiled=False)  10 us
    ppermute x1, waiting for transfers between devices, gather_sp_relay(): from_right = lax.ppermute(block, 'sp', perm=backward)  7.85 us
    reshape x1, local copies, waits for them, and re-layouts, gather_weights(): return gathered.reshape(-1, shard.shape[1])  7.28 us
    dot_general x1, matrix products, per_device(): jnp.dot(hidden_rows, whole_kv[:model_width], preferred_element_type=jnp.f...  7.06 us
    ppermute x1, starting transfers between devices, gather_sp_relay(): far_second = lax.ppermute(from_right[:, half:], 'sp', perm=backward)  5.17 us
  transfers between devices with their start and end apart: 9, of which 4 were waited for; matrix products, arithmetic and copies ran while one was open for 16% of the time, Pallas kernels for 0%

profile of v8, /device:TPU:1, one launch (start us, length us, event | category | flops | bytes accessed | tf_op | source)
XLA Modules:
  0.0 194.8 jit_solution(8357054490033160649)
XLA Ops:
  6.5 0.8 maximum_bitcast_fusion.1
  7.4 4.0 %all-gather.4 = bf16[2,43,256]{2,1,0:T(8,128)(2,1)S(1)} all-gather(bf16[1,43,256]{2,1,0:T(8,128)(2,1)S(1)} %maximum_bitcast_fusion.1), channel_id=2, replica_groups=mesh['ylo'=2,'x'=4,'z'=12,'core'=2,'sp'=4] {'ylo'}, dimensions={0}, use_global_device_ids=true | all-gather | bytes 66048 | tf_op jit(solution)/shard_map/all_gather | solution.py:118
  11.3 9.8 %all-gather.1 = bf16[8,43,256]{2,1,0:T(8,128)(2,1)S(1)} all-gather(bf16[2,43,256]{2,1,0:T(8,128)(2,1)S(1)} %all-gather.4), channel_id=3, replica_groups=mesh['ylo'=2,'x'=4,'z'=12,'core'=2,'sp'=4] {'x'}, dimensions={0}, use_global_device_ids=true | all-gather | bytes 220160 | tf_op jit(solution)/shard_map/all_gather | solution.py:118
  21.1 0.8 copy.36
  21.9 0.0 all-gather.8.cloned.1.call-update
  21.9 0.0 all-gather.10.cloned.1.call-start
  22.0 65.7 %all-gather.8.cloned.1.call-done = bf16[48,2,43,256]{3,1,2,0:T(2,128)(2,1)} async-done(((bf16[4,2,43,256]{3,1,2,0:T(2,128)(2,1)}), bf16[48,2,43,256]{3,1,2,0:T(2,128)(2,1)}) %all-gather.8.cloned.1.call-update) | async-done | bytes 2113552 | tf_op jit(solution)/shard_map/all_gather | solution.py:118
  87.7 3.8 %copy.37 = bf16[12,4,2,43,256]{4,1,3,2,0:T(4,128)(2,1)} copy(bf16[12,4,2,43,256]{4,2,3,1,0:T(2,128)(2,1)} %bitcast.94) | data formatting | bytes 4227072 | tf_op jit(solution)/shard_map/all_gather | solution.py:118
  91.4 0.0 all-gather.10.cloned.1.call-update
  91.5 0.7 fusion.49
  92.2 5.3 %collective-permute-start.2 = (bf16[256,256]{1,0:T(8,128)(2,1)}, bf16[256,256]{1,0:T(8,128)(2,1)}, u32[]{:S(2)}, u32[]{:S(2)}) collective-permute-start(bf16[256,256]{1,0:T(8,128)(2,1)} %get-tuple-element.12), channel_id=1, source_target_pairs={{0,3},{1,0},{2,1},{3,2},{4,7},{5,4},{6,5},{7,6},{8,11},{9,8},{10,9... | collective-permute-start | bytes 393224 | tf_op jit(solution)/shard_map/ppermute | solution.py:137
  97.5 3.9 %collective-permute-start.1 = (bf16[256,256]{1,0:T(8,128)(2,1)}, bf16[256,256]{1,0:T(8,128)(2,1)}, u32[]{:S(2)}, u32[]{:S(2)}) collective-permute-start(bf16[256,256]{1,0:T(8,128)(2,1)} %get-tuple-element.12), channel_id=1, source_target_pairs={{0,2},{1,3},{2,0},{3,1},{4,6},{5,7},{6,4},{7,5},{8,10},{9,11},{10,... | collective-permute-start | bytes 393224 | tf_op jit(solution)/shard_map/ppermute | solution.py:137
  101.5 4.0 %collective-permute-start = (bf16[256,256]{1,0:T(8,128)(2,1)}, bf16[256,256]{1,0:T(8,128)(2,1)}, u32[]{:S(2)}, u32[]{:S(2)}) collective-permute-start(bf16[256,256]{1,0:T(8,128)(2,1)} %get-tuple-element.12), channel_id=1, source_target_pairs={{0,1},{1,2},{2,3},{3,0},{4,5},{5,6},{6,7},{7,4},{8,9},{9,10},{10,1... | collective-permute-start | bytes 393224 | tf_op jit(solution)/shard_map/ppermute | solution.py:137
  106.2 0.7 copy.34
  106.8 0.2 convert.21
  107.9 0.2 fusion.38
  108.1 0.3 subtract_convert_fusion
  108.4 0.1 pad_maximum_fusion
  108.6 13.6 %all-gather.10.cloned.1.call-done = bf16[24,4,2,43,256]{4,1,3,2,0:T(4,128)(2,1)} async-done(((bf16[12,4,2,43,256]{4,1,3,2,0:T(4,128)(2,1)}), bf16[24,4,2,43,256]{4,1,3,2,0:T(4,128)(2,1)}) %all-gather.10.cloned.1.call-update) | async-done | bytes 4227088 | tf_op jit(solution)/shard_map/all_gather | solution.py:118
  122.2 5.5 %copy.38 = bf16[24,4,2,43,256]{4,2,3,1,0:T(2,128)(2,1)S(1)} copy(bf16[24,4,2,43,256]{4,1,3,2,0:T(4,128)(2,1)} %all-gather.10.cloned.1.call-done) | data formatting | bytes 8454144 | tf_op jit(solution)/shard_map/all_gather | solution.py:118
  127.6 3.1 %copy.39 = bf16[2,4,12,2,43,256]{5,4,3,2,1,0:T(8,128)(2,1)} copy(bf16[2,4,12,2,43,256]{5,0,4,1,2,3:T(2,128)(2,1)S(1)} %bitcast.90) | data formatting | bytes 8454144 | tf_op jit(solution)/shard_map/transpose | solution.py:127
  130.8 7.3 %reshape.287 = bf16[8256,256]{1,0:T(8,128)(2,1)} reshape(bf16[2,4,12,2,43,256]{5,4,3,2,1,0:T(8,128)(2,1)} %copy.39) | data formatting | bytes 8454144 | tf_op jit(solution)/shard_map/reshape | solution.py:128
  138.0 7.1 %fusion.23 = f32[512,256]{0,1:T(8,128)S(1)} fusion(bf16[512,8192]{1,0:T(8,128)(2,1)} %param.8, bf16[8256,256]{1,0:T(8,128)(2,1)} %reshape.287), kind=kOutput, calls=%fused_computation.27 | convolution fusion | flops 2147483648 | bytes 13107200 | tf_op jit(solution)/shard_map/dot_general | solution.py:186
  145.1 0.6 fusion.32
  145.8 3.6 %collective-permute-start.5 = (bf16[512,256]{0,1:T(8,128)(2,1)S(1)}, bf16[512,256]{0,1:T(8,128)(2,1)S(1)}, u32[]{:S(2)}, u32[]{:S(2)}) collective-permute-start(bf16[512,256]{0,1:T(8,128)(2,1)S(1)} %get-tuple-element.10), channel_id=1, source_target_pairs={{0,3},{1,0},{2,1},{3,2},{4,7},{5,4},{6,5},{7,6},{8,11},{9,8},{10,9... | collective-permute-start | bytes 786440 | tf_op jit(solution)/shard_map/ppermute | solution.py:151
  149.4 2.6 %collective-permute-start.3 = (bf16[512,256]{0,1:T(8,128)(2,1)S(1)}, bf16[512,256]{0,1:T(8,128)(2,1)S(1)}, u32[]{:S(2)}, u32[]{:S(2)}) collective-permute-start(bf16[512,256]{0,1:T(8,128)(2,1)S(1)} %get-tuple-element.10), channel_id=1, source_target_pairs={{0,1},{1,2},{2,3},{3,0},{4,5},{5,6},{6,7},{7,4},{8,9},{9,10},{10,1... | collective-permute-start | bytes 786440 | tf_op jit(solution)/shard_map/ppermute | solution.py:150
  152.0 0.0 collective-permute-done
  152.1 1.1 pad_maximum_fusion.2
  153.2 0.6 gather_fusion
  153.7 0.1 broadcast_select_fusion.1
  153.9 0.0 copy-start.1
  153.9 7.8 %collective-permute-done.5 = bf16[512,256]{0,1:T(8,128)(2,1)S(1)} collective-permute-done((bf16[512,256]{0,1:T(8,128)(2,1)S(1)}, bf16[512,256]{0,1:T(8,128)(2,1)S(1)}, u32[]{:S(2)}, u32[]{:S(2)}) %collective-permute-start.5) | collective-permute-done | bytes 262176 | tf_op jit(solution)/shard_map/ppermute | solution.py:151
  161.7 5.2 %collective-permute-start.6 = (bf16[512,128]{0,1:T(8,128)(2,1)S(1)}, bf16[512,128]{0,1:T(8,128)(2,1)S(1)}, u32[]{:S(2)}, u32[]{:S(2)}) collective-permute-start(bf16[512,128]{0,1:T(8,128)(2,1)S(1)} %slice.66), channel_id=1, source_target_pairs={{0,3},{1,0},{2,1},{3,2},{4,7},{5,4},{6,5},{7,6},{8,11},{9,8},{10,9... | collective-permute-start | bytes 393224 | tf_op jit(solution)/shard_map/ppermute | solution.py:154
  167.0 2.1 %collective-permute-start.4 = (bf16[512,128]{0,1:T(8,128)(2,1)S(1)}, bf16[512,128]{0,1:T(8,128)(2,1)S(1)}, u32[]{:S(2)}, u32[]{:S(2)}) collective-permute-start(bf16[512,128]{0,1:T(8,128)(2,1)S(1)} %slice.65), channel_id=1, source_target_pairs={{0,1},{1,2},{2,3},{3,0},{4,5},{5,6},{6,7},{7,4},{8,9},{9,10},{10,1... | collective-permute-start | bytes 393224 | tf_op jit(solution)/shard_map/ppermute | solution.py:153
  169.1 2.7 %bitcast_reduce_fusion = (f32[4,8,128]{2,1,0:T(8,128)S(1)}, f32[4,256,128,8]{2,1,3,0:T(8,128)}) fusion(pred[256]{0:T(512)(128)(4,1)S(1)} %iota_compare_fusion.1, bf16[128,4,8,128]{0,3,2,1:T(8,128)(2,1)S(1)} %bitcast.91, bf16[4,256,256]{2,1,0:T(8,128)(2,1)S(1)} %broadcast_select_fusion.1), kind=kOutput, calls=%fused_computation.10 | convolution fusion | flops 271577088 | bytes 5521920 | tf_op jit(solution)/shard_map/thgd,hjd->hgtj/dot_general | solution.py:200
  171.8 3.5 %collective-permute-done.4 = bf16[512,128]{0,1:T(8,128)(2,1)S(1)} collective-permute-done((bf16[512,128]{0,1:T(8,128)(2,1)S(1)}, bf16[512,128]{0,1:T(8,128)(2,1)S(1)}, u32[]{:S(2)}, u32[]{:S(2)}) %collective-permute-start.4) | collective-permute-done | bytes 131104 | tf_op jit(solution)/shard_map/ppermute | solution.py:153
  175.4 1.2 pad_maximum_fusion.1
  176.5 0.6 gather_fusion.1
  177.2 0.2 broadcast_select_fusion
  177.3 0.0 copy-start.2
  177.3 1.4 fusion
  178.8 0.7 copy-done
  179.5 0.1 copy-done.2
  179.6 1.2 fusion.12
  180.8 1.2 fusion.10
  182.0 2.2 %fusion.1 = f32[4,8,128]{2,1,0:T(8,128)S(1)} fusion(f32[4,512,128,8]{2,1,3,0:T(8,128)S(1)} %get-tuple-element.18, f32[4,8,128]{2,1,0:T(8,128)S(1)} %max.16, pred[128,512]{0,1:T(8,128)(4,1)S(1)} %iota_compare_fusion), kind=kLoop, calls=%fused_computation.5 | loop fusion | flops 10481664 | bytes 8486912 | tf_op jit(solution)/shard_map/reduce_sum | solution.py:216
  184.2 2.5 %fusion.14 = bf16[128,4,8,128]{0,3,2,1:T(8,128)(2,1)S(1)} fusion(f32[4,8,128,128]{2,3,1,0:T(8,128)S(1)} %fusion.12, f32[4,512,128,8]{2,1,3,0:T(8,128)S(1)} %get-tuple-element.18, f32[4,8,128]{2,1,0:T(8,128)S(1)} %max.16, pred[128,512]{0,1:T(8,128)(4,1)S(1)} %iota_compare_fusion, f32[128,4,8]{0,2,1:T(8,128)S(1)} %add_bitcast_fusion, ...), kind=kOutput, calls=%fused_computation.20 | convolution fusion | flops 548929536 | bytes 12156928 | tf_op jit(solution)/shard_map/hgtu,hud->hgtd/dot_general | solution.py:222
  186.7 1.3 copy.45
  (37 shorter events, 0.3 us)
Async XLA Ops:
  6.5 84.9 %copy-start.7 = (bf16[1,256,128]{2,1,0:T(8,128)(2,1)S(1)}, bf16[1,256,128]{2,1,0:T(8,128)(2,1)}, u32[]{:S(2)}) copy-start(bf16[1,256,128]{2,1,0:T(8,128)(2,1)} %param.13) | copy-start | bytes 196612
  6.5 84.9 %copy-start.8 = (bf16[1,256,128]{2,1,0:T(8,128)(2,1)S(1)}, bf16[1,256,128]{2,1,0:T(8,128)(2,1)}, u32[]{:S(2)}) copy-start(bf16[1,256,128]{2,1,0:T(8,128)(2,1)} %param.12) | copy-start | bytes 196612
  6.5 99.6 %copy-start.3 = (bf16[128,4096]{1,0:T(8,128)(2,1)S(1)}, bf16[128,4096]{1,0:T(8,128)(2,1)}, u32[]{:S(2)}) copy-start(bf16[128,4096]{1,0:T(8,128)(2,1)} %param.9) | copy-start | bytes 3145732
  6.5 81.1 %all-gather.8.cloned.1.call-start = ((), (), s32[]{:S(2)}) async-start(), calls=%async_computation | async-start | bytes 2289664 | tf_op jit(solution)/shard_map/all_gather | solution.py:118
  21.9 100.2 %all-gather.10.cloned.1.call-start = ((), (), s32[]{:S(2)}) async-start(), calls=%async_computation.1 | async-start | bytes 6340608 | tf_op jit(solution)/shard_map/all_gather | solution.py:118
  92.2 59.8 %collective-permute-start.2 = (bf16[256,256]{1,0:T(8,128)(2,1)}, bf16[256,256]{1,0:T(8,128)(2,1)}, u32[]{:S(2)}, u32[]{:S(2)}) collective-permute-start(bf16[256,256]{1,0:T(8,128)(2,1)} %get-tuple-element.12), channel_id=1, source_target_pairs={{0,3},{1,0},{2,1},{3,2},{4,7},{5,4},{6,5},{7,6},{8,11},{9,8},{10,9... | collective-permute-start | bytes 393224 | tf_op jit(solution)/shard_map/ppermute | solution.py:137
  97.5 54.5 %collective-permute-start.1 = (bf16[256,256]{1,0:T(8,128)(2,1)}, bf16[256,256]{1,0:T(8,128)(2,1)}, u32[]{:S(2)}, u32[]{:S(2)}) collective-permute-start(bf16[256,256]{1,0:T(8,128)(2,1)} %get-tuple-element.12), channel_id=1, source_target_pairs={{0,2},{1,3},{2,0},{3,1},{4,6},{5,7},{6,4},{7,5},{8,10},{9,11},{10,... | collective-permute-start | bytes 393224 | tf_op jit(solution)/shard_map/ppermute | solution.py:137
  101.5 50.6 %collective-permute-start = (bf16[256,256]{1,0:T(8,128)(2,1)}, bf16[256,256]{1,0:T(8,128)(2,1)}, u32[]{:S(2)}, u32[]{:S(2)}) collective-permute-start(bf16[256,256]{1,0:T(8,128)(2,1)} %get-tuple-element.12), channel_id=1, source_target_pairs={{0,1},{1,2},{2,3},{3,0},{4,5},{5,6},{6,7},{7,4},{8,9},{9,10},{10,1... | collective-permute-start | bytes 393224 | tf_op jit(solution)/shard_map/ppermute | solution.py:137
  138.0 14.0 %copy-start.6 = (bf16[1,256,256]{2,1,0:T(8,128)(2,1)S(1)}, bf16[1,256,256]{2,1,0:T(8,128)(2,1)}, u32[]{:S(2)}) copy-start(bf16[1,256,256]{2,1,0:T(8,128)(2,1)} %get-tuple-element.11) | copy-start | bytes 393220
  145.8 15.9 %collective-permute-start.5 = (bf16[512,256]{0,1:T(8,128)(2,1)S(1)}, bf16[512,256]{0,1:T(8,128)(2,1)S(1)}, u32[]{:S(2)}, u32[]{:S(2)}) collective-permute-start(bf16[512,256]{0,1:T(8,128)(2,1)S(1)} %get-tuple-element.10), channel_id=1, source_target_pairs={{0,3},{1,0},{2,1},{3,2},{4,7},{5,4},{6,5},{7,6},{8,11},{9,8},{10,9... | collective-permute-start | bytes 786440 | tf_op jit(solution)/shard_map/ppermute | solution.py:151
  149.4 17.5 %collective-permute-start.3 = (bf16[512,256]{0,1:T(8,128)(2,1)S(1)}, bf16[512,256]{0,1:T(8,128)(2,1)S(1)}, u32[]{:S(2)}, u32[]{:S(2)}) collective-permute-start(bf16[512,256]{0,1:T(8,128)(2,1)S(1)} %get-tuple-element.10), channel_id=1, source_target_pairs={{0,1},{1,2},{2,3},{3,0},{4,5},{5,6},{6,7},{7,4},{8,9},{9,10},{10,1... | collective-permute-start | bytes 786440 | tf_op jit(solution)/shard_map/ppermute | solution.py:150
  153.9 21.5 %copy-start.1 = (bf16[4,256,256]{2,1,0:T(8,128)(2,1)}, bf16[4,256,256]{2,1,0:T(8,128)(2,1)S(1)}, u32[]{:S(2)}) copy-start(bf16[4,256,256]{2,1,0:T(8,128)(2,1)S(1)} %broadcast_select_fusion.1) | copy-start | bytes 1572868
  161.7 13.6 %copy-start.4 = (bf16[512,256]{0,1:T(8,128)(2,1)}, bf16[512,256]{0,1:T(8,128)(2,1)S(1)}, u32[]{:S(2)}) copy-start(bf16[512,256]{0,1:T(8,128)(2,1)S(1)} %collective-permute-done.5) | copy-start | bytes 786436
  161.7 10.0 %collective-permute-start.6 = (bf16[512,128]{0,1:T(8,128)(2,1)S(1)}, bf16[512,128]{0,1:T(8,128)(2,1)S(1)}, u32[]{:S(2)}, u32[]{:S(2)}) collective-permute-start(bf16[512,128]{0,1:T(8,128)(2,1)S(1)} %slice.66), channel_id=1, source_target_pairs={{0,3},{1,0},{2,1},{3,2},{4,7},{5,4},{6,5},{7,6},{8,11},{9,8},{10,9... | collective-permute-start | bytes 393224 | tf_op jit(solution)/shard_map/ppermute | solution.py:154
  166.9 8.4 %copy-start.5 = (bf16[512,256]{0,1:T(8,128)(2,1)}, bf16[512,256]{0,1:T(8,128)(2,1)S(1)}, u32[]{:S(2)}) copy-start(bf16[512,256]{0,1:T(8,128)(2,1)S(1)} %collective-permute-done.3) | copy-start | bytes 786436
  167.0 8.4 %collective-permute-start.4 = (bf16[512,128]{0,1:T(8,128)(2,1)S(1)}, bf16[512,128]{0,1:T(8,128)(2,1)S(1)}, u32[]{:S(2)}, u32[]{:S(2)}) collective-permute-start(bf16[512,128]{0,1:T(8,128)(2,1)S(1)} %slice.65), channel_id=1, source_target_pairs={{0,1},{1,2},{2,3},{3,0},{4,5},{5,6},{6,7},{7,4},{8,9},{9,10},{10,1... | collective-permute-start | bytes 393224 | tf_op jit(solution)/shard_map/ppermute | solution.py:153
  177.3 2.2 %copy-start = (f32[4,256,128,8]{2,1,3,0:T(8,128)S(1)}, f32[4,256,128,8]{2,1,3,0:T(8,128)}, u32[]{:S(2)}) copy-start(f32[4,256,128,8]{2,1,3,0:T(8,128)} %get-tuple-element.16) | copy-start | bytes 12582916
  177.3 2.3 %copy-start.2 = (bf16[4,256,256]{2,1,0:T(8,128)(2,1)S(1)}, bf16[4,256,256]{2,1,0:T(8,128)(2,1)}, u32[]{:S(2)}) copy-start(bf16[4,256,256]{2,1,0:T(8,128)(2,1)} %copy-done.1) | copy-start | bytes 1572868
Sparse Core Ops, SparseCore 0:
  22.1 65.5 all-gather.7
  91.6 30.5 all-gather.9

commit v9 on v4

--- a/solution.py
+++ b/solution.py
@@ -114,17 +114,14 @@
 
 def gather_weights(shard):
     gathered = shard
-    for stage in GATHER_STAGES:
+    for stage in GATHER_STAGES[:-1]:
         gathered = lax.all_gather(gathered, stage, axis=0, tiled=False)
-        if len(stage) > 1:
-            sizes = tuple(dict(FSDP_PARTS)[name] for name in stage)
-            gathered = gathered.reshape(sizes + gathered.shape[1:])
-    layout = []
-    for stage in reversed(GATHER_STAGES):
-        layout.extend(stage)
-    perm = [layout.index(name) for name in FSDP_AXES]
-    rank = len(FSDP_AXES)
-    gathered = gathered.transpose(perm + [rank, rank + 1])
+    early = [name for stage in reversed(GATHER_STAGES[:-1]) for name in stage]
+    wanted = [name for name in FSDP_AXES if name in early]
+    rank = len(early)
+    gathered = gathered.transpose([early.index(name) for name in wanted] + [rank, rank + 1])
+    (last,) = GATHER_STAGES[-1]
+    gathered = lax.all_gather(gathered, last, axis=FSDP_AXES.index(last), tiled=False)
     return gathered.reshape(-1, shard.shape[1])
 
 

time: 197 us -> 191 us (0.970)
  local copies, waits for them, and re-layouts: 24.5 us -> 17.7 us
    all_gather x0 -> x1, waiting for transfers between devices: none -> 9.91 us  [gather_weights(): lax.all_gather(gathered, last, axis=FSDP_AXES.index(last), tiled=False)]
    all_gather x3 -> x1, local copies, waits for them, and re-layouts: 10 us -> 0.81 us  [gather_weights(): gathered = lax.all_gather(gathered, stage, axis=0, tiled=False)]
    all_gather x2 -> x1, waiting for transfers between devices: 74.1 us -> 65.6 us  [gather_weights(): gathered = lax.all_gather(gathered, stage, axis=0, tiled=False)]
    all_gather x0 -> x1, local copies, waits for them, and re-layouts: none -> 4.78 us  [gather_weights(): lax.all_gather(gathered, last, axis=FSDP_AXES.index(last), tiled=False)]
    transpose x1 -> x0, local copies, waits for them, and re-layouts: 3.13 us -> none  [gather_weights(): gathered = gathered.transpose(perm + [rank, rank + 1])]
  transfers between devices with their start and end apart: 8 -> 8, of which waited for: 6 -> 5; matrix products, arithmetic and copies ran while one was open for 3% -> 4% of each run, Pallas kernels for 0% -> 0%
where the time goes in v9:
time: 191 us
  waiting for transfers between devices  97.3 us (51%)
  starting transfers between devices  25 us (13%)
  local copies, waits for them, and re-layouts  17.7 us (9%)
  between operations  15 us (8%)
  matrix products  14.8 us (8%)
  blocking collectives  12.9 us (7%)
  other arithmetic  7.99 us (4%)
    all_gather x1, waiting for transfers between devices, gather_weights(): gathered = lax.all_gather(gathered, stage, axis=0, tiled=False)  65.6 us
    ppermute x6, starting transfers between devices, gather_sp(): pieces.append(lax.ppermute(block, 'sp', perm=pairs))  24.9 us
    ppermute x6, waiting for transfers between devices, gather_sp(): pieces.append(lax.ppermute(block, 'sp', perm=pairs))  21.7 us
    all_gather x2, blocking collectives, gather_weights(): gathered = lax.all_gather(gathered, stage, axis=0, tiled=False)  12.9 us
    all_gather x1, waiting for transfers between devices, gather_weights(): lax.all_gather(gathered, last, axis=FSDP_AXES.index(last), tiled=False)  9.91 us
    reshape x1, local copies, waits for them, and re-layouts, gather_weights(): return gathered.reshape(-1, shard.shape[1])  7.07 us
    dot_general x1, matrix products, per_device(): jnp.dot(hidden_rows, whole_kv[:model_width], preferred_element_type=jnp.f...  7.03 us
    all_gather x1, local copies, waits for them, and re-layouts, gather_weights(): lax.all_gather(gathered, last, axis=FSDP_AXES.index(last), tiled=False)  4.78 us
  transfers between devices with their start and end apart: 8, of which 5 were waited for; matrix products, arithmetic and copies ran while one was open for 4% of the time, Pallas kernels for 0%

profile of v9, /device:TPU:9, one launch (start us, length us, event | category | flops | bytes accessed | tf_op | source)
XLA Modules:
  0.0 190.7 jit_solution(17591168674690648088)
XLA Ops:
  6.5 0.7 maximum_bitcast_fusion
  7.3 3.3 %all-gather.4 = bf16[2,43,256]{2,1,0:T(8,128)(2,1)S(1)} all-gather(bf16[1,43,256]{2,1,0:T(8,128)(2,1)S(1)} %maximum_bitcast_fusion), channel_id=2, replica_groups=mesh['ylo'=2,'x'=4,'z'=12,'core'=2,'sp'=4] {'ylo'}, dimensions={0}, use_global_device_ids=true | all-gather | bytes 66048 | tf_op jit(solution)/shard_map/all_gather | solution.py:118
  10.6 9.6 %all-gather.1 = bf16[8,43,256]{2,1,0:T(8,128)(2,1)S(1)} all-gather(bf16[2,43,256]{2,1,0:T(8,128)(2,1)S(1)} %all-gather.4), channel_id=3, replica_groups=mesh['ylo'=2,'x'=4,'z'=12,'core'=2,'sp'=4] {'x'}, dimensions={0}, use_global_device_ids=true | all-gather | bytes 220160 | tf_op jit(solution)/shard_map/all_gather | solution.py:118
  20.2 0.8 copy.36
  21.0 0.0 all-gather.8.cloned.1.call-update
  21.0 0.0 all-gather.10.cloned.1.call-start
  21.1 65.6 %all-gather.8.cloned.1.call-done = bf16[48,2,43,256]{3,1,2,0:T(2,128)(2,1)} async-done(((bf16[4,2,43,256]{3,1,2,0:T(2,128)(2,1)}), bf16[48,2,43,256]{3,1,2,0:T(2,128)(2,1)}) %all-gather.8.cloned.1.call-update) | async-done | bytes 2113552 | tf_op jit(solution)/shard_map/all_gather | solution.py:118
  86.7 0.0 all-gather.10.cloned.1.call-update
  86.7 0.9 fusion.49
  87.6 4.4 %collective-permute-start.2 = (bf16[256,256]{1,0:T(8,128)(2,1)S(1)}, bf16[256,256]{1,0:T(8,128)(2,1)}, u32[]{:S(2)}, u32[]{:S(2)}) collective-permute-start(bf16[256,256]{1,0:T(8,128)(2,1)S(1)} %get-tuple-element.12), channel_id=1, source_target_pairs={{0,3},{1,0},{2,1},{3,2},{4,7},{5,4},{6,5},{7,6},{8,11},{9,8},{10,9... | collective-permute-start | bytes 393224 | tf_op jit(solution)/shard_map/ppermute | solution.py:134
  92.0 4.8 %collective-permute-start.1 = (bf16[256,256]{1,0:T(8,128)(2,1)S(1)}, bf16[256,256]{1,0:T(8,128)(2,1)}, u32[]{:S(2)}, u32[]{:S(2)}) collective-permute-start(bf16[256,256]{1,0:T(8,128)(2,1)S(1)} %get-tuple-element.12), channel_id=1, source_target_pairs={{0,2},{1,3},{2,0},{3,1},{4,6},{5,7},{6,4},{7,5},{8,10},{9,11},{10,... | collective-permute-start | bytes 393224 | tf_op jit(solution)/shard_map/ppermute | solution.py:134
  96.8 3.1 %collective-permute-start = (bf16[256,256]{1,0:T(8,128)(2,1)S(1)}, bf16[256,256]{1,0:T(8,128)(2,1)}, u32[]{:S(2)}, u32[]{:S(2)}) collective-permute-start(bf16[256,256]{1,0:T(8,128)(2,1)S(1)} %get-tuple-element.12), channel_id=1, source_target_pairs={{0,1},{1,2},{2,3},{3,0},{4,5},{5,6},{6,7},{7,4},{8,9},{9,10},{10,1... | collective-permute-start | bytes 393224 | tf_op jit(solution)/shard_map/ppermute | solution.py:134
  100.6 1.6 copy.34
  102.3 0.2 convert.21
  103.4 0.2 fusion.38
  103.6 0.3 subtract_convert_fusion
  103.9 0.1 pad_maximum_fusion
  104.0 0.0 collective-permute-done.2
  104.0 0.0 collective-permute-done.1
  104.0 2.2 %collective-permute-done = bf16[256,256]{1,0:T(8,128)(2,1)} collective-permute-done((bf16[256,256]{1,0:T(8,128)(2,1)S(1)}, bf16[256,256]{1,0:T(8,128)(2,1)}, u32[]{:S(2)}, u32[]{:S(2)}) %collective-permute-start) | collective-permute-done | bytes 131104 | tf_op jit(solution)/shard_map/ppermute | solution.py:134
  106.1 1.1 pad_maximum_fusion.2
  107.2 0.6 gather_fusion
  107.8 0.1 broadcast_select_fusion.1
  108.0 0.0 copy-start.1
  108.0 9.9 %all-gather.10.cloned.1.call-done = bf16[2,4,12,86,256]{4,0,3,1,2:T(2,128)(2,1)} async-done(((bf16[2,4,12,43,256]{4,0,3,1,2:T(2,128)(2,1)}), bf16[2,4,12,86,256]{4,0,3,1,2:T(2,128)(2,1)}) %all-gather.10.cloned.1.call-update) | async-done | bytes 4227088 | tf_op jit(solution)/shard_map/all_gather | solution.py:124
  117.9 4.8 %copy.37 = bf16[2,4,12,86,256]{4,3,2,1,0:T(8,128)(2,1)} copy(bf16[2,4,12,86,256]{4,0,3,1,2:T(2,128)(2,1)} %all-gather.10.cloned.1.call-done) | data formatting | bytes 8454144 | tf_op jit(solution)/shard_map/all_gather | solution.py:124
  122.7 7.1 %reshape.287 = bf16[8256,256]{1,0:T(8,128)(2,1)} reshape(bf16[2,4,12,86,256]{4,3,2,1,0:T(8,128)(2,1)} %copy.37) | data formatting | bytes 8454144 | tf_op jit(solution)/shard_map/reshape | solution.py:125
  129.7 7.0 %fusion.23 = f32[512,256]{0,1:T(8,128)S(1)} fusion(bf16[512,8192]{1,0:T(8,128)(2,1)} %param.8, bf16[8256,256]{1,0:T(8,128)(2,1)} %reshape.287), kind=kOutput, calls=%fused_computation.27 | convolution fusion | flops 2147483648 | bytes 13107200 | tf_op jit(solution)/shard_map/dot_general | solution.py:165
  136.8 0.6 fusion.32
  137.5 4.4 %collective-permute-start.5 = (bf16[512,256]{0,1:T(8,128)(2,1)S(1)}, bf16[512,256]{0,1:T(8,128)(2,1)S(1)}, u32[]{:S(2)}, u32[]{:S(2)}) collective-permute-start(bf16[512,256]{0,1:T(8,128)(2,1)S(1)} %get-tuple-element.10), channel_id=1, source_target_pairs={{0,3},{1,0},{2,1},{3,2},{4,7},{5,4},{6,5},{7,6},{8,11},{9,8},{10,9... | collective-permute-start | bytes 786440 | tf_op jit(solution)/shard_map/ppermute | solution.py:134
  141.9 4.8 %collective-permute-start.4 = (bf16[512,256]{0,1:T(8,128)(2,1)S(1)}, bf16[512,256]{0,1:T(8,128)(2,1)S(1)}, u32[]{:S(2)}, u32[]{:S(2)}) collective-permute-start(bf16[512,256]{0,1:T(8,128)(2,1)S(1)} %get-tuple-element.10), channel_id=1, source_target_pairs={{0,2},{1,3},{2,0},{3,1},{4,6},{5,7},{6,4},{7,5},{8,10},{9,11},{10,... | collective-permute-start | bytes 786440 | tf_op jit(solution)/shard_map/ppermute | solution.py:134
  146.7 3.3 %collective-permute-start.3 = (bf16[512,256]{0,1:T(8,128)(2,1)S(1)}, bf16[512,256]{0,1:T(8,128)(2,1)S(1)}, u32[]{:S(2)}, u32[]{:S(2)}) collective-permute-start(bf16[512,256]{0,1:T(8,128)(2,1)S(1)} %get-tuple-element.10), channel_id=1, source_target_pairs={{0,1},{1,2},{2,3},{3,0},{4,5},{5,6},{6,7},{7,4},{8,9},{9,10},{10,1... | collective-permute-start | bytes 786440 | tf_op jit(solution)/shard_map/ppermute | solution.py:134
  150.1 2.7 %bitcast_reduce_fusion = (f32[4,8,128]{2,1,0:T(8,128)S(1)}, f32[4,256,128,8]{2,1,3,0:T(8,128)}) fusion(pred[256]{0:T(512)(128)(4,1)S(1)} %iota_compare_fusion.1, bf16[128,4,8,128]{0,3,2,1:T(8,128)(2,1)S(1)} %bitcast.88, bf16[4,256,256]{2,1,0:T(8,128)(2,1)S(1)} %broadcast_select_fusion.1), kind=kOutput, calls=%fused_computation.10 | convolution fusion | flops 271577088 | bytes 5521920 | tf_op jit(solution)/shard_map/thgd,hjd->hgtj/dot_general | solution.py:179
  152.8 0.0 collective-permute-done.5
  152.8 15.1 %collective-permute-done.4 = bf16[512,256]{0,1:T(8,128)(2,1)S(1)} collective-permute-done((bf16[512,256]{0,1:T(8,128)(2,1)S(1)}, bf16[512,256]{0,1:T(8,128)(2,1)S(1)}, u32[]{:S(2)}, u32[]{:S(2)}) %collective-permute-start.4) | collective-permute-done | bytes 262176 | tf_op jit(solution)/shard_map/ppermute | solution.py:134
  167.9 4.5 %collective-permute-done.3 = bf16[512,256]{0,1:T(8,128)(2,1)S(1)} collective-permute-done((bf16[512,256]{0,1:T(8,128)(2,1)S(1)}, bf16[512,256]{0,1:T(8,128)(2,1)S(1)}, u32[]{:S(2)}, u32[]{:S(2)}) %collective-permute-start.3) | collective-permute-done | bytes 262176 | tf_op jit(solution)/shard_map/ppermute | solution.py:134
  172.4 0.1 pad_maximum_fusion.1
  172.5 0.6 gather_fusion.1
  173.1 0.2 broadcast_select_fusion
  173.3 0.0 copy-start.2
  173.3 1.4 fusion
  174.7 0.7 copy-done
  175.5 0.1 copy-done.2
  175.6 1.2 fusion.12
  176.8 1.1 fusion.10
  177.9 2.1 %fusion.1 = f32[4,8,128]{2,1,0:T(8,128)S(1)} fusion(f32[4,512,128,8]{2,1,3,0:T(8,128)S(1)} %get-tuple-element.18, f32[4,8,128]{2,1,0:T(8,128)S(1)} %max.16, pred[128,512]{0,1:T(8,128)(4,1)S(1)} %iota_compare_fusion), kind=kLoop, calls=%fused_computation.5 | loop fusion | flops 10481664 | bytes 8486912 | tf_op jit(solution)/shard_map/reduce_sum | solution.py:195
  180.1 2.5 %fusion.14 = bf16[128,4,8,128]{0,3,2,1:T(8,128)(2,1)S(1)} fusion(f32[4,8,128,128]{2,3,1,0:T(8,128)S(1)} %fusion.12, f32[4,512,128,8]{2,1,3,0:T(8,128)S(1)} %get-tuple-element.18, f32[4,8,128]{2,1,0:T(8,128)S(1)} %max.16, pred[128,512]{0,1:T(8,128)(4,1)S(1)} %iota_compare_fusion, f32[128,4,8]{0,2,1:T(8,128)S(1)} %add_bitcast_fusion, ...), kind=kOutput, calls=%fused_computation.20 | convolution fusion | flops 548929536 | bytes 12156928 | tf_op jit(solution)/shard_map/hgtu,hud->hgtd/dot_general | solution.py:201
  182.5 1.3 copy.43
  (18 shorter events, 0.2 us)
Async XLA Ops:
  6.5 80.1 %all-gather.8.cloned.1.call-start = ((), (), s32[]{:S(2)}) async-start(), calls=%async_computation | async-start | bytes 2289664 | tf_op jit(solution)/shard_map/all_gather | solution.py:118
  21.0 96.9 %all-gather.10.cloned.1.call-start = ((), (), s32[]{:S(2)}) async-start(), calls=%async_computation.1 | async-start | bytes 6340608 | tf_op jit(solution)/shard_map/all_gather | solution.py:124
  87.6 16.4 %collective-permute-start.2 = (bf16[256,256]{1,0:T(8,128)(2,1)S(1)}, bf16[256,256]{1,0:T(8,128)(2,1)}, u32[]{:S(2)}, u32[]{:S(2)}) collective-permute-start(bf16[256,256]{1,0:T(8,128)(2,1)S(1)} %get-tuple-element.12), channel_id=1, source_target_pairs={{0,3},{1,0},{2,1},{3,2},{4,7},{5,4},{6,5},{7,6},{8,11},{9,8},{10,9... | collective-permute-start | bytes 393224 | tf_op jit(solution)/shard_map/ppermute | solution.py:134
  92.0 12.0 %collective-permute-start.1 = (bf16[256,256]{1,0:T(8,128)(2,1)S(1)}, bf16[256,256]{1,0:T(8,128)(2,1)}, u32[]{:S(2)}, u32[]{:S(2)}) collective-permute-start(bf16[256,256]{1,0:T(8,128)(2,1)S(1)} %get-tuple-element.12), channel_id=1, source_target_pairs={{0,2},{1,3},{2,0},{3,1},{4,6},{5,7},{6,4},{7,5},{8,10},{9,11},{10,... | collective-permute-start | bytes 393224 | tf_op jit(solution)/shard_map/ppermute | solution.py:134
  96.8 9.3 %collective-permute-start = (bf16[256,256]{1,0:T(8,128)(2,1)S(1)}, bf16[256,256]{1,0:T(8,128)(2,1)}, u32[]{:S(2)}, u32[]{:S(2)}) collective-permute-start(bf16[256,256]{1,0:T(8,128)(2,1)S(1)} %get-tuple-element.12), channel_id=1, source_target_pairs={{0,1},{1,2},{2,3},{3,0},{4,5},{5,6},{6,7},{7,4},{8,9},{9,10},{10,1... | collective-permute-start | bytes 393224 | tf_op jit(solution)/shard_map/ppermute | solution.py:134
  108.0 42.1 %copy-start.1 = (bf16[4,256,256]{2,1,0:T(8,128)(2,1)}, bf16[4,256,256]{2,1,0:T(8,128)(2,1)S(1)}, u32[]{:S(2)}) copy-start(bf16[4,256,256]{2,1,0:T(8,128)(2,1)S(1)} %broadcast_select_fusion.1) | copy-start | bytes 1572868
  137.5 15.3 %collective-permute-start.5 = (bf16[512,256]{0,1:T(8,128)(2,1)S(1)}, bf16[512,256]{0,1:T(8,128)(2,1)S(1)}, u32[]{:S(2)}, u32[]{:S(2)}) collective-permute-start(bf16[512,256]{0,1:T(8,128)(2,1)S(1)} %get-tuple-element.10), channel_id=1, source_target_pairs={{0,3},{1,0},{2,1},{3,2},{4,7},{5,4},{6,5},{7,6},{8,11},{9,8},{10,9... | collective-permute-start | bytes 786440 | tf_op jit(solution)/shard_map/ppermute | solution.py:134
  141.9 26.0 %collective-permute-start.4 = (bf16[512,256]{0,1:T(8,128)(2,1)S(1)}, bf16[512,256]{0,1:T(8,128)(2,1)S(1)}, u32[]{:S(2)}, u32[]{:S(2)}) collective-permute-start(bf16[512,256]{0,1:T(8,128)(2,1)S(1)} %get-tuple-element.10), channel_id=1, source_target_pairs={{0,2},{1,3},{2,0},{3,1},{4,6},{5,7},{6,4},{7,5},{8,10},{9,11},{10,... | collective-permute-start | bytes 786440 | tf_op jit(solution)/shard_map/ppermute | solution.py:134
  146.7 25.6 %collective-permute-start.3 = (bf16[512,256]{0,1:T(8,128)(2,1)S(1)}, bf16[512,256]{0,1:T(8,128)(2,1)S(1)}, u32[]{:S(2)}, u32[]{:S(2)}) collective-permute-start(bf16[512,256]{0,1:T(8,128)(2,1)S(1)} %get-tuple-element.10), channel_id=1, source_target_pairs={{0,1},{1,2},{2,3},{3,0},{4,5},{5,6},{6,7},{7,4},{8,9},{9,10},{10,1... | collective-permute-start | bytes 786440 | tf_op jit(solution)/shard_map/ppermute | solution.py:134
  173.3 2.2 %copy-start = (f32[4,256,128,8]{2,1,3,0:T(8,128)S(1)}, f32[4,256,128,8]{2,1,3,0:T(8,128)}, u32[]{:S(2)}) copy-start(f32[4,256,128,8]{2,1,3,0:T(8,128)} %get-tuple-element.16) | copy-start | bytes 12582916
  173.3 2.3 %copy-start.2 = (bf16[4,256,256]{2,1,0:T(8,128)(2,1)S(1)}, bf16[4,256,256]{2,1,0:T(8,128)(2,1)}, u32[]{:S(2)}) copy-start(bf16[4,256,256]{2,1,0:T(8,128)(2,1)} %copy-done.1) | copy-start | bytes 1572868
Sparse Core Ops, SparseCore 0:
  21.1 65.4 all-gather.7
  89.0 28.7 all-gather.9

commit v10 on v9

--- a/solution.py
+++ b/solution.py
@@ -165,7 +165,9 @@
     kv_sum = jnp.dot(hidden_rows, whole_kv[:model_width], preferred_element_type=jnp.float32)
     new_keys = rotate(kv_sum[:, :kv_cols], cosine_table, sine_table, kv_local).astype(jnp.bfloat16)
     new_values = kv_sum[:, kv_cols:].astype(jnp.bfloat16)
-    new_all = gather_sp(jnp.concatenate([new_keys, new_values], axis=1))
+    new_kv = jnp.concatenate([new_keys, new_values], axis=1)
+    repeated = jnp.broadcast_to(new_kv[None], (lax.axis_size("sp"),) + new_kv.shape)
+    new_all = lax.all_to_all(repeated, "sp", split_axis=0, concat_axis=0, tiled=True)
 
     rotated_q = rotate(queries.astype(jnp.float32), query_cosine, query_sine, HQ).astype(
         jnp.bfloat16

time: 191 us -> 190 us (level)
  the two profiles are of different devices: /device:TPU:9 before, /device:TPU:1 now
where the time goes in v10:
time: 190 us; the launch traced here: 189 us
  waiting for transfers between devices  102 us (54%)
  local copies, waits for them, and re-layouts  18.2 us (10%)
  starting transfers between devices  18 us (9%)
  between operations  15 us (8%)
  matrix products  14.7 us (8%)
  blocking collectives  13.7 us (7%)
  other arithmetic  7.75 us (4%)
    all_gather x1, waiting for transfers between devices, gather_weights(): gathered = lax.all_gather(gathered, stage, axis=0, tiled=False)  65.7 us
    all_to_all x1, waiting for transfers between devices, per_device(): lax.all_to_all(repeated, 'sp', split_axis=0, concat_axis=0, tiled=True)  21 us
    all_gather x1, waiting for transfers between devices, gather_weights(): lax.all_gather(gathered, last, axis=FSDP_AXES.index(last), tiled=False)  15.4 us
    all_gather x2, blocking collectives, gather_weights(): gathered = lax.all_gather(gathered, stage, axis=0, tiled=False)  13.7 us
    ppermute x3, starting transfers between devices, gather_sp(): pieces.append(lax.ppermute(block, 'sp', perm=pairs))  13.3 us
    reshape x1, local copies, waits for them, and re-layouts, gather_weights(): return gathered.reshape(-1, shard.shape[1])  7.09 us
    dot_general x1, matrix products, per_device(): jnp.dot(hidden_rows, whole_kv[:model_width], preferred_element_type=jnp.f...  7.04 us
    all_gather x1, local copies, waits for them, and re-layouts, gather_weights(): lax.all_gather(gathered, last, axis=FSDP_AXES.index(last), tiled=False)  4.77 us
  transfers between devices with their start and end apart: 6, of which 3 were waited for; matrix products, arithmetic and copies ran while one was open for 15% of the time, Pallas kernels for 0%

profile of v10, /device:TPU:1, one launch (start us, length us, event | category | flops | bytes accessed | tf_op | source)
XLA Modules:
  0.0 189.5 jit_solution(8988300905180278798)
XLA Ops:
  6.5 0.0 all-gather.8.cloned.1.call-start
  6.5 0.7 maximum_bitcast_fusion
  7.3 4.0 %all-gather.4 = bf16[2,43,256]{2,1,0:T(8,128)(2,1)S(1)} all-gather(bf16[1,43,256]{2,1,0:T(8,128)(2,1)S(1)} %maximum_bitcast_fusion), channel_id=2, replica_groups=mesh['ylo'=2,'x'=4,'z'=12,'core'=2,'sp'=4] {'ylo'}, dimensions={0}, use_global_device_ids=true | all-gather | bytes 66048 | tf_op jit(solution)/shard_map/all_gather | solution.py:118
  11.2 9.8 %all-gather.1 = bf16[8,43,256]{2,1,0:T(8,128)(2,1)S(1)} all-gather(bf16[2,43,256]{2,1,0:T(8,128)(2,1)S(1)} %all-gather.4), channel_id=3, replica_groups=mesh['ylo'=2,'x'=4,'z'=12,'core'=2,'sp'=4] {'x'}, dimensions={0}, use_global_device_ids=true | all-gather | bytes 220160 | tf_op jit(solution)/shard_map/all_gather | solution.py:118
  21.0 0.8 copy.39
  21.8 0.0 all-gather.8.cloned.1.call-update
  21.8 0.0 all-gather.10.cloned.1.call-start
  21.9 65.7 %all-gather.8.cloned.1.call-done = bf16[48,2,43,256]{3,1,2,0:T(2,128)(2,1)} async-done(((bf16[4,2,43,256]{3,1,2,0:T(2,128)(2,1)}), bf16[48,2,43,256]{3,1,2,0:T(2,128)(2,1)}) %all-gather.8.cloned.1.call-update) | async-done | bytes 2113552 | tf_op jit(solution)/shard_map/all_gather | solution.py:118
  87.6 0.0 all-gather.10.cloned.1.call-update
  87.6 0.9 fusion.49
  88.5 5.3 %collective-permute-start.2 = (bf16[256,256]{1,0:T(8,128)(2,1)S(1)}, bf16[256,256]{1,0:T(8,128)(2,1)}, u32[]{:S(2)}, u32[]{:S(2)}) collective-permute-start(bf16[256,256]{1,0:T(8,128)(2,1)S(1)} %get-tuple-element.10), channel_id=1, source_target_pairs={{0,3},{1,0},{2,1},{3,2},{4,7},{5,4},{6,5},{7,6},{8,11},{9,8},{10,9... | collective-permute-start | bytes 393224 | tf_op jit(solution)/shard_map/ppermute | solution.py:134
  93.8 3.9 %collective-permute-start.1 = (bf16[256,256]{1,0:T(8,128)(2,1)S(1)}, bf16[256,256]{1,0:T(8,128)(2,1)}, u32[]{:S(2)}, u32[]{:S(2)}) collective-permute-start(bf16[256,256]{1,0:T(8,128)(2,1)S(1)} %get-tuple-element.10), channel_id=1, source_target_pairs={{0,2},{1,3},{2,0},{3,1},{4,6},{5,7},{6,4},{7,5},{8,10},{9,11},{10,... | collective-permute-start | bytes 393224 | tf_op jit(solution)/shard_map/ppermute | solution.py:134
  97.8 4.0 %collective-permute-start = (bf16[256,256]{1,0:T(8,128)(2,1)S(1)}, bf16[256,256]{1,0:T(8,128)(2,1)}, u32[]{:S(2)}, u32[]{:S(2)}) collective-permute-start(bf16[256,256]{1,0:T(8,128)(2,1)S(1)} %get-tuple-element.10), channel_id=1, source_target_pairs={{0,1},{1,2},{2,3},{3,0},{4,5},{5,6},{6,7},{7,4},{8,9},{9,10},{10,1... | collective-permute-start | bytes 393224 | tf_op jit(solution)/shard_map/ppermute | solution.py:134
  102.4 1.6 copy.37
  104.1 0.2 convert.21
  105.1 15.4 %all-gather.10.cloned.1.call-done = bf16[2,4,12,86,256]{4,0,3,1,2:T(2,128)(2,1)} async-done(((bf16[2,4,12,43,256]{4,0,3,1,2:T(2,128)(2,1)}), bf16[2,4,12,86,256]{4,0,3,1,2:T(2,128)(2,1)}) %all-gather.10.cloned.1.call-update) | async-done | bytes 4227088 | tf_op jit(solution)/shard_map/all_gather | solution.py:124
  120.5 4.8 %copy.40 = bf16[2,4,12,86,256]{4,3,2,1,0:T(8,128)(2,1)} copy(bf16[2,4,12,86,256]{4,0,3,1,2:T(2,128)(2,1)} %all-gather.10.cloned.1.call-done) | data formatting | bytes 8454144 | tf_op jit(solution)/shard_map/all_gather | solution.py:124
  125.3 7.1 %reshape.288 = bf16[8256,256]{1,0:T(8,128)(2,1)} reshape(bf16[2,4,12,86,256]{4,3,2,1,0:T(8,128)(2,1)} %copy.40) | data formatting | bytes 8454144 | tf_op jit(solution)/shard_map/reshape | solution.py:125
  132.4 7.0 %fusion.23 = f32[512,256]{0,1:T(8,128)S(1)} fusion(bf16[512,8192]{1,0:T(8,128)(2,1)} %param.8, bf16[8256,256]{1,0:T(8,128)(2,1)} %reshape.288), kind=kOutput, calls=%fused_computation.26 | convolution fusion | flops 2147483648 | bytes 13107200 | tf_op jit(solution)/shard_map/dot_general | solution.py:165
  139.5 0.6 fusion.32
  140.1 0.1 copy.41
  140.2 1.0 broadcast_in_dim.74
  141.3 4.7 %all-to-all-start = ((bf16[4,512,256]{2,1,0:T(8,128)(2,1)}), bf16[4,512,256]{2,1,0:T(8,128)(2,1)S(1)}, u32[]{:S(2)}, u32[]{:S(2)}) async-start(bf16[4,512,256]{2,1,0:T(8,128)(2,1)} %broadcast_in_dim.74), calls=%async_computation | async-start | bytes 2097152 | tf_op jit(solution)/shard_map/all_to_all | solution.py:170
  146.1 0.2 fusion.38
  146.3 0.3 subtract_convert_fusion
  146.6 0.1 pad_maximum_fusion
  146.7 0.0 collective-permute-done.2
  146.7 0.0 collective-permute-done.1
  146.7 0.0 collective-permute-done
  146.7 1.1 pad_maximum_fusion.1
  147.8 0.6 gather_fusion
  148.4 0.1 broadcast_select_fusion
  148.5 2.7 %bitcast_reduce_fusion = (f32[4,8,128]{2,1,0:T(8,128)S(1)}, f32[4,256,128,8]{2,1,3,0:T(8,128)}) fusion(pred[256]{0:T(512)(128)(4,1)S(1)} %iota_compare_fusion.1, bf16[128,4,8,128]{0,3,2,1:T(8,128)(2,1)S(1)} %bitcast.83, bf16[4,256,256]{2,1,0:T(8,128)(2,1)S(1)} %broadcast_select_fusion), kind=kOutput, calls=%fused_computation.9 | convolution fusion | flops 271577088 | bytes 5521920 | tf_op jit(solution)/shard_map/thgd,hjd->hgtj/dot_general | solution.py:181
  151.2 21.0 %all-to-all-done = bf16[4,512,256]{2,1,0:T(8,128)(2,1)S(1)} async-done(((bf16[4,512,256]{2,1,0:T(8,128)(2,1)}), bf16[4,512,256]{2,1,0:T(8,128)(2,1)S(1)}, u32[]{:S(2)}, u32[]{:S(2)}) %all-to-all-start) | async-done | bytes 1048608 | tf_op jit(solution)/shard_map/all_to_all | solution.py:170
  172.2 0.0 copy-start
  172.2 1.3 fusion
  173.5 0.8 copy-done
  174.4 1.2 fusion.12
  175.6 1.2 fusion.10
  176.7 2.2 %fusion.1 = f32[4,8,128]{2,1,0:T(8,128)S(1)} fusion(f32[4,512,128,8]{2,1,3,0:T(8,128)S(1)} %get-tuple-element.16, f32[4,8,128]{2,1,0:T(8,128)S(1)} %max.16, pred[128,512]{0,1:T(8,128)(4,1)S(1)} %iota_compare_fusion), kind=kLoop, calls=%fused_computation.4 | loop fusion | flops 10481664 | bytes 8486912 | tf_op jit(solution)/shard_map/reduce_sum | solution.py:197
  178.9 2.4 %fusion.14 = bf16[128,4,8,128]{0,3,2,1:T(8,128)(2,1)S(1)} fusion(f32[4,8,128,128]{2,3,1,0:T(8,128)S(1)} %fusion.12, f32[4,512,128,8]{2,1,3,0:T(8,128)S(1)} %get-tuple-element.16, f32[4,8,128]{2,1,0:T(8,128)S(1)} %max.16, pred[128,512]{0,1:T(8,128)(4,1)S(1)} %iota_compare_fusion, f32[128,4,8]{0,2,1:T(8,128)S(1)} %add_bitcast_fusion, ...), kind=kOutput, calls=%fused_computation.19 | convolution fusion | flops 548929536 | bytes 12156928 | tf_op jit(solution)/shard_map/hgtu,hud->hgtd/dot_general | solution.py:203
  181.3 1.3 copy.47
  (15 shorter events, 0.2 us)
Async XLA Ops:
  6.5 81.0 %all-gather.8.cloned.1.call-start = ((), (), s32[]{:S(2)}) async-start(), calls=%async_computation.1 | async-start | bytes 2289664 | tf_op jit(solution)/shard_map/all_gather | solution.py:118
  21.8 98.7 %all-gather.10.cloned.1.call-start = ((), (), s32[]{:S(2)}) async-start(), calls=%async_computation.2 | async-start | bytes 6340608 | tf_op jit(solution)/shard_map/all_gather | solution.py:124
  88.5 58.2 %collective-permute-start.2 = (bf16[256,256]{1,0:T(8,128)(2,1)S(1)}, bf16[256,256]{1,0:T(8,128)(2,1)}, u32[]{:S(2)}, u32[]{:S(2)}) collective-permute-start(bf16[256,256]{1,0:T(8,128)(2,1)S(1)} %get-tuple-element.10), channel_id=1, source_target_pairs={{0,3},{1,0},{2,1},{3,2},{4,7},{5,4},{6,5},{7,6},{8,11},{9,8},{10,9... | collective-permute-start | bytes 393224 | tf_op jit(solution)/shard_map/ppermute | solution.py:134
  93.8 52.8 %collective-permute-start.1 = (bf16[256,256]{1,0:T(8,128)(2,1)S(1)}, bf16[256,256]{1,0:T(8,128)(2,1)}, u32[]{:S(2)}, u32[]{:S(2)}) collective-permute-start(bf16[256,256]{1,0:T(8,128)(2,1)S(1)} %get-tuple-element.10), channel_id=1, source_target_pairs={{0,2},{1,3},{2,0},{3,1},{4,6},{5,7},{6,4},{7,5},{8,10},{9,11},{10,... | collective-permute-start | bytes 393224 | tf_op jit(solution)/shard_map/ppermute | solution.py:134
  97.8 48.9 %collective-permute-start = (bf16[256,256]{1,0:T(8,128)(2,1)S(1)}, bf16[256,256]{1,0:T(8,128)(2,1)}, u32[]{:S(2)}, u32[]{:S(2)}) collective-permute-start(bf16[256,256]{1,0:T(8,128)(2,1)S(1)} %get-tuple-element.10), channel_id=1, source_target_pairs={{0,1},{1,2},{2,3},{3,0},{4,5},{5,6},{6,7},{7,4},{8,9},{9,10},{10,1... | collective-permute-start | bytes 393224 | tf_op jit(solution)/shard_map/ppermute | solution.py:134
  141.3 30.9 %all-to-all-start = ((bf16[4,512,256]{2,1,0:T(8,128)(2,1)}), bf16[4,512,256]{2,1,0:T(8,128)(2,1)S(1)}, u32[]{:S(2)}, u32[]{:S(2)}) async-start(bf16[4,512,256]{2,1,0:T(8,128)(2,1)} %broadcast_in_dim.74), calls=%async_computation | async-start | bytes 2097152 | tf_op jit(solution)/shard_map/all_to_all | solution.py:170
  172.2 2.2 %copy-start = (f32[4,256,128,8]{2,1,3,0:T(8,128)S(1)}, f32[4,256,128,8]{2,1,3,0:T(8,128)}, u32[]{:S(2)}) copy-start(f32[4,256,128,8]{2,1,3,0:T(8,128)} %get-tuple-element.14) | copy-start | bytes 12582916
Sparse Core Ops, SparseCore 0:
  22.0 65.5 all-gather.7
  90.0 30.5 all-gather.9

commit v11 on v10

--- a/solution.py
+++ b/solution.py
@@ -135,6 +135,25 @@
     stacked = jnp.stack(pieces)
     order = (here - jnp.arange(count, dtype=jnp.int32)) % count
     return jnp.take(stacked, order, axis=0)
+
+
+def exchange_causal(block, query_rows):
+    count = lax.axis_size("sp")
+    here = lax.axis_index("sp")
+    split = block.shape[0] // 2
+    head = block[:split]
+    repeated = jnp.broadcast_to(head[None], (count,) + head.shape)
+    head_all = lax.all_to_all(repeated, "sp", split_axis=0, concat_axis=0, tiled=True)
+    tail = block[split:]
+    readers = [j for j in range(count) if query_rows * (j + 1) > split]
+    pieces = [tail]
+    for shift in range(1, count):
+        pairs = [((j - shift) % count, j) for j in readers]
+        pieces.append(lax.ppermute(tail, "sp", perm=pairs))
+    stacked = jnp.stack(pieces)
+    order = (here - jnp.arange(count, dtype=jnp.int32)) % count
+    tail_all = jnp.take(stacked, order, axis=0)
+    return jnp.concatenate([head_all, tail_all], axis=1)
 
 
 def per_device(
@@ -166,8 +185,7 @@
     new_keys = rotate(kv_sum[:, :kv_cols], cosine_table, sine_table, kv_local).astype(jnp.bfloat16)
     new_values = kv_sum[:, kv_cols:].astype(jnp.bfloat16)
     new_kv = jnp.concatenate([new_keys, new_values], axis=1)
-    repeated = jnp.broadcast_to(new_kv[None], (lax.axis_size("sp"),) + new_kv.shape)
-    new_all = lax.all_to_all(repeated, "sp", split_axis=0, concat_axis=0, tiled=True)
+    new_all = exchange_causal(new_kv, query_rows)
 
     rotated_q = rotate(queries.astype(jnp.float32), query_cosine, query_sine, HQ).astype(
         jnp.bfloat16

time: 190 us -> 188 us (0.989)
  waiting for transfers between devices: 102 us -> 89.6 us
  starting transfers between devices: 18 us -> 27.5 us
    all_to_all x1, waiting for transfers between devices: 21 us -> 0.01 us  [exchange_causal(): lax.all_to_all(repeated, 'sp', split_axis=0, concat_axis=0, tiled=True)]
    ppermute x0 -> x3, waiting for transfers between devices: none -> 10.8 us  [exchange_causal(): pieces.append(lax.ppermute(tail, 'sp', perm=pairs))]
    ppermute x0 -> x3, starting transfers between devices: none -> 9.42 us  [exchange_causal(): pieces.append(lax.ppermute(tail, 'sp', perm=pairs))]
    all_gather x1, waiting for transfers between devices: 15.4 us -> 13 us  [gather_weights(): lax.all_gather(gathered, last, axis=FSDP_AXES.index(last), tiled=False)]
  transfers between devices with their start and end apart: 6 -> 9, of which waited for: 3 -> 3; matrix products, arithmetic and copies ran while one was open for 15% -> 5% of each run, Pallas kernels for 0% -> 0%
where the time goes in v11:
time: 188 us; the launch traced here: 187 us
  waiting for transfers between devices  89.6 us (48%)
  starting transfers between devices  27.5 us (15%)
  local copies, waits for them, and re-layouts  18.4 us (10%)
  between operations  15 us (8%)
  matrix products  14.8 us (8%)
  blocking collectives  13.7 us (7%)
  other arithmetic  7.85 us (4%)
    all_gather x1, waiting for transfers between devices, gather_weights(): gathered = lax.all_gather(gathered, stage, axis=0, tiled=False)  65.7 us
    all_gather x2, blocking collectives, gather_weights(): gathered = lax.all_gather(gathered, stage, axis=0, tiled=False)  13.7 us
    ppermute x3, starting transfers between devices, gather_sp(): pieces.append(lax.ppermute(block, 'sp', perm=pairs))  13.3 us
    all_gather x1, waiting for transfers between devices, gather_weights(): lax.all_gather(gathered, last, axis=FSDP_AXES.index(last), tiled=False)  13 us
    ppermute x3, waiting for transfers between devices, exchange_causal(): pieces.append(lax.ppermute(tail, 'sp', perm=pairs))  10.8 us
    ppermute x3, starting transfers between devices, exchange_causal(): pieces.append(lax.ppermute(tail, 'sp', perm=pairs))  9.42 us
    reshape x1, local copies, waits for them, and re-layouts, gather_weights(): return gathered.reshape(-1, shard.shape[1])  7.07 us
    dot_general x1, matrix products, per_device(): jnp.dot(hidden_rows, whole_kv[:model_width], preferred_element_type=jnp.f...  7.03 us
  transfers between devices with their start and end apart: 9, of which 3 were waited for; matrix products, arithmetic and copies ran while one was open for 5% of the time, Pallas kernels for 0%

profile of v11, /device:TPU:1, one launch (start us, length us, event | category | flops | bytes accessed | tf_op | source)
XLA Modules:
  0.0 186.8 jit_solution(16936634738965949271)
XLA Ops:
  6.5 0.7 maximum_bitcast_fusion
  7.3 4.0 %all-gather.4 = bf16[2,43,256]{2,1,0:T(8,128)(2,1)S(1)} all-gather(bf16[1,43,256]{2,1,0:T(8,128)(2,1)S(1)} %maximum_bitcast_fusion), channel_id=2, replica_groups=mesh['ylo'=2,'x'=4,'z'=12,'core'=2,'sp'=4] {'ylo'}, dimensions={0}, use_global_device_ids=true | all-gather | bytes 66048 | tf_op jit(solution)/shard_map/all_gather | solution.py:118
  11.2 9.8 %all-gather.1 = bf16[8,43,256]{2,1,0:T(8,128)(2,1)S(1)} all-gather(bf16[2,43,256]{2,1,0:T(8,128)(2,1)S(1)} %all-gather.4), channel_id=3, replica_groups=mesh['ylo'=2,'x'=4,'z'=12,'core'=2,'sp'=4] {'x'}, dimensions={0}, use_global_device_ids=true | all-gather | bytes 220160 | tf_op jit(solution)/shard_map/all_gather | solution.py:118
  21.0 0.8 copy.36
  21.8 0.0 all-gather.8.cloned.1.call-update
  21.8 0.0 all-gather.10.cloned.1.call-start
  21.9 65.7 %all-gather.8.cloned.1.call-done = bf16[48,2,43,256]{3,1,2,0:T(2,128)(2,1)} async-done(((bf16[4,2,43,256]{3,1,2,0:T(2,128)(2,1)}), bf16[48,2,43,256]{3,1,2,0:T(2,128)(2,1)}) %all-gather.8.cloned.1.call-update) | async-done | bytes 2113552 | tf_op jit(solution)/shard_map/all_gather | solution.py:118
  87.6 0.0 all-gather.10.cloned.1.call-update
  87.6 0.9 fusion.56
  88.5 5.3 %collective-permute-start.2 = (bf16[256,256]{1,0:T(8,128)(2,1)S(1)}, bf16[256,256]{1,0:T(8,128)(2,1)}, u32[]{:S(2)}, u32[]{:S(2)}) collective-permute-start(bf16[256,256]{1,0:T(8,128)(2,1)S(1)} %get-tuple-element.13), channel_id=1, source_target_pairs={{0,3},{1,0},{2,1},{3,2},{4,7},{5,4},{6,5},{7,6},{8,11},{9,8},{10,9... | collective-permute-start | bytes 393224 | tf_op jit(solution)/shard_map/ppermute | solution.py:134
  93.8 3.9 %collective-permute-start.1 = (bf16[256,256]{1,0:T(8,128)(2,1)S(1)}, bf16[256,256]{1,0:T(8,128)(2,1)}, u32[]{:S(2)}, u32[]{:S(2)}) collective-permute-start(bf16[256,256]{1,0:T(8,128)(2,1)S(1)} %get-tuple-element.13), channel_id=1, source_target_pairs={{0,2},{1,3},{2,0},{3,1},{4,6},{5,7},{6,4},{7,5},{8,10},{9,11},{10,... | collective-permute-start | bytes 393224 | tf_op jit(solution)/shard_map/ppermute | solution.py:134
  97.8 4.0 %collective-permute-start = (bf16[256,256]{1,0:T(8,128)(2,1)S(1)}, bf16[256,256]{1,0:T(8,128)(2,1)}, u32[]{:S(2)}, u32[]{:S(2)}) collective-permute-start(bf16[256,256]{1,0:T(8,128)(2,1)S(1)} %get-tuple-element.13), channel_id=1, source_target_pairs={{0,1},{1,2},{2,3},{3,0},{4,5},{5,6},{6,7},{7,4},{8,9},{9,10},{10,1... | collective-permute-start | bytes 393224 | tf_op jit(solution)/shard_map/ppermute | solution.py:134
  102.4 1.6 copy.34
  104.1 0.2 convert.21
  105.2 0.2 fusion.45
  105.4 0.3 subtract_convert_fusion
  105.7 0.1 pad_maximum_fusion
  105.8 0.0 collective-permute-done.2
  105.8 0.0 collective-permute-done.1
  105.8 0.0 collective-permute-done
  105.8 1.1 pad_maximum_fusion.2
  106.9 0.6 gather_fusion
  107.5 13.0 %all-gather.10.cloned.1.call-done = bf16[2,4,12,86,256]{4,0,3,1,2:T(2,128)(2,1)} async-done(((bf16[2,4,12,43,256]{4,0,3,1,2:T(2,128)(2,1)}), bf16[2,4,12,86,256]{4,0,3,1,2:T(2,128)(2,1)}) %all-gather.10.cloned.1.call-update) | async-done | bytes 4227088 | tf_op jit(solution)/shard_map/all_gather | solution.py:124
  120.5 4.8 %copy.37 = bf16[2,4,12,86,256]{4,3,2,1,0:T(8,128)(2,1)} copy(bf16[2,4,12,86,256]{4,0,3,1,2:T(2,128)(2,1)} %all-gather.10.cloned.1.call-done) | data formatting | bytes 8454144 | tf_op jit(solution)/shard_map/all_gather | solution.py:124
  125.3 7.1 %reshape.239 = bf16[8256,256]{1,0:T(8,128)(2,1)} reshape(bf16[2,4,12,86,256]{4,3,2,1,0:T(8,128)(2,1)} %copy.37) | data formatting | bytes 8454144 | tf_op jit(solution)/shard_map/reshape | solution.py:125
  132.4 7.0 %fusion.23 = f32[512,256]{0,1:T(8,128)S(1)} fusion(bf16[512,8192]{1,0:T(8,128)(2,1)} %param.10, bf16[8256,256]{1,0:T(8,128)(2,1)} %reshape.239), kind=kOutput, calls=%fused_computation.27 | convolution fusion | flops 2147483648 | bytes 13107200 | tf_op jit(solution)/shard_map/dot_general | solution.py:184
  139.5 0.6 fusion.38
  140.1 0.8 broadcast_in_dim.71
  140.9 4.7 %all-to-all-start = ((bf16[4,256,256]{1,2,0:T(8,128)(2,1)}), bf16[4,256,256]{1,2,0:T(8,128)(2,1)S(1)}, u32[]{:S(2)}, u32[]{:S(2)}) async-start(bf16[4,256,256]{1,2,0:T(8,128)(2,1)} %broadcast_in_dim.71), calls=%async_computation | async-start | bytes 1048576 | tf_op jit(solution)/shard_map/all_to_all | solution.py:146
  145.7 0.1 broadcast_select_fusion.1
  145.8 5.5 %collective-permute-start.5 = (bf16[256,256]{0,1:T(8,128)(2,1)S(1)}, bf16[256,256]{0,1:T(8,128)(2,1)S(1)}, u32[]{:S(2)}, u32[]{:S(2)}) collective-permute-start(bf16[256,256]{0,1:T(8,128)(2,1)S(1)} %get-tuple-element.10), channel_id=1, source_target_pairs={{3,2},{0,3},{7,6},{4,7},{11,10},{8,11},{15,14},{12,15},{19,18},{16... | collective-permute-start | bytes 393224 | tf_op jit(solution)/shard_map/ppermute | solution.py:152
  151.3 3.1 %collective-permute-start.4 = (bf16[256,256]{0,1:T(8,128)(2,1)S(1)}, bf16[256,256]{0,1:T(8,128)(2,1)S(1)}, u32[]{:S(2)}, u32[]{:S(2)}) collective-permute-start(bf16[256,256]{0,1:T(8,128)(2,1)S(1)} %get-tuple-element.10), channel_id=1, source_target_pairs={{0,2},{1,3},{4,6},{5,7},{8,10},{9,11},{12,14},{13,15},{16,18},{17,... | collective-permute-start | bytes 393224 | tf_op jit(solution)/shard_map/ppermute | solution.py:152
  154.4 0.8 collective-permute-start.3
  155.2 2.7 %bitcast_reduce_fusion = (f32[4,8,128]{2,1,0:T(8,128)S(1)}, f32[4,256,128,8]{2,1,3,0:T(8,128)}) fusion(pred[256]{0:T(512)(128)(4,1)S(1)} %iota_compare_fusion.1, bf16[128,4,8,128]{0,3,2,1:T(8,128)(2,1)S(1)} %bitcast.85, bf16[4,256,256]{2,1,0:T(8,128)(2,1)S(1)} %broadcast_select_fusion.1), kind=kOutput, calls=%fused_computation.10 | convolution fusion | flops 271577088 | bytes 5521920 | tf_op jit(solution)/shard_map/thgd,hjd->hgtj/dot_general | solution.py:199
  157.9 10.8 %collective-permute-done.5 = bf16[256,256]{0,1:T(8,128)(2,1)S(1)} collective-permute-done((bf16[256,256]{0,1:T(8,128)(2,1)S(1)}, bf16[256,256]{0,1:T(8,128)(2,1)S(1)}, u32[]{:S(2)}, u32[]{:S(2)}) %collective-permute-start.5) | collective-permute-done | bytes 131104 | tf_op jit(solution)/shard_map/ppermute | solution.py:152
  168.7 0.0 collective-permute-done.4
  168.7 0.0 collective-permute-done.3
  168.7 0.1 pad_maximum_fusion.3
  168.8 0.6 gather_fusion.1
  169.4 0.1 broadcast_select_fusion
  169.5 0.0 all-to-all-done
  169.5 1.4 fusion
  171.0 0.7 copy-done
  171.7 1.2 fusion.12
  172.9 1.1 fusion.10
  174.0 2.1 %fusion.1 = f32[4,8,128]{2,1,0:T(8,128)S(1)} fusion(f32[4,512,128,8]{2,1,3,0:T(8,128)S(1)} %get-tuple-element.19, f32[4,8,128]{2,1,0:T(8,128)S(1)} %max.16, pred[128,512]{0,1:T(8,128)(4,1)S(1)} %iota_compare_fusion), kind=kLoop, calls=%fused_computation.5 | loop fusion | flops 10481664 | bytes 8486912 | tf_op jit(solution)/shard_map/reduce_sum | solution.py:215
  176.2 2.5 %fusion.14 = bf16[128,4,8,128]{0,3,2,1:T(8,128)(2,1)S(1)} fusion(f32[4,8,128,128]{2,3,1,0:T(8,128)S(1)} %fusion.12, f32[4,512,128,8]{2,1,3,0:T(8,128)S(1)} %get-tuple-element.19, f32[4,8,128]{2,1,0:T(8,128)S(1)} %max.16, pred[128,512]{0,1:T(8,128)(4,1)S(1)} %iota_compare_fusion, f32[128,4,8]{0,2,1:T(8,128)S(1)} %add_bitcast_fusion, ...), kind=kOutput, calls=%fused_computation.20 | convolution fusion | flops 549978112 | bytes 12681216 | tf_op jit(solution)/shard_map/hgtu,hud->hgtd/dot_general | solution.py:221
  178.7 1.3 copy.43
  (17 shorter events, 0.2 us)
Async XLA Ops:
  6.5 81.0 %all-gather.8.cloned.1.call-start = ((), (), s32[]{:S(2)}) async-start(), calls=%async_computation.1 | async-start | bytes 2289664 | tf_op jit(solution)/shard_map/all_gather | solution.py:118
  21.8 98.7 %all-gather.10.cloned.1.call-start = ((), (), s32[]{:S(2)}) async-start(), calls=%async_computation.2 | async-start | bytes 6340608 | tf_op jit(solution)/shard_map/all_gather | solution.py:124
  88.5 17.3 %collective-permute-start.2 = (bf16[256,256]{1,0:T(8,128)(2,1)S(1)}, bf16[256,256]{1,0:T(8,128)(2,1)}, u32[]{:S(2)}, u32[]{:S(2)}) collective-permute-start(bf16[256,256]{1,0:T(8,128)(2,1)S(1)} %get-tuple-element.13), channel_id=1, source_target_pairs={{0,3},{1,0},{2,1},{3,2},{4,7},{5,4},{6,5},{7,6},{8,11},{9,8},{10,9... | collective-permute-start | bytes 393224 | tf_op jit(solution)/shard_map/ppermute | solution.py:134
  93.8 11.9 %collective-permute-start.1 = (bf16[256,256]{1,0:T(8,128)(2,1)S(1)}, bf16[256,256]{1,0:T(8,128)(2,1)}, u32[]{:S(2)}, u32[]{:S(2)}) collective-permute-start(bf16[256,256]{1,0:T(8,128)(2,1)S(1)} %get-tuple-element.13), channel_id=1, source_target_pairs={{0,2},{1,3},{2,0},{3,1},{4,6},{5,7},{6,4},{7,5},{8,10},{9,11},{10,... | collective-permute-start | bytes 393224 | tf_op jit(solution)/shard_map/ppermute | solution.py:134
  97.8 8.0 %collective-permute-start = (bf16[256,256]{1,0:T(8,128)(2,1)S(1)}, bf16[256,256]{1,0:T(8,128)(2,1)}, u32[]{:S(2)}, u32[]{:S(2)}) collective-permute-start(bf16[256,256]{1,0:T(8,128)(2,1)S(1)} %get-tuple-element.13), channel_id=1, source_target_pairs={{0,1},{1,2},{2,3},{3,0},{4,5},{5,6},{6,7},{7,4},{8,9},{9,10},{10,1... | collective-permute-start | bytes 393224 | tf_op jit(solution)/shard_map/ppermute | solution.py:134
  140.9 28.6 %all-to-all-start = ((bf16[4,256,256]{1,2,0:T(8,128)(2,1)}), bf16[4,256,256]{1,2,0:T(8,128)(2,1)S(1)}, u32[]{:S(2)}, u32[]{:S(2)}) async-start(bf16[4,256,256]{1,2,0:T(8,128)(2,1)} %broadcast_in_dim.71), calls=%async_computation | async-start | bytes 1048576 | tf_op jit(solution)/shard_map/all_to_all | solution.py:146
  145.8 22.9 %collective-permute-start.5 = (bf16[256,256]{0,1:T(8,128)(2,1)S(1)}, bf16[256,256]{0,1:T(8,128)(2,1)S(1)}, u32[]{:S(2)}, u32[]{:S(2)}) collective-permute-start(bf16[256,256]{0,1:T(8,128)(2,1)S(1)} %get-tuple-element.10), channel_id=1, source_target_pairs={{3,2},{0,3},{7,6},{4,7},{11,10},{8,11},{15,14},{12,15},{19,18},{16... | collective-permute-start | bytes 393224 | tf_op jit(solution)/shard_map/ppermute | solution.py:152
  151.3 17.5 %collective-permute-start.4 = (bf16[256,256]{0,1:T(8,128)(2,1)S(1)}, bf16[256,256]{0,1:T(8,128)(2,1)S(1)}, u32[]{:S(2)}, u32[]{:S(2)}) collective-permute-start(bf16[256,256]{0,1:T(8,128)(2,1)S(1)} %get-tuple-element.10), channel_id=1, source_target_pairs={{0,2},{1,3},{4,6},{5,7},{8,10},{9,11},{12,14},{13,15},{16,18},{17,... | collective-permute-start | bytes 393224 | tf_op jit(solution)/shard_map/ppermute | solution.py:152
  154.4 14.4 %collective-permute-start.3 = (bf16[256,256]{0,1:T(8,128)(2,1)S(1)}, bf16[256,256]{0,1:T(8,128)(2,1)S(1)}, u32[]{:S(2)}, u32[]{:S(2)}) collective-permute-start(bf16[256,256]{0,1:T(8,128)(2,1)S(1)} %get-tuple-element.10), channel_id=1, source_target_pairs={{1,2},{2,3},{5,6},{6,7},{9,10},{10,11},{13,14},{14,15},{17,18},{18... | collective-permute-start | bytes 393224 | tf_op jit(solution)/shard_map/ppermute | solution.py:152
  169.5 2.2 %copy-start = (f32[4,256,128,8]{2,1,3,0:T(8,128)S(1)}, f32[4,256,128,8]{2,1,3,0:T(8,128)}, u32[]{:S(2)}) copy-start(f32[4,256,128,8]{2,1,3,0:T(8,128)} %get-tuple-element.17) | copy-start | bytes 12582916
Sparse Core Ops, SparseCore 0:
  22.0 65.5 all-gather.7
  90.0 30.5 all-gather.9

commit v12 on v11

--- a/solution.py
+++ b/solution.py
@@ -109,7 +109,7 @@
 
 FSDP_PARTS = (("ylo", 2), ("x", 4), ("z", 12), ("core", 2))
 FSDP_AXES = tuple(name for name, _ in FSDP_PARTS)
-GATHER_STAGES = (("ylo",), ("x",), ("z",), ("core",))
+GATHER_STAGES = (("ylo",), ("z",), ("x",), ("core",))
 
 
 def gather_weights(shard):

time: 188 us -> 183 us (0.973)
  waiting for transfers between devices: 89.6 us -> 59.7 us
  blocking collectives: 13.7 us -> 34.9 us
  local copies, waits for them, and re-layouts: 18.4 us -> 23.6 us
    all_gather x1, waiting for transfers between devices: 65.7 us -> 40 us  [gather_weights(): gathered = lax.all_gather(gathered, stage, axis=0, tiled=False)]
    all_gather x2, blocking collectives: 13.7 us -> 34.9 us  [gather_weights(): gathered = lax.all_gather(gathered, stage, axis=0, tiled=False)]
    all_gather x1, waiting for transfers between devices: 13 us -> 6.89 us  [gather_weights(): lax.all_gather(gathered, last, axis=FSDP_AXES.index(last), tiled=False)]
    all_gather x1 -> x2, local copies, waits for them, and re-layouts: 0.81 us -> 5.27 us  [gather_weights(): gathered = lax.all_gather(gathered, stage, axis=0, tiled=False)]
    ppermute x3, waiting for transfers between devices: 0.01 us -> 1.98 us  [gather_sp(): pieces.append(lax.ppermute(block, 'sp', perm=pairs))]
  transfers between devices with their start and end apart: 9 -> 9, of which waited for: 3 -> 4; matrix products, arithmetic and copies ran while one was open for 5% -> 4% of each run, Pallas kernels for 0% -> 0%
where the time goes in v12:
time: 183 us
  waiting for transfers between devices  59.7 us (33%)
  blocking collectives  34.9 us (19%)
  starting transfers between devices  27.5 us (15%)
  local copies, waits for them, and re-layouts  23.6 us (13%)
  between operations  15 us (8%)
  matrix products  14.8 us (8%)
  other arithmetic  7.16 us (4%)
    all_gather x1, waiting for transfers between devices, gather_weights(): gathered = lax.all_gather(gathered, stage, axis=0, tiled=False)  40 us
    all_gather x2, blocking collectives, gather_weights(): gathered = lax.all_gather(gathered, stage, axis=0, tiled=False)  34.9 us
    ppermute x3, starting transfers between devices, gather_sp(): pieces.append(lax.ppermute(block, 'sp', perm=pairs))  13.3 us
    ppermute x3, waiting for transfers between devices, exchange_causal(): pieces.append(lax.ppermute(tail, 'sp', perm=pairs))  10.8 us
    ppermute x3, starting transfers between devices, exchange_causal(): pieces.append(lax.ppermute(tail, 'sp', perm=pairs))  9.42 us
    reshape x1, local copies, waits for them, and re-layouts, gather_weights(): return gathered.reshape(-1, shard.shape[1])  7.04 us
    dot_general x1, matrix products, per_device(): jnp.dot(hidden_rows, whole_kv[:model_width], preferred_element_type=jnp.f...  7.04 us
    all_gather x1, waiting for transfers between devices, gather_weights(): lax.all_gather(gathered, last, axis=FSDP_AXES.index(last), tiled=False)  6.89 us
  transfers between devices with their start and end apart: 9, of which 4 were waited for; matrix products, arithmetic and copies ran while one was open for 4% of the time, Pallas kernels for 0%

profile of v12, /device:TPU:1, one launch (start us, length us, event | category | flops | bytes accessed | tf_op | source)
XLA Modules:
  0.0 182.7 jit_solution(3559550821366507725)
XLA Ops:
  6.5 0.7 maximum_bitcast_fusion
  7.3 4.0 %all-gather.4 = bf16[2,43,256]{2,1,0:T(8,128)(2,1)S(1)} all-gather(bf16[1,43,256]{2,1,0:T(8,128)(2,1)S(1)} %maximum_bitcast_fusion), channel_id=2, replica_groups=mesh['ylo'=2,'x'=4,'z'=12,'core'=2,'sp'=4] {'ylo'}, dimensions={0}, use_global_device_ids=true | all-gather | bytes 66048 | tf_op jit(solution)/shard_map/all_gather | solution.py:118
  11.3 30.9 %all-gather.1 = bf16[24,43,256]{2,1,0:T(8,128)(2,1)S(1)} all-gather(bf16[2,43,256]{2,1,0:T(8,128)(2,1)S(1)} %all-gather.4), channel_id=3, replica_groups=mesh['ylo'=2,'x'=4,'z'=12,'core'=2,'sp'=4] {'z'}, dimensions={0}, use_global_device_ids=true | all-gather | bytes 572416 | tf_op jit(solution)/shard_map/all_gather | solution.py:118
  42.2 1.2 copy.27
  43.4 0.0 all-gather.8.cloned.1.call-update
  43.4 0.0 all-gather.10.cloned.1.call-start
  43.4 40.0 %all-gather.8.cloned.1.call-done = bf16[48,2,43,256]{3,1,2,0:T(2,128)(2,1)} async-done(((bf16[12,2,43,256]{3,1,2,0:T(2,128)(2,1)}), bf16[48,2,43,256]{3,1,2,0:T(2,128)(2,1)}) %all-gather.8.cloned.1.call-update) | async-done | bytes 2113552 | tf_op jit(solution)/shard_map/all_gather | solution.py:118
  83.4 4.1 %copy.49 = bf16[4,12,2,43,256]{4,0,1,2,3:T(4,128)(2,1)} copy(bf16[4,12,2,43,256]{4,2,3,1,0:T(2,128)(2,1)} %bitcast.91) | data formatting | bytes 4227072 | tf_op jit(solution)/shard_map/all_gather | solution.py:118
  87.5 0.0 all-gather.10.cloned.1.call-update
  87.5 5.3 %collective-permute-start.2 = (bf16[256,256]{1,0:T(8,128)(2,1)S(1)}, bf16[256,256]{1,0:T(8,128)(2,1)}, u32[]{:S(2)}, u32[]{:S(2)}) collective-permute-start(bf16[256,256]{1,0:T(8,128)(2,1)S(1)} %get-tuple-element.13), channel_id=1, source_target_pairs={{0,3},{1,0},{2,1},{3,2},{4,7},{5,4},{6,5},{7,6},{8,11},{9,8},{10,9... | collective-permute-start | bytes 393224 | tf_op jit(solution)/shard_map/ppermute | solution.py:134
  92.9 3.9 %collective-permute-start.1 = (bf16[256,256]{1,0:T(8,128)(2,1)S(1)}, bf16[256,256]{1,0:T(8,128)(2,1)}, u32[]{:S(2)}, u32[]{:S(2)}) collective-permute-start(bf16[256,256]{1,0:T(8,128)(2,1)S(1)} %get-tuple-element.13), channel_id=1, source_target_pairs={{0,2},{1,3},{2,0},{3,1},{4,6},{5,7},{6,4},{7,5},{8,10},{9,11},{10,... | collective-permute-start | bytes 393224 | tf_op jit(solution)/shard_map/ppermute | solution.py:134
  96.8 4.0 %collective-permute-start = (bf16[256,256]{1,0:T(8,128)(2,1)S(1)}, bf16[256,256]{1,0:T(8,128)(2,1)}, u32[]{:S(2)}, u32[]{:S(2)}) collective-permute-start(bf16[256,256]{1,0:T(8,128)(2,1)S(1)} %get-tuple-element.13), channel_id=1, source_target_pairs={{0,1},{1,2},{2,3},{3,0},{4,5},{5,6},{6,7},{7,4},{8,9},{9,10},{10,1... | collective-permute-start | bytes 393224 | tf_op jit(solution)/shard_map/ppermute | solution.py:134
  101.5 0.7 copy.25
  102.2 0.2 convert.21
  103.3 0.2 fusion.45
  103.5 0.3 subtract_convert_fusion
  103.8 0.1 pad_maximum_fusion
  103.9 0.0 collective-permute-done.2
  103.9 0.0 collective-permute-done.1
  103.9 2.0 %collective-permute-done = bf16[256,256]{1,0:T(8,128)(2,1)} collective-permute-done((bf16[256,256]{1,0:T(8,128)(2,1)S(1)}, bf16[256,256]{1,0:T(8,128)(2,1)}, u32[]{:S(2)}, u32[]{:S(2)}) %collective-permute-start) | collective-permute-done | bytes 131104 | tf_op jit(solution)/shard_map/ppermute | solution.py:134
  105.9 1.2 pad_maximum_fusion.2
  107.1 0.6 gather_fusion
  107.6 6.9 %all-gather.10.cloned.1.call-done = bf16[2,4,12,86,256]{4,1,2,0,3:T(4,128)(2,1)} async-done(((bf16[2,4,12,43,256]{4,1,2,0,3:T(4,128)(2,1)}), bf16[2,4,12,86,256]{4,1,2,0,3:T(4,128)(2,1)}) %all-gather.10.cloned.1.call-update) | async-done | bytes 4227088 | tf_op jit(solution)/shard_map/all_gather | solution.py:124
  114.5 6.6 %copy.29 = bf16[2,4,12,86,256]{4,3,2,1,0:T(8,128)(2,1)} copy(bf16[2,4,12,86,256]{4,1,2,0,3:T(4,128)(2,1)} %all-gather.10.cloned.1.call-done) | data formatting | bytes 8454144 | tf_op jit(solution)/shard_map/all_gather | solution.py:124
  121.1 7.0 %reshape.239 = bf16[8256,256]{1,0:T(8,128)(2,1)} reshape(bf16[2,4,12,86,256]{4,3,2,1,0:T(8,128)(2,1)} %copy.29) | data formatting | bytes 8454144 | tf_op jit(solution)/shard_map/reshape | solution.py:125
  128.1 7.0 %fusion.23 = f32[512,256]{0,1:T(8,128)S(1)} fusion(bf16[512,8192]{1,0:T(8,128)(2,1)} %param.10, bf16[8256,256]{1,0:T(8,128)(2,1)} %reshape.239), kind=kOutput, calls=%fused_computation.28 | convolution fusion | flops 2147483648 | bytes 13107200 | tf_op jit(solution)/shard_map/dot_general | solution.py:184
  135.2 0.6 fusion.38
  135.9 0.8 broadcast_in_dim.71
  136.7 4.7 %all-to-all-start = ((bf16[4,256,256]{1,2,0:T(8,128)(2,1)}), bf16[4,256,256]{1,2,0:T(8,128)(2,1)S(1)}, u32[]{:S(2)}, u32[]{:S(2)}) async-start(bf16[4,256,256]{1,2,0:T(8,128)(2,1)} %broadcast_in_dim.71), calls=%async_computation | async-start | bytes 1048576 | tf_op jit(solution)/shard_map/all_to_all | solution.py:146
  141.4 0.1 broadcast_select_fusion.1
  141.5 5.5 %collective-permute-start.5 = (bf16[256,256]{0,1:T(8,128)(2,1)S(1)}, bf16[256,256]{0,1:T(8,128)(2,1)S(1)}, u32[]{:S(2)}, u32[]{:S(2)}) collective-permute-start(bf16[256,256]{0,1:T(8,128)(2,1)S(1)} %get-tuple-element.10), channel_id=1, source_target_pairs={{3,2},{0,3},{7,6},{4,7},{11,10},{8,11},{15,14},{12,15},{19,18},{16... | collective-permute-start | bytes 393224 | tf_op jit(solution)/shard_map/ppermute | solution.py:152
  147.0 3.1 %collective-permute-start.4 = (bf16[256,256]{0,1:T(8,128)(2,1)S(1)}, bf16[256,256]{0,1:T(8,128)(2,1)S(1)}, u32[]{:S(2)}, u32[]{:S(2)}) collective-permute-start(bf16[256,256]{0,1:T(8,128)(2,1)S(1)} %get-tuple-element.10), channel_id=1, source_target_pairs={{0,2},{1,3},{4,6},{5,7},{8,10},{9,11},{12,14},{13,15},{16,18},{17,... | collective-permute-start | bytes 393224 | tf_op jit(solution)/shard_map/ppermute | solution.py:152
  150.1 0.8 collective-permute-start.3
  151.0 2.7 %bitcast_reduce_fusion = (f32[4,8,128]{2,1,0:T(8,128)S(1)}, f32[4,256,128,8]{2,1,3,0:T(8,128)}) fusion(pred[256]{0:T(512)(128)(4,1)S(1)} %iota_compare_fusion.1, bf16[128,4,8,128]{0,3,2,1:T(8,128)(2,1)S(1)} %bitcast.86, bf16[4,256,256]{2,1,0:T(8,128)(2,1)S(1)} %broadcast_select_fusion.1), kind=kOutput, calls=%fused_computation.10 | convolution fusion | flops 271577088 | bytes 5521920 | tf_op jit(solution)/shard_map/thgd,hjd->hgtj/dot_general | solution.py:199
  153.7 10.8 %collective-permute-done.5 = bf16[256,256]{0,1:T(8,128)(2,1)S(1)} collective-permute-done((bf16[256,256]{0,1:T(8,128)(2,1)S(1)}, bf16[256,256]{0,1:T(8,128)(2,1)S(1)}, u32[]{:S(2)}, u32[]{:S(2)}) %collective-permute-start.5) | collective-permute-done | bytes 131104 | tf_op jit(solution)/shard_map/ppermute | solution.py:152
  164.5 0.0 collective-permute-done.4
  164.5 0.0 collective-permute-done.3
  164.5 0.1 pad_maximum_fusion.3
  164.6 0.6 gather_fusion.1
  165.2 0.1 broadcast_select_fusion
  165.3 0.0 all-to-all-done
  165.3 1.4 fusion
  166.7 0.7 copy-done
  167.5 1.2 fusion.12
  168.7 1.2 fusion.10
  169.8 2.2 %fusion.1 = f32[4,8,128]{2,1,0:T(8,128)S(1)} fusion(f32[4,512,128,8]{2,1,3,0:T(8,128)S(1)} %get-tuple-element.19, f32[4,8,128]{2,1,0:T(8,128)S(1)} %max.16, pred[128,512]{0,1:T(8,128)(4,1)S(1)} %iota_compare_fusion), kind=kLoop, calls=%fused_computation.5 | loop fusion | flops 10481664 | bytes 8486912 | tf_op jit(solution)/shard_map/reduce_sum | solution.py:215
  172.0 2.5 %fusion.14 = bf16[128,4,8,128]{0,3,2,1:T(8,128)(2,1)S(1)} fusion(f32[4,8,128,128]{2,3,1,0:T(8,128)S(1)} %fusion.12, f32[4,512,128,8]{2,1,3,0:T(8,128)S(1)} %get-tuple-element.19, f32[4,8,128]{2,1,0:T(8,128)S(1)} %max.16, pred[128,512]{0,1:T(8,128)(4,1)S(1)} %iota_compare_fusion, f32[128,4,8]{0,2,1:T(8,128)S(1)} %add_bitcast_fusion, ...), kind=kOutput, calls=%fused_computation.21 | convolution fusion | flops 549978112 | bytes 12681216 | tf_op jit(solution)/shard_map/hgtu,hud->hgtd/dot_general | solution.py:221
  174.5 1.3 copy.35
  (24 shorter events, 0.3 us)
Async XLA Ops:
  6.5 76.9 %all-gather.8.cloned.1.call-start = ((), (), s32[]{:S(2)}) async-start(), calls=%async_computation.1 | async-start | bytes 2641920 | tf_op jit(solution)/shard_map/all_gather | solution.py:118
  11.2 76.2 %copy-start.2 = (bf16[1,256,128]{2,1,0:T(8,128)(2,1)S(1)}, bf16[1,256,128]{2,1,0:T(8,128)(2,1)}, u32[]{:S(2)}) copy-start(bf16[1,256,128]{2,1,0:T(8,128)(2,1)} %param.15) | copy-start | bytes 196612
  11.2 76.2 %copy-start.3 = (bf16[1,256,128]{2,1,0:T(8,128)(2,1)S(1)}, bf16[1,256,128]{2,1,0:T(8,128)(2,1)}, u32[]{:S(2)}) copy-start(bf16[1,256,128]{2,1,0:T(8,128)(2,1)} %param.14) | copy-start | bytes 196612
  42.2 59.3 %copy-start.1 = (bf16[128,4096]{1,0:T(8,128)(2,1)S(1)}, bf16[128,4096]{1,0:T(8,128)(2,1)}, u32[]{:S(2)}) copy-start(bf16[128,4096]{1,0:T(8,128)(2,1)} %param.11) | copy-start | bytes 3145732
  43.4 71.1 %all-gather.10.cloned.1.call-start = ((), (), s32[]{:S(2)}) async-start(), calls=%async_computation.2 | async-start | bytes 6340608 | tf_op jit(solution)/shard_map/all_gather | solution.py:124
  87.5 16.4 %collective-permute-start.2 = (bf16[256,256]{1,0:T(8,128)(2,1)S(1)}, bf16[256,256]{1,0:T(8,128)(2,1)}, u32[]{:S(2)}, u32[]{:S(2)}) collective-permute-start(bf16[256,256]{1,0:T(8,128)(2,1)S(1)} %get-tuple-element.13), channel_id=1, source_target_pairs={{0,3},{1,0},{2,1},{3,2},{4,7},{5,4},{6,5},{7,6},{8,11},{9,8},{10,9... | collective-permute-start | bytes 393224 | tf_op jit(solution)/shard_map/ppermute | solution.py:134
  92.9 11.0 %collective-permute-start.1 = (bf16[256,256]{1,0:T(8,128)(2,1)S(1)}, bf16[256,256]{1,0:T(8,128)(2,1)}, u32[]{:S(2)}, u32[]{:S(2)}) collective-permute-start(bf16[256,256]{1,0:T(8,128)(2,1)S(1)} %get-tuple-element.13), channel_id=1, source_target_pairs={{0,2},{1,3},{2,0},{3,1},{4,6},{5,7},{6,4},{7,5},{8,10},{9,11},{10,... | collective-permute-start | bytes 393224 | tf_op jit(solution)/shard_map/ppermute | solution.py:134
  96.8 9.1 %collective-permute-start = (bf16[256,256]{1,0:T(8,128)(2,1)S(1)}, bf16[256,256]{1,0:T(8,128)(2,1)}, u32[]{:S(2)}, u32[]{:S(2)}) collective-permute-start(bf16[256,256]{1,0:T(8,128)(2,1)S(1)} %get-tuple-element.13), channel_id=1, source_target_pairs={{0,1},{1,2},{2,3},{3,0},{4,5},{5,6},{6,7},{7,4},{8,9},{9,10},{10,1... | collective-permute-start | bytes 393224 | tf_op jit(solution)/shard_map/ppermute | solution.py:134
  136.7 28.6 %all-to-all-start = ((bf16[4,256,256]{1,2,0:T(8,128)(2,1)}), bf16[4,256,256]{1,2,0:T(8,128)(2,1)S(1)}, u32[]{:S(2)}, u32[]{:S(2)}) async-start(bf16[4,256,256]{1,2,0:T(8,128)(2,1)} %broadcast_in_dim.71), calls=%async_computation | async-start | bytes 1048576 | tf_op jit(solution)/shard_map/all_to_all | solution.py:146
  141.5 22.9 %collective-permute-start.5 = (bf16[256,256]{0,1:T(8,128)(2,1)S(1)}, bf16[256,256]{0,1:T(8,128)(2,1)S(1)}, u32[]{:S(2)}, u32[]{:S(2)}) collective-permute-start(bf16[256,256]{0,1:T(8,128)(2,1)S(1)} %get-tuple-element.10), channel_id=1, source_target_pairs={{3,2},{0,3},{7,6},{4,7},{11,10},{8,11},{15,14},{12,15},{19,18},{16... | collective-permute-start | bytes 393224 | tf_op jit(solution)/shard_map/ppermute | solution.py:152
  147.0 17.5 %collective-permute-start.4 = (bf16[256,256]{0,1:T(8,128)(2,1)S(1)}, bf16[256,256]{0,1:T(8,128)(2,1)S(1)}, u32[]{:S(2)}, u32[]{:S(2)}) collective-permute-start(bf16[256,256]{0,1:T(8,128)(2,1)S(1)} %get-tuple-element.10), channel_id=1, source_target_pairs={{0,2},{1,3},{4,6},{5,7},{8,10},{9,11},{12,14},{13,15},{16,18},{17,... | collective-permute-start | bytes 393224 | tf_op jit(solution)/shard_map/ppermute | solution.py:152
  150.1 14.4 %collective-permute-start.3 = (bf16[256,256]{0,1:T(8,128)(2,1)S(1)}, bf16[256,256]{0,1:T(8,128)(2,1)S(1)}, u32[]{:S(2)}, u32[]{:S(2)}) collective-permute-start(bf16[256,256]{0,1:T(8,128)(2,1)S(1)} %get-tuple-element.10), channel_id=1, source_target_pairs={{1,2},{2,3},{5,6},{6,7},{9,10},{10,11},{13,14},{14,15},{17,18},{18... | collective-permute-start | bytes 393224 | tf_op jit(solution)/shard_map/ppermute | solution.py:152
  165.3 2.2 %copy-start = (f32[4,256,128,8]{2,1,3,0:T(8,128)S(1)}, f32[4,256,128,8]{2,1,3,0:T(8,128)}, u32[]{:S(2)}) copy-start(f32[4,256,128,8]{2,1,3,0:T(8,128)} %get-tuple-element.17) | copy-start | bytes 12582916
Sparse Core Ops, SparseCore 0:
  43.5 39.8 all-gather.7
  87.6 26.8 all-gather.9

commit v13 on v12

--- a/solution.py
+++ b/solution.py
@@ -109,7 +109,7 @@
 
 FSDP_PARTS = (("ylo", 2), ("x", 4), ("z", 12), ("core", 2))
 FSDP_AXES = tuple(name for name, _ in FSDP_PARTS)
-GATHER_STAGES = (("ylo",), ("z",), ("x",), ("core",))
+GATHER_STAGES = (("z",), ("ylo",), ("x",), ("core",))
 
 
 def gather_weights(shard):

time: 183 us -> 185 us (1.011)
  waiting for transfers between devices: 59.7 us -> 61.8 us
    all_gather x1, waiting for transfers between devices: 40 us -> 42 us  [gather_weights(): gathered = lax.all_gather(gathered, stage, axis=0, tiled=False)]
    all_gather x2 -> x1, local copies, waits for them, and re-layouts: 5.27 us -> 5.22 us  [gather_weights(): gathered = lax.all_gather(gathered, stage, axis=0, tiled=False)]
where the time goes in v13:
time: 185 us
  waiting for transfers between devices  61.8 us (33%)
  blocking collectives  36.2 us (20%)
  starting transfers between devices  27.5 us (15%)
  local copies, waits for them, and re-layouts  22.2 us (12%)
  between operations  15.1 us (8%)
  matrix products  14.8 us (8%)
  other arithmetic  7.16 us (4%)
    all_gather x1, waiting for transfers between devices, gather_weights(): gathered = lax.all_gather(gathered, stage, axis=0, tiled=False)  42 us
    all_gather x2, blocking collectives, gather_weights(): gathered = lax.all_gather(gathered, stage, axis=0, tiled=False)  36.2 us
    ppermute x3, starting transfers between devices, gather_sp(): pieces.append(lax.ppermute(block, 'sp', perm=pairs))  13.3 us
    ppermute x3, waiting for transfers between devices, exchange_causal(): pieces.append(lax.ppermute(tail, 'sp', perm=pairs))  10.8 us
    ppermute x3, starting transfers between devices, exchange_causal(): pieces.append(lax.ppermute(tail, 'sp', perm=pairs))  9.42 us
    reshape x1, local copies, waits for them, and re-layouts, gather_weights(): return gathered.reshape(-1, shard.shape[1])  7.04 us
    dot_general x1, matrix products, per_device(): jnp.dot(hidden_rows, whole_kv[:model_width], preferred_element_type=jnp.f...  7.04 us
    all_gather x1, waiting for transfers between devices, gather_weights(): lax.all_gather(gathered, last, axis=FSDP_AXES.index(last), tiled=False)  6.94 us
  transfers between devices with their start and end apart: 9, of which 4 were waited for; matrix products, arithmetic and copies ran while one was open for 4% of the time, Pallas kernels for 0%

profile of v13, /device:TPU:1, one launch (start us, length us, event | category | flops | bytes accessed | tf_op | source)
XLA Modules:
  0.0 184.6 jit_solution(17718873972444293841)
XLA Ops:
  6.5 0.7 maximum_bitcast_fusion
  7.3 29.7 %all-gather.4 = bf16[12,43,256]{2,1,0:T(8,128)(2,1)S(1)} all-gather(bf16[1,43,256]{2,1,0:T(8,128)(2,1)S(1)} %maximum_bitcast_fusion), channel_id=2, replica_groups=mesh['ylo'=2,'x'=4,'z'=12,'core'=2,'sp'=4] {'z'}, dimensions={0}, use_global_device_ids=true | all-gather | bytes 286208 | tf_op jit(solution)/shard_map/all_gather | solution.py:118
  37.0 6.5 %all-gather.1 = bf16[24,43,256]{2,1,0:T(8,128)(2,1)} all-gather(bf16[12,43,256]{2,1,0:T(8,128)(2,1)S(1)} %all-gather.4), channel_id=3, replica_groups=mesh['ylo'=2,'x'=4,'z'=12,'core'=2,'sp'=4] {'ylo'}, dimensions={0}, use_global_device_ids=true | all-gather | bytes 792576 | tf_op jit(solution)/shard_map/all_gather | solution.py:118
  43.5 0.0 all-gather.8.cloned.1.call-update
  43.5 0.0 all-gather.10.cloned.1.call-start
  43.6 42.0 %all-gather.8.cloned.1.call-done = bf16[8,12,43,256]{3,2,1,0:T(8,128)(2,1)} async-done(((bf16[2,12,43,256]{3,2,1,0:T(8,128)(2,1)}), bf16[8,12,43,256]{3,2,1,0:T(8,128)(2,1)}) %all-gather.8.cloned.1.call-update) | async-done | bytes 2113552 | tf_op jit(solution)/shard_map/all_gather | solution.py:118
  85.6 5.2 %copy.58 = bf16[4,2,12,43,256]{4,1,0,3,2:T(2,128)(2,1)} copy(bf16[4,2,12,43,256]{4,3,2,1,0:T(8,128)(2,1)} %bitcast.90) | data formatting | bytes 4227072 | tf_op jit(solution)/shard_map/all_gather | solution.py:118
  90.8 0.0 all-gather.10.cloned.1.call-update
  90.9 5.3 %collective-permute-start.2 = (bf16[256,256]{1,0:T(8,128)(2,1)S(1)}, bf16[256,256]{1,0:T(8,128)(2,1)}, u32[]{:S(2)}, u32[]{:S(2)}) collective-permute-start(bf16[256,256]{1,0:T(8,128)(2,1)S(1)} %get-tuple-element.13), channel_id=1, source_target_pairs={{0,3},{1,0},{2,1},{3,2},{4,7},{5,4},{6,5},{7,6},{8,11},{9,8},{10,9... | collective-permute-start | bytes 393224 | tf_op jit(solution)/shard_map/ppermute | solution.py:134
  96.2 3.9 %collective-permute-start.1 = (bf16[256,256]{1,0:T(8,128)(2,1)S(1)}, bf16[256,256]{1,0:T(8,128)(2,1)}, u32[]{:S(2)}, u32[]{:S(2)}) collective-permute-start(bf16[256,256]{1,0:T(8,128)(2,1)S(1)} %get-tuple-element.13), channel_id=1, source_target_pairs={{0,2},{1,3},{2,0},{3,1},{4,6},{5,7},{6,4},{7,5},{8,10},{9,11},{10,... | collective-permute-start | bytes 393224 | tf_op jit(solution)/shard_map/ppermute | solution.py:134
  100.1 4.0 %collective-permute-start = (bf16[256,256]{1,0:T(8,128)(2,1)S(1)}, bf16[256,256]{1,0:T(8,128)(2,1)}, u32[]{:S(2)}, u32[]{:S(2)}) collective-permute-start(bf16[256,256]{1,0:T(8,128)(2,1)S(1)} %get-tuple-element.13), channel_id=1, source_target_pairs={{0,1},{1,2},{2,3},{3,0},{4,5},{5,6},{6,7},{7,4},{8,9},{9,10},{10,1... | collective-permute-start | bytes 393224 | tf_op jit(solution)/shard_map/ppermute | solution.py:134
  104.8 0.0 copy-done.1
  104.8 0.7 copy.34
  105.5 0.2 convert.21
  106.6 0.2 fusion.45
  106.8 0.3 subtract_convert_fusion
  107.1 0.1 pad_maximum_fusion
  107.2 0.0 collective-permute-done.2
  107.2 0.0 collective-permute-done.1
  107.2 2.0 %collective-permute-done = bf16[256,256]{1,0:T(8,128)(2,1)} collective-permute-done((bf16[256,256]{1,0:T(8,128)(2,1)S(1)}, bf16[256,256]{1,0:T(8,128)(2,1)}, u32[]{:S(2)}, u32[]{:S(2)}) %collective-permute-start) | collective-permute-done | bytes 131104 | tf_op jit(solution)/shard_map/ppermute | solution.py:134
  109.2 1.2 pad_maximum_fusion.2
  110.4 0.6 gather_fusion
  111.0 6.9 %all-gather.10.cloned.1.call-done = bf16[2,4,12,86,256]{4,0,1,3,2:T(2,128)(2,1)} async-done(((bf16[2,4,12,43,256]{4,0,1,3,2:T(2,128)(2,1)}), bf16[2,4,12,86,256]{4,0,1,3,2:T(2,128)(2,1)}) %all-gather.10.cloned.1.call-update) | async-done | bytes 4227088 | tf_op jit(solution)/shard_map/all_gather | solution.py:124
  117.9 5.1 %copy.37 = bf16[2,4,12,86,256]{4,3,2,1,0:T(8,128)(2,1)} copy(bf16[2,4,12,86,256]{4,0,1,3,2:T(2,128)(2,1)} %all-gather.10.cloned.1.call-done) | data formatting | bytes 8454144 | tf_op jit(solution)/shard_map/all_gather | solution.py:124
  123.0 7.0 %reshape.239 = bf16[8256,256]{1,0:T(8,128)(2,1)} reshape(bf16[2,4,12,86,256]{4,3,2,1,0:T(8,128)(2,1)} %copy.37) | data formatting | bytes 8454144 | tf_op jit(solution)/shard_map/reshape | solution.py:125
  130.1 7.0 %fusion.23 = f32[512,256]{0,1:T(8,128)S(1)} fusion(bf16[512,8192]{1,0:T(8,128)(2,1)} %param.10, bf16[8256,256]{1,0:T(8,128)(2,1)} %reshape.239), kind=kOutput, calls=%fused_computation.28 | convolution fusion | flops 2147483648 | bytes 13107200 | tf_op jit(solution)/shard_map/dot_general | solution.py:184
  137.2 0.6 fusion.38
  137.8 0.8 broadcast_in_dim.71
  138.7 4.7 %all-to-all-start = ((bf16[4,256,256]{1,2,0:T(8,128)(2,1)}), bf16[4,256,256]{1,2,0:T(8,128)(2,1)S(1)}, u32[]{:S(2)}, u32[]{:S(2)}) async-start(bf16[4,256,256]{1,2,0:T(8,128)(2,1)} %broadcast_in_dim.71), calls=%async_computation | async-start | bytes 1048576 | tf_op jit(solution)/shard_map/all_to_all | solution.py:146
  143.4 0.1 broadcast_select_fusion.1
  143.5 5.5 %collective-permute-start.5 = (bf16[256,256]{0,1:T(8,128)(2,1)S(1)}, bf16[256,256]{0,1:T(8,128)(2,1)S(1)}, u32[]{:S(2)}, u32[]{:S(2)}) collective-permute-start(bf16[256,256]{0,1:T(8,128)(2,1)S(1)} %get-tuple-element.10), channel_id=1, source_target_pairs={{3,2},{0,3},{7,6},{4,7},{11,10},{8,11},{15,14},{12,15},{19,18},{16... | collective-permute-start | bytes 393224 | tf_op jit(solution)/shard_map/ppermute | solution.py:152
  149.0 3.1 %collective-permute-start.4 = (bf16[256,256]{0,1:T(8,128)(2,1)S(1)}, bf16[256,256]{0,1:T(8,128)(2,1)S(1)}, u32[]{:S(2)}, u32[]{:S(2)}) collective-permute-start(bf16[256,256]{0,1:T(8,128)(2,1)S(1)} %get-tuple-element.10), channel_id=1, source_target_pairs={{0,2},{1,3},{4,6},{5,7},{8,10},{9,11},{12,14},{13,15},{16,18},{17,... | collective-permute-start | bytes 393224 | tf_op jit(solution)/shard_map/ppermute | solution.py:152
  152.1 0.8 collective-permute-start.3
  152.9 2.7 %bitcast_reduce_fusion = (f32[4,8,128]{2,1,0:T(8,128)S(1)}, f32[4,256,128,8]{2,1,3,0:T(8,128)}) fusion(pred[256]{0:T(512)(128)(4,1)S(1)} %iota_compare_fusion.1, bf16[128,4,8,128]{0,3,2,1:T(8,128)(2,1)S(1)} %bitcast.86, bf16[4,256,256]{2,1,0:T(8,128)(2,1)S(1)} %broadcast_select_fusion.1), kind=kOutput, calls=%fused_computation.10 | convolution fusion | flops 271577088 | bytes 5521920 | tf_op jit(solution)/shard_map/thgd,hjd->hgtj/dot_general | solution.py:199
  155.6 10.8 %collective-permute-done.5 = bf16[256,256]{0,1:T(8,128)(2,1)S(1)} collective-permute-done((bf16[256,256]{0,1:T(8,128)(2,1)S(1)}, bf16[256,256]{0,1:T(8,128)(2,1)S(1)}, u32[]{:S(2)}, u32[]{:S(2)}) %collective-permute-start.5) | collective-permute-done | bytes 131104 | tf_op jit(solution)/shard_map/ppermute | solution.py:152
  166.4 0.0 collective-permute-done.4
  166.4 0.0 collective-permute-done.3
  166.4 0.1 pad_maximum_fusion.3
  166.5 0.6 gather_fusion.1
  167.1 0.1 broadcast_select_fusion
  167.2 0.0 all-to-all-done
  167.3 1.4 fusion
  168.7 0.7 copy-done
  169.4 1.2 fusion.12
  170.6 1.2 fusion.10
  171.8 2.2 %fusion.1 = f32[4,8,128]{2,1,0:T(8,128)S(1)} fusion(f32[4,512,128,8]{2,1,3,0:T(8,128)S(1)} %get-tuple-element.19, f32[4,8,128]{2,1,0:T(8,128)S(1)} %max.16, pred[128,512]{0,1:T(8,128)(4,1)S(1)} %iota_compare_fusion), kind=kLoop, calls=%fused_computation.5 | loop fusion | flops 10481664 | bytes 8486912 | tf_op jit(solution)/shard_map/reduce_sum | solution.py:215
  174.0 2.5 %fusion.14 = bf16[128,4,8,128]{0,3,2,1:T(8,128)(2,1)S(1)} fusion(f32[4,8,128,128]{2,3,1,0:T(8,128)S(1)} %fusion.12, f32[4,512,128,8]{2,1,3,0:T(8,128)S(1)} %get-tuple-element.19, f32[4,8,128]{2,1,0:T(8,128)S(1)} %max.16, pred[128,512]{0,1:T(8,128)(4,1)S(1)} %iota_compare_fusion, f32[128,4,8]{0,2,1:T(8,128)S(1)} %add_bitcast_fusion, ...), kind=kOutput, calls=%fused_computation.21 | convolution fusion | flops 549978112 | bytes 12681216 | tf_op jit(solution)/shard_map/hgtu,hud->hgtd/dot_general | solution.py:221
  176.5 1.3 copy.43
  (23 shorter events, 0.2 us)
Async XLA Ops:
  6.5 79.0 %all-gather.8.cloned.1.call-start = ((), (), s32[]{:S(2)}) async-start(), calls=%async_computation.1 | async-start | bytes 2949120 | tf_op jit(solution)/shard_map/all_gather | solution.py:118
  7.3 83.6 %copy-start.2 = (bf16[1,256,128]{2,1,0:T(8,128)(2,1)S(1)}, bf16[1,256,128]{2,1,0:T(8,128)(2,1)}, u32[]{:S(2)}) copy-start(bf16[1,256,128]{2,1,0:T(8,128)(2,1)} %param.15) | copy-start | bytes 196612
  7.3 83.6 %copy-start.3 = (bf16[1,256,128]{2,1,0:T(8,128)(2,1)S(1)}, bf16[1,256,128]{2,1,0:T(8,128)(2,1)}, u32[]{:S(2)}) copy-start(bf16[1,256,128]{2,1,0:T(8,128)(2,1)} %param.14) | copy-start | bytes 196612
  37.0 67.8 %copy-start.1 = (bf16[128,4096]{1,0:T(8,128)(2,1)S(1)}, bf16[128,4096]{1,0:T(8,128)(2,1)}, u32[]{:S(2)}) copy-start(bf16[128,4096]{1,0:T(8,128)(2,1)} %param.11) | copy-start | bytes 3145732
  43.5 74.4 %all-gather.10.cloned.1.call-start = ((), (), s32[]{:S(2)}) async-start(), calls=%async_computation.2 | async-start | bytes 6340608 | tf_op jit(solution)/shard_map/all_gather | solution.py:124
  90.9 16.4 %collective-permute-start.2 = (bf16[256,256]{1,0:T(8,128)(2,1)S(1)}, bf16[256,256]{1,0:T(8,128)(2,1)}, u32[]{:S(2)}, u32[]{:S(2)}) collective-permute-start(bf16[256,256]{1,0:T(8,128)(2,1)S(1)} %get-tuple-element.13), channel_id=1, source_target_pairs={{0,3},{1,0},{2,1},{3,2},{4,7},{5,4},{6,5},{7,6},{8,11},{9,8},{10,9... | collective-permute-start | bytes 393224 | tf_op jit(solution)/shard_map/ppermute | solution.py:134
  96.2 11.0 %collective-permute-start.1 = (bf16[256,256]{1,0:T(8,128)(2,1)S(1)}, bf16[256,256]{1,0:T(8,128)(2,1)}, u32[]{:S(2)}, u32[]{:S(2)}) collective-permute-start(bf16[256,256]{1,0:T(8,128)(2,1)S(1)} %get-tuple-element.13), channel_id=1, source_target_pairs={{0,2},{1,3},{2,0},{3,1},{4,6},{5,7},{6,4},{7,5},{8,10},{9,11},{10,... | collective-permute-start | bytes 393224 | tf_op jit(solution)/shard_map/ppermute | solution.py:134
  100.1 9.1 %collective-permute-start = (bf16[256,256]{1,0:T(8,128)(2,1)S(1)}, bf16[256,256]{1,0:T(8,128)(2,1)}, u32[]{:S(2)}, u32[]{:S(2)}) collective-permute-start(bf16[256,256]{1,0:T(8,128)(2,1)S(1)} %get-tuple-element.13), channel_id=1, source_target_pairs={{0,1},{1,2},{2,3},{3,0},{4,5},{5,6},{6,7},{7,4},{8,9},{9,10},{10,1... | collective-permute-start | bytes 393224 | tf_op jit(solution)/shard_map/ppermute | solution.py:134
  138.7 28.6 %all-to-all-start = ((bf16[4,256,256]{1,2,0:T(8,128)(2,1)}), bf16[4,256,256]{1,2,0:T(8,128)(2,1)S(1)}, u32[]{:S(2)}, u32[]{:S(2)}) async-start(bf16[4,256,256]{1,2,0:T(8,128)(2,1)} %broadcast_in_dim.71), calls=%async_computation | async-start | bytes 1048576 | tf_op jit(solution)/shard_map/all_to_all | solution.py:146
  143.5 22.9 %collective-permute-start.5 = (bf16[256,256]{0,1:T(8,128)(2,1)S(1)}, bf16[256,256]{0,1:T(8,128)(2,1)S(1)}, u32[]{:S(2)}, u32[]{:S(2)}) collective-permute-start(bf16[256,256]{0,1:T(8,128)(2,1)S(1)} %get-tuple-element.10), channel_id=1, source_target_pairs={{3,2},{0,3},{7,6},{4,7},{11,10},{8,11},{15,14},{12,15},{19,18},{16... | collective-permute-start | bytes 393224 | tf_op jit(solution)/shard_map/ppermute | solution.py:152
  149.0 17.5 %collective-permute-start.4 = (bf16[256,256]{0,1:T(8,128)(2,1)S(1)}, bf16[256,256]{0,1:T(8,128)(2,1)S(1)}, u32[]{:S(2)}, u32[]{:S(2)}) collective-permute-start(bf16[256,256]{0,1:T(8,128)(2,1)S(1)} %get-tuple-element.10), channel_id=1, source_target_pairs={{0,2},{1,3},{4,6},{5,7},{8,10},{9,11},{12,14},{13,15},{16,18},{17,... | collective-permute-start | bytes 393224 | tf_op jit(solution)/shard_map/ppermute | solution.py:152
  152.1 14.4 %collective-permute-start.3 = (bf16[256,256]{0,1:T(8,128)(2,1)S(1)}, bf16[256,256]{0,1:T(8,128)(2,1)S(1)}, u32[]{:S(2)}, u32[]{:S(2)}) collective-permute-start(bf16[256,256]{0,1:T(8,128)(2,1)S(1)} %get-tuple-element.10), channel_id=1, source_target_pairs={{1,2},{2,3},{5,6},{6,7},{9,10},{10,11},{13,14},{14,15},{17,18},{18... | collective-permute-start | bytes 393224 | tf_op jit(solution)/shard_map/ppermute | solution.py:152
  167.2 2.2 %copy-start = (f32[4,256,128,8]{2,1,3,0:T(8,128)S(1)}, f32[4,256,128,8]{2,1,3,0:T(8,128)}, u32[]{:S(2)}) copy-start(f32[4,256,128,8]{2,1,3,0:T(8,128)} %get-tuple-element.17) | copy-start | bytes 12582916
Sparse Core Ops, SparseCore 0:
  43.6 41.8 all-gather.7
  90.9 26.9 all-gather.9

commit v14 on v12

--- a/solution.py
+++ b/solution.py
@@ -114,14 +114,17 @@
 
 def gather_weights(shard):
     gathered = shard
-    for stage in GATHER_STAGES[:-1]:
+    for stage in GATHER_STAGES:
         gathered = lax.all_gather(gathered, stage, axis=0, tiled=False)
-    early = [name for stage in reversed(GATHER_STAGES[:-1]) for name in stage]
-    wanted = [name for name in FSDP_AXES if name in early]
-    rank = len(early)
-    gathered = gathered.transpose([early.index(name) for name in wanted] + [rank, rank + 1])
-    (last,) = GATHER_STAGES[-1]
-    gathered = lax.all_gather(gathered, last, axis=FSDP_AXES.index(last), tiled=False)
+        if len(stage) > 1:
+            sizes = tuple(dict(FSDP_PARTS)[name] for name in stage)
+            gathered = gathered.reshape(sizes + gathered.shape[1:])
+    layout = []
+    for stage in reversed(GATHER_STAGES):
+        layout.extend(stage)
+    perm = [layout.index(name) for name in FSDP_AXES]
+    rank = len(FSDP_AXES)
+    gathered = gathered.transpose(perm + [rank, rank + 1])
     return gathered.reshape(-1, shard.shape[1])
 
 

time: 183 us -> 180 us (0.984)
  local copies, waits for them, and re-layouts: 23.6 us -> 18.5 us
  waiting for transfers between devices: 59.7 us -> 61.9 us
    all_gather x1 -> x2, waiting for transfers between devices: 40 us -> 49.1 us  [gather_weights(): gathered = lax.all_gather(gathered, stage, axis=0, tiled=False)]
    all_gather x1 -> x0, waiting for transfers between devices: 6.89 us -> none  [gather_weights(): lax.all_gather(gathered, last, axis=FSDP_AXES.index(last), tiled=False)]
    all_gather x1 -> x0, local copies, waits for them, and re-layouts: 6.57 us -> none  [gather_weights(): lax.all_gather(gathered, last, axis=FSDP_AXES.index(last), tiled=False)]
    transpose x0 -> x1, local copies, waits for them, and re-layouts: none -> 5.21 us  [gather_weights(): gathered = gathered.transpose(perm + [rank, rank + 1])]
    all_gather x2 -> x1, local copies, waits for them, and re-layouts: 5.27 us -> 1.21 us  [gather_weights(): gathered = lax.all_gather(gathered, stage, axis=0, tiled=False)]
where the time goes in v14:
time: 180 us
  waiting for transfers between devices  61.9 us (34%)
  blocking collectives  34.7 us (19%)
  starting transfers between devices  27.5 us (15%)
  local copies, waits for them, and re-layouts  18.5 us (10%)
  between operations  15 us (8%)
  matrix products  14.8 us (8%)
  other arithmetic  7.24 us (4%)
    all_gather x2, waiting for transfers between devices, gather_weights(): gathered = lax.all_gather(gathered, stage, axis=0, tiled=False)  49.1 us
    all_gather x2, blocking collectives, gather_weights(): gathered = lax.all_gather(gathered, stage, axis=0, tiled=False)  34.7 us
    ppermute x3, starting transfers between devices, gather_sp(): pieces.append(lax.ppermute(block, 'sp', perm=pairs))  13.3 us
    ppermute x3, waiting for transfers between devices, exchange_causal(): pieces.append(lax.ppermute(tail, 'sp', perm=pairs))  10.8 us
    ppermute x3, starting transfers between devices, exchange_causal(): pieces.append(lax.ppermute(tail, 'sp', perm=pairs))  9.42 us
    reshape x1, local copies, waits for them, and re-layouts, gather_weights(): return gathered.reshape(-1, shard.shape[1])  7.27 us
    dot_general x1, matrix products, per_device(): jnp.dot(hidden_rows, whole_kv[:model_width], preferred_element_type=jnp.f...  7.04 us
    transpose x1, local copies, waits for them, and re-layouts, gather_weights(): gathered = gathered.transpose(perm + [rank, rank + 1])  5.21 us
  transfers between devices with their start and end apart: 9, of which 4 were waited for; matrix products, arithmetic and copies ran while one was open for 4% of the time, Pallas kernels for 0%

profile of v14, /device:TPU:1, one launch (start us, length us, event | category | flops | bytes accessed | tf_op | source)
XLA Modules:
  0.0 179.7 jit_solution(13507262029545570415)
XLA Ops:
  6.5 0.0 all-gather.8.cloned.1.call-start
  6.5 0.8 maximum_bitcast_fusion
  7.4 4.0 %all-gather.4 = bf16[2,43,256]{2,1,0:T(8,128)(2,1)S(1)} all-gather(bf16[1,43,256]{2,1,0:T(8,128)(2,1)S(1)} %maximum_bitcast_fusion), channel_id=2, replica_groups=mesh['ylo'=2,'x'=4,'z'=12,'core'=2,'sp'=4] {'ylo'}, dimensions={0}, use_global_device_ids=true | all-gather | bytes 66048 | tf_op jit(solution)/shard_map/all_gather | solution.py:118
  11.3 30.8 %all-gather.1 = bf16[24,43,256]{2,1,0:T(8,128)(2,1)S(1)} all-gather(bf16[2,43,256]{2,1,0:T(8,128)(2,1)S(1)} %all-gather.4), channel_id=3, replica_groups=mesh['ylo'=2,'x'=4,'z'=12,'core'=2,'sp'=4] {'z'}, dimensions={0}, use_global_device_ids=true | all-gather | bytes 572416 | tf_op jit(solution)/shard_map/all_gather | solution.py:118
  42.1 1.2 copy.36
  43.3 0.0 all-gather.8.cloned.1.call-update
  43.4 0.0 all-gather.10.cloned.1.call-start
  43.4 40.0 %all-gather.8.cloned.1.call-done = bf16[48,2,43,256]{3,1,2,0:T(2,128)(2,1)} async-done(((bf16[12,2,43,256]{3,1,2,0:T(2,128)(2,1)}), bf16[48,2,43,256]{3,1,2,0:T(2,128)(2,1)}) %all-gather.8.cloned.1.call-update) | async-done | bytes 2113552 | tf_op jit(solution)/shard_map/all_gather | solution.py:118
  83.3 0.0 all-gather.10.cloned.1.call-update
  83.4 5.3 %collective-permute-start.2 = (bf16[256,256]{1,0:T(8,128)(2,1)S(1)}, bf16[256,256]{1,0:T(8,128)(2,1)}, u32[]{:S(2)}, u32[]{:S(2)}) collective-permute-start(bf16[256,256]{1,0:T(8,128)(2,1)S(1)} %get-tuple-element.13), channel_id=1, source_target_pairs={{0,3},{1,0},{2,1},{3,2},{4,7},{5,4},{6,5},{7,6},{8,11},{9,8},{10,9... | collective-permute-start | bytes 393224 | tf_op jit(solution)/shard_map/ppermute | solution.py:137
  88.8 3.9 %collective-permute-start.1 = (bf16[256,256]{1,0:T(8,128)(2,1)S(1)}, bf16[256,256]{1,0:T(8,128)(2,1)}, u32[]{:S(2)}, u32[]{:S(2)}) collective-permute-start(bf16[256,256]{1,0:T(8,128)(2,1)S(1)} %get-tuple-element.13), channel_id=1, source_target_pairs={{0,2},{1,3},{2,0},{3,1},{4,6},{5,7},{6,4},{7,5},{8,10},{9,11},{10,... | collective-permute-start | bytes 393224 | tf_op jit(solution)/shard_map/ppermute | solution.py:137
  92.7 4.0 %collective-permute-start = (bf16[256,256]{1,0:T(8,128)(2,1)S(1)}, bf16[256,256]{1,0:T(8,128)(2,1)}, u32[]{:S(2)}, u32[]{:S(2)}) collective-permute-start(bf16[256,256]{1,0:T(8,128)(2,1)S(1)} %get-tuple-element.13), channel_id=1, source_target_pairs={{0,1},{1,2},{2,3},{3,0},{4,5},{5,6},{6,7},{7,4},{8,9},{9,10},{10,1... | collective-permute-start | bytes 393224 | tf_op jit(solution)/shard_map/ppermute | solution.py:137
  97.4 0.7 copy.34
  98.1 0.2 convert.21
  99.2 0.2 fusion.45
  99.4 0.3 subtract_convert_fusion
  99.7 0.1 pad_maximum_fusion
  99.8 0.0 collective-permute-done.2
  99.8 0.0 collective-permute-done.1
  99.8 2.0 %collective-permute-done = bf16[256,256]{1,0:T(8,128)(2,1)} collective-permute-done((bf16[256,256]{1,0:T(8,128)(2,1)S(1)}, bf16[256,256]{1,0:T(8,128)(2,1)}, u32[]{:S(2)}, u32[]{:S(2)}) %collective-permute-start) | collective-permute-done | bytes 131104 | tf_op jit(solution)/shard_map/ppermute | solution.py:137
  101.8 1.2 pad_maximum_fusion.2
  102.9 0.6 gather_fusion
  103.5 9.1 %all-gather.10.cloned.1.call-done = bf16[8,12,2,43,256]{4,2,3,1,0:T(2,128)(2,1)} async-done(((bf16[4,12,2,43,256]{4,2,3,1,0:T(2,128)(2,1)}), bf16[8,12,2,43,256]{4,2,3,1,0:T(2,128)(2,1)}) %all-gather.10.cloned.1.call-update) | async-done | bytes 4227088 | tf_op jit(solution)/shard_map/all_gather | solution.py:118
  112.7 5.2 %copy.37 = bf16[2,4,12,2,43,256]{5,4,3,2,1,0:T(8,128)(2,1)} copy(bf16[2,4,12,2,43,256]{5,0,4,2,1,3:T(2,128)(2,1)} %bitcast.88) | data formatting | bytes 8454144 | tf_op jit(solution)/shard_map/transpose | solution.py:127
  117.9 7.3 %reshape.239 = bf16[8256,256]{1,0:T(8,128)(2,1)} reshape(bf16[2,4,12,2,43,256]{5,4,3,2,1,0:T(8,128)(2,1)} %copy.37) | data formatting | bytes 8454144 | tf_op jit(solution)/shard_map/reshape | solution.py:128
  125.1 7.0 %fusion.23 = f32[512,256]{0,1:T(8,128)S(1)} fusion(bf16[512,8192]{1,0:T(8,128)(2,1)} %param.10, bf16[8256,256]{1,0:T(8,128)(2,1)} %reshape.239), kind=kOutput, calls=%fused_computation.27 | convolution fusion | flops 2147483648 | bytes 13107200 | tf_op jit(solution)/shard_map/dot_general | solution.py:187
  132.2 0.6 fusion.38
  132.9 0.8 broadcast_in_dim.71
  133.7 4.7 %all-to-all-start = ((bf16[4,256,256]{1,2,0:T(8,128)(2,1)}), bf16[4,256,256]{1,2,0:T(8,128)(2,1)S(1)}, u32[]{:S(2)}, u32[]{:S(2)}) async-start(bf16[4,256,256]{1,2,0:T(8,128)(2,1)} %broadcast_in_dim.71), calls=%async_computation | async-start | bytes 1048576 | tf_op jit(solution)/shard_map/all_to_all | solution.py:149
  138.4 0.1 broadcast_select_fusion.1
  138.5 5.5 %collective-permute-start.5 = (bf16[256,256]{0,1:T(8,128)(2,1)S(1)}, bf16[256,256]{0,1:T(8,128)(2,1)S(1)}, u32[]{:S(2)}, u32[]{:S(2)}) collective-permute-start(bf16[256,256]{0,1:T(8,128)(2,1)S(1)} %get-tuple-element.10), channel_id=1, source_target_pairs={{3,2},{0,3},{7,6},{4,7},{11,10},{8,11},{15,14},{12,15},{19,18},{16... | collective-permute-start | bytes 393224 | tf_op jit(solution)/shard_map/ppermute | solution.py:155
  144.0 3.1 %collective-permute-start.4 = (bf16[256,256]{0,1:T(8,128)(2,1)S(1)}, bf16[256,256]{0,1:T(8,128)(2,1)S(1)}, u32[]{:S(2)}, u32[]{:S(2)}) collective-permute-start(bf16[256,256]{0,1:T(8,128)(2,1)S(1)} %get-tuple-element.10), channel_id=1, source_target_pairs={{0,2},{1,3},{4,6},{5,7},{8,10},{9,11},{12,14},{13,15},{16,18},{17,... | collective-permute-start | bytes 393224 | tf_op jit(solution)/shard_map/ppermute | solution.py:155
  147.1 0.8 collective-permute-start.3
  148.0 2.7 %bitcast_reduce_fusion = (f32[4,8,128]{2,1,0:T(8,128)S(1)}, f32[4,256,128,8]{2,1,3,0:T(8,128)}) fusion(pred[256]{0:T(512)(128)(4,1)S(1)} %iota_compare_fusion.1, bf16[128,4,8,128]{0,3,2,1:T(8,128)(2,1)S(1)} %bitcast.86, bf16[4,256,256]{2,1,0:T(8,128)(2,1)S(1)} %broadcast_select_fusion.1), kind=kOutput, calls=%fused_computation.10 | convolution fusion | flops 271577088 | bytes 5521920 | tf_op jit(solution)/shard_map/thgd,hjd->hgtj/dot_general | solution.py:202
  150.7 10.8 %collective-permute-done.5 = bf16[256,256]{0,1:T(8,128)(2,1)S(1)} collective-permute-done((bf16[256,256]{0,1:T(8,128)(2,1)S(1)}, bf16[256,256]{0,1:T(8,128)(2,1)S(1)}, u32[]{:S(2)}, u32[]{:S(2)}) %collective-permute-start.5) | collective-permute-done | bytes 131104 | tf_op jit(solution)/shard_map/ppermute | solution.py:155
  161.5 0.0 collective-permute-done.4
  161.5 0.0 collective-permute-done.3
  161.5 0.1 pad_maximum_fusion.3
  161.6 0.6 gather_fusion.1
  162.2 0.1 broadcast_select_fusion
  162.3 0.0 all-to-all-done
  162.3 1.4 fusion
  163.7 0.7 copy-done
  164.5 1.2 fusion.12
  165.7 1.2 fusion.10
  166.8 2.2 %fusion.1 = f32[4,8,128]{2,1,0:T(8,128)S(1)} fusion(f32[4,512,128,8]{2,1,3,0:T(8,128)S(1)} %get-tuple-element.19, f32[4,8,128]{2,1,0:T(8,128)S(1)} %max.16, pred[128,512]{0,1:T(8,128)(4,1)S(1)} %iota_compare_fusion), kind=kLoop, calls=%fused_computation.5 | loop fusion | flops 10481664 | bytes 8486912 | tf_op jit(solution)/shard_map/reduce_sum | solution.py:218
  169.0 2.5 %fusion.14 = bf16[128,4,8,128]{0,3,2,1:T(8,128)(2,1)S(1)} fusion(f32[4,8,128,128]{2,3,1,0:T(8,128)S(1)} %fusion.12, f32[4,512,128,8]{2,1,3,0:T(8,128)S(1)} %get-tuple-element.19, f32[4,8,128]{2,1,0:T(8,128)S(1)} %max.16, pred[128,512]{0,1:T(8,128)(4,1)S(1)} %iota_compare_fusion, f32[128,4,8]{0,2,1:T(8,128)S(1)} %add_bitcast_fusion, ...), kind=kOutput, calls=%fused_computation.20 | convolution fusion | flops 549978112 | bytes 12681216 | tf_op jit(solution)/shard_map/hgtu,hud->hgtd/dot_general | solution.py:224
  171.5 1.3 copy.43
  (23 shorter events, 0.2 us)
Async XLA Ops:
  6.5 76.8 %copy-start.2 = (bf16[1,256,128]{2,1,0:T(8,128)(2,1)S(1)}, bf16[1,256,128]{2,1,0:T(8,128)(2,1)}, u32[]{:S(2)}) copy-start(bf16[1,256,128]{2,1,0:T(8,128)(2,1)} %param.15) | copy-start | bytes 196612
  6.5 76.8 %copy-start.3 = (bf16[1,256,128]{2,1,0:T(8,128)(2,1)S(1)}, bf16[1,256,128]{2,1,0:T(8,128)(2,1)}, u32[]{:S(2)}) copy-start(bf16[1,256,128]{2,1,0:T(8,128)(2,1)} %param.14) | copy-start | bytes 196612
  6.5 90.8 %copy-start.1 = (bf16[128,4096]{1,0:T(8,128)(2,1)S(1)}, bf16[128,4096]{1,0:T(8,128)(2,1)}, u32[]{:S(2)}) copy-start(bf16[128,4096]{1,0:T(8,128)(2,1)} %param.11) | copy-start | bytes 3145732
  6.5 76.8 %all-gather.8.cloned.1.call-start = ((), (), s32[]{:S(2)}) async-start(), calls=%async_computation.1 | async-start | bytes 2641920 | tf_op jit(solution)/shard_map/all_gather | solution.py:118
  43.4 69.3 %all-gather.10.cloned.1.call-start = ((), (), s32[]{:S(2)}) async-start(), calls=%async_computation.2 | async-start | bytes 6340608 | tf_op jit(solution)/shard_map/all_gather | solution.py:118
  83.4 16.4 %collective-permute-start.2 = (bf16[256,256]{1,0:T(8,128)(2,1)S(1)}, bf16[256,256]{1,0:T(8,128)(2,1)}, u32[]{:S(2)}, u32[]{:S(2)}) collective-permute-start(bf16[256,256]{1,0:T(8,128)(2,1)S(1)} %get-tuple-element.13), channel_id=1, source_target_pairs={{0,3},{1,0},{2,1},{3,2},{4,7},{5,4},{6,5},{7,6},{8,11},{9,8},{10,9... | collective-permute-start | bytes 393224 | tf_op jit(solution)/shard_map/ppermute | solution.py:137
  88.8 11.0 %collective-permute-start.1 = (bf16[256,256]{1,0:T(8,128)(2,1)S(1)}, bf16[256,256]{1,0:T(8,128)(2,1)}, u32[]{:S(2)}, u32[]{:S(2)}) collective-permute-start(bf16[256,256]{1,0:T(8,128)(2,1)S(1)} %get-tuple-element.13), channel_id=1, source_target_pairs={{0,2},{1,3},{2,0},{3,1},{4,6},{5,7},{6,4},{7,5},{8,10},{9,11},{10,... | collective-permute-start | bytes 393224 | tf_op jit(solution)/shard_map/ppermute | solution.py:137
  92.7 9.1 %collective-permute-start = (bf16[256,256]{1,0:T(8,128)(2,1)S(1)}, bf16[256,256]{1,0:T(8,128)(2,1)}, u32[]{:S(2)}, u32[]{:S(2)}) collective-permute-start(bf16[256,256]{1,0:T(8,128)(2,1)S(1)} %get-tuple-element.13), channel_id=1, source_target_pairs={{0,1},{1,2},{2,3},{3,0},{4,5},{5,6},{6,7},{7,4},{8,9},{9,10},{10,1... | collective-permute-start | bytes 393224 | tf_op jit(solution)/shard_map/ppermute | solution.py:137
  133.7 28.6 %all-to-all-start = ((bf16[4,256,256]{1,2,0:T(8,128)(2,1)}), bf16[4,256,256]{1,2,0:T(8,128)(2,1)S(1)}, u32[]{:S(2)}, u32[]{:S(2)}) async-start(bf16[4,256,256]{1,2,0:T(8,128)(2,1)} %broadcast_in_dim.71), calls=%async_computation | async-start | bytes 1048576 | tf_op jit(solution)/shard_map/all_to_all | solution.py:149
  138.5 22.9 %collective-permute-start.5 = (bf16[256,256]{0,1:T(8,128)(2,1)S(1)}, bf16[256,256]{0,1:T(8,128)(2,1)S(1)}, u32[]{:S(2)}, u32[]{:S(2)}) collective-permute-start(bf16[256,256]{0,1:T(8,128)(2,1)S(1)} %get-tuple-element.10), channel_id=1, source_target_pairs={{3,2},{0,3},{7,6},{4,7},{11,10},{8,11},{15,14},{12,15},{19,18},{16... | collective-permute-start | bytes 393224 | tf_op jit(solution)/shard_map/ppermute | solution.py:155
  144.0 17.5 %collective-permute-start.4 = (bf16[256,256]{0,1:T(8,128)(2,1)S(1)}, bf16[256,256]{0,1:T(8,128)(2,1)S(1)}, u32[]{:S(2)}, u32[]{:S(2)}) collective-permute-start(bf16[256,256]{0,1:T(8,128)(2,1)S(1)} %get-tuple-element.10), channel_id=1, source_target_pairs={{0,2},{1,3},{4,6},{5,7},{8,10},{9,11},{12,14},{13,15},{16,18},{17,... | collective-permute-start | bytes 393224 | tf_op jit(solution)/shard_map/ppermute | solution.py:155
  147.1 14.4 %collective-permute-start.3 = (bf16[256,256]{0,1:T(8,128)(2,1)S(1)}, bf16[256,256]{0,1:T(8,128)(2,1)S(1)}, u32[]{:S(2)}, u32[]{:S(2)}) collective-permute-start(bf16[256,256]{0,1:T(8,128)(2,1)S(1)} %get-tuple-element.10), channel_id=1, source_target_pairs={{1,2},{2,3},{5,6},{6,7},{9,10},{10,11},{13,14},{14,15},{17,18},{18... | collective-permute-start | bytes 393224 | tf_op jit(solution)/shard_map/ppermute | solution.py:155
  162.3 2.2 %copy-start = (f32[4,256,128,8]{2,1,3,0:T(8,128)S(1)}, f32[4,256,128,8]{2,1,3,0:T(8,128)}, u32[]{:S(2)}) copy-start(f32[4,256,128,8]{2,1,3,0:T(8,128)} %get-tuple-element.17) | copy-start | bytes 12582916
Sparse Core Ops, SparseCore 0:
  43.5 39.8 all-gather.7
  85.7 26.8 all-gather.9
